TPU v7x, 512 devices: a whole 4x8x8 slice. The times are simulated.
512 devices in a mesh: space: 64 (over x, y, core), rep: 8 (over z).
Axes of the slice: x: 4, y: 8, z: 8, core: 2. Of those that a mesh axis runs over, the one named last changes fastest.
Arguments:
- features: bfloat16 [8, 16384, 128], P('rep', 'space'), may hold values from -6 to 6
- cotangent: bfloat16 [8, 16384, 128], P('rep', 'space'), may hold values from -6 to 6
- point_owner: int32 [8, 16384], P('rep', 'space'), may hold values from 0 to 63, as said below
- point_slot: int32 [8, 16384], P('rep', 'space'), may hold values from 0 to 511, as said below
- block_links: int32 [8, 64, 26], P('rep', 'space'), may hold values from 0 to 1, as said below
- weights: bfloat16 [27, 128, 128], replicated, may hold values from -0.109375 to 0.109375
Outputs:
- out_features: bfloat16 [8, 16384, 128], P('rep', 'space')
- input_grad: bfloat16 [8, 16384, 128], P('rep', 'space')
- weight_grad: float32 [27, 128, 128], replicated
Inputs may be any that keep to these rules, and one draw needn't show every extreme that they name: `point_owner`: among the points of one scan shard (256 consecutive rows of one replica), at most 8 have the same owner, and every scan shard has an owner that receives exactly 8 of its points. `point_slot`: within one replica, two points with the same owner never have the same slot. `block_links`: each slab is one block thick in x and has 3 x 3 block positions in y and z, each holding at most one of its blocks; slab o lies at x position o. Entry j names the block of slab o + dx at the neighbouring position, or 1 if no block is there or the slab is off the ends; the relation is symmetric (if b names c at offset d, c names b at offset -d).
All inputs are finite; a program needn't handle non-finite values.
Results may differ from a plain program's by a relative error of at most 0.001.
Values may be sent and summed in bfloat16 or wider, within the bound.
No kernel may reach another device: no remote copies, remote signals or barrier semaphores. Data moves between devices by JAX's collectives and lax.ppermute only.
A program may use at most 64 MiB of HBM per device.

v0:
```python
import math

import jax
import jax.numpy as jnp
from jax import lax
from jax.sharding import PartitionSpec as P

NEIGHBOR_OFFSETS = [
    (shift_x, shift_y, shift_z)
    for shift_x in (-1, 0, 1)
    for shift_y in (-1, 0, 1)
    for shift_z in (-1, 0, 1)
    if (shift_x, shift_y, shift_z) != (0, 0, 0)
]
ALL_TAPS = [
    (shift_x, shift_y, shift_z)
    for shift_x in (-1, 0, 1)
    for shift_y in (-1, 0, 1)
    for shift_z in (-1, 0, 1)
]


def padded_2(value, sides, width):
    for axis, dim in sides:
        size, length = (lax.axis_size(axis), value.shape[dim])
        up = [(i, (i + 1) % size) for i in range(size - 1)]
        down = [(j, i) for i, j in up]
        last = lax.slice_in_dim(value, length - width, length, axis=dim)
        first = lax.slice_in_dim(value, 0, width, axis=dim)
        before = lax.ppermute(last, axis, up)
        after = lax.ppermute(first, axis, down)
        value = jnp.concatenate([before, value, after], axis=dim)
    return value


def extent(offset):
    if offset < 0:
        return (7, 8)
    if offset == 0:
        return (0, 8)
    return (0, 1)


def pad_blocks(blocks, low_faces, high_faces, slab_links):
    zero_block = jnp.zeros((1,) + blocks.shape[1:], blocks.dtype)
    zero_face = jnp.zeros((1,) + low_faces.shape[1:], low_faces.dtype)
    own_table = jnp.concatenate([blocks, zero_block], 0)
    low_table = jnp.concatenate([low_faces, zero_face], 0)
    high_table = jnp.concatenate([high_faces, zero_face], 0)
    slab_parts = []
    for shift_x in (-1, 0, 1):
        layers = []
        for shift_y in (-1, 0, 1):
            lower_y, upper_y = extent(shift_y)
            pieces = []
            for shift_z in (-1, 0, 1):
                lower_z, upper_z = extent(shift_z)
                if shift_x == 0 and shift_y == 0 and (shift_z == 0):
                    portion = blocks
                else:
                    column = slab_links[:, NEIGHBOR_OFFSETS.index((shift_x, shift_y, shift_z))]
                    if shift_x == 0:
                        portion = own_table[:, :, lower_y:upper_y, lower_z:upper_z][column]
                    elif shift_x < 0:
                        portion = low_table[:, lower_y:upper_y, lower_z:upper_z][column][:, None]
                    else:
                        portion = high_table[:, lower_y:upper_y, lower_z:upper_z][column][:, None]
                pieces.append(portion)
            layers.append(jnp.concatenate(pieces, 3))
        slab_parts.append(jnp.concatenate(layers, 2))
    return jnp.concatenate(slab_parts, 1)


def tap_view(padded, shift_x, shift_y, shift_z, direction):
    channels = padded.shape[-1]
    start_x = 1 + direction * shift_x
    start_y = 1 + direction * shift_y
    start_z = 1 + direction * shift_z
    return padded[
        :, start_x : start_x + 8, start_y : start_y + 8, start_z : start_z + 8, :
    ].reshape(-1, channels)


def local_section(blocks_h, blocks_g, low_h, high_h, low_g, high_g, slab_links, weights):
    channels = weights.shape[-1]
    padded_h = pad_blocks(blocks_h, low_h, high_h, slab_links)
    padded_g = pad_blocks(blocks_g, low_g, high_g, slab_links)
    grads_flat = blocks_g.reshape(-1, channels)
    row_count = grads_flat.shape[0]
    convolved = jnp.zeros((row_count, channels), jnp.float32)
    backward = jnp.zeros((row_count, channels), jnp.float32)
    tap_grads = []
    for tap_index, (shift_x, shift_y, shift_z) in enumerate(ALL_TAPS):
        view_h = tap_view(padded_h, shift_x, shift_y, shift_z, 1)
        view_g = tap_view(padded_g, shift_x, shift_y, shift_z, -1)
        tap_weight = weights[tap_index]
        convolved = convolved + jnp.dot(view_h, tap_weight, preferred_element_type=jnp.float32)
        backward = backward + lax.dot_general(
            view_g, tap_weight, (((1,), (1,)), ((), ())), preferred_element_type=jnp.float32
        )
        tap_grads.append(
            lax.dot_general(
                view_h, grads_flat, (((0,), (0,)), ((), ())), preferred_element_type=jnp.float32
            )
        )
    grad_part = jnp.stack(tap_grads, 0)
    return (convolved, backward, grad_part)


def local(features, cotangent, point_owner, point_slot, block_links, weights):
    peer_count = lax.axis_size("space")
    channels = features.shape[-1]
    data_type = features.dtype
    links_here = block_links[0]
    blocks_here = links_here.shape[0]
    voxels = blocks_here * 512
    capacity = voxels // peer_count
    owners = point_owner[0]
    slots_here = point_slot[0]
    matches = (owners[:, None] == jnp.arange(peer_count, dtype=jnp.int32)[None, :]).astype(
        jnp.int32
    )
    earlier = jnp.cumsum(matches, axis=0) - matches
    bucket = owners * capacity + jnp.sum(earlier * matches, axis=1)
    send_x = (
        jnp.zeros((peer_count * capacity, channels), data_type)
        .at[bucket]
        .set(features[0])
        .reshape(peer_count, capacity, channels)
    )
    send_g = (
        jnp.zeros((peer_count * capacity, channels), data_type)
        .at[bucket]
        .set(cotangent[0])
        .reshape(peer_count, capacity, channels)
    )
    send_slot = (
        jnp.full((peer_count * capacity,), voxels, jnp.int32)
        .at[bucket]
        .set(slots_here)
        .reshape(peer_count, capacity)
    )
    recv_x, recv_g, recv_slot = (
        lax.all_to_all(send_x, "space", split_axis=0, concat_axis=0, tiled=True),
        lax.all_to_all(send_g, "space", split_axis=0, concat_axis=0, tiled=True),
        lax.all_to_all(send_slot, "space", split_axis=0, concat_axis=0, tiled=True),
    )
    arrived = recv_slot.reshape(-1)
    dense_x = (
        jnp.zeros((voxels + 1, channels), data_type)
        .at[arrived]
        .set(recv_x.reshape(-1, channels))[:voxels]
    )
    dense_g = (
        jnp.zeros((voxels + 1, channels), data_type)
        .at[arrived]
        .set(recv_g.reshape(-1, channels))[:voxels]
    )
    block_shape = (blocks_here, 8, 8, 8, channels)
    blocks_x = dense_x.reshape(block_shape)
    blocks_h = jnp.maximum(blocks_x, 0)
    blocks_g = dense_g.reshape(block_shape)
    faces_h = jnp.stack([blocks_h[:, 0], blocks_h[:, 7]])
    faces_g = jnp.stack([blocks_g[:, 0], blocks_g[:, 7]])
    framed_h, framed_g = (
        padded_2(faces_h, (("space", 0),), 1),
        padded_2(faces_g, (("space", 0),), 1),
    )
    convolved, backward, grad_part = local_section(
        blocks_h, blocks_g, framed_h[0], framed_h[3], framed_g[0], framed_g[3], links_here, weights
    )
    out_x = (dense_x.astype(jnp.float32) + convolved).astype(data_type)
    out_dx = (dense_g.astype(jnp.float32) + jnp.where(dense_x > 0, backward, 0.0)).astype(data_type)
    empty_row = jnp.zeros((1, channels), data_type)
    ret_x = jnp.concatenate([out_x, empty_row], 0)[arrived].reshape(peer_count, capacity, channels)
    ret_dx = jnp.concatenate([out_dx, empty_row], 0)[arrived].reshape(
        peer_count, capacity, channels
    )
    home_x, home_dx = (
        lax.all_to_all(ret_x, "space", split_axis=0, concat_axis=0, tiled=True),
        lax.all_to_all(ret_dx, "space", split_axis=0, concat_axis=0, tiled=True),
    )
    final_x = home_x.reshape(-1, channels)[bucket]
    final_dx = home_dx.reshape(-1, channels)[bucket]
    summed = lax.psum(grad_part, ("space", "rep"))
    norm_scale = 1.0 / math.sqrt(peer_count * lax.axis_size("rep") * owners.shape[0])
    weight_grad = summed * norm_scale
    return (final_x[None], final_dx[None], weight_grad)


def solution(mesh):
    in_specs = (
        P("rep", "space", None),
        P("rep", "space", None),
        P("rep", "space"),
        P("rep", "space"),
        P("rep", "space", None),
        P(),
    )
    out_specs = (P("rep", "space", None), P("rep", "space", None), P())
    return jax.shard_map(local, mesh=mesh, in_specs=in_specs, out_specs=out_specs, check_vma=False)
```

profile of v0, /device:TPU:1, one launch (start us, length us, event | category | flops | bytes accessed | tf_op | source)
XLA Modules:
  0.0 471.8 jit_solution(5676217496131264771)
XLA Ops:
  7.2 0.7 fusion.47
  7.9 0.6 reduce-window.6
  8.7 0.8 fusion.40
  9.5 0.7 compare_select_fusion.1
  10.2 1.6 scatter_custom_fusion
  11.8 0.7 all_to_all.18
  12.5 11.6 %all-to-all-start = ((s32[64,1,8]{2,1,0:T(1,128)}), s32[64,1,8]{2,1,0:T(1,128)S(1)}, u32[]{:S(2)}, u32[]{:S(2)}) async-start(s32[64,1,8]{2,1,0:T(1,128)} %bitcast.7), calls=%async_computation | async-start | bytes 65536 | tf_op jit(solution)/shard_map/all_to_all | solution.py:146
  24.1 1.6 fusion.235
  34.3 2.1 fusion.234
  60.1 1.8 scatter_custom_fusion.3
  61.9 2.1 scatter_custom_fusion.1
  80.1 10.3 %all-to-all-start.1 = ((bf16[64,8,128]{2,1,0:T(8,128)(2,1)}), bf16[64,8,128]{2,1,0:T(8,128)(2,1)S(1)}, u32[]{:S(2)}, u32[]{:S(2)}) async-start(bf16[64,8,128]{2,1,0:T(8,128)(2,1)} %bitcast.10), calls=%async_computation.1 | async-start | bytes 262144 | tf_op jit(solution)/shard_map/all_to_all | solution.py:144
  90.5 0.5 broadcast.1056
  91.0 0.7 reduce.5
  91.8 0.6 pad_clamp_fusion.1
  92.4 8.4 %all-to-all-done.1 = bf16[64,8,128]{2,1,0:T(8,128)(2,1)S(1)} async-done(((bf16[64,8,128]{2,1,0:T(8,128)(2,1)}), bf16[64,8,128]{2,1,0:T(8,128)(2,1)S(1)}, u32[]{:S(2)}, u32[]{:S(2)}) %all-to-all-start.1) | async-done | bytes 131104 | tf_op jit(solution)/shard_map/all_to_all | solution.py:144
  100.8 4.9 %all-to-all-start.3 = ((bf16[64,8,128]{2,1,0:T(8,128)(2,1)}), bf16[64,8,128]{2,1,0:T(8,128)(2,1)S(1)}, u32[]{:S(2)}, u32[]{:S(2)}) async-start(bf16[64,8,128]{2,1,0:T(8,128)(2,1)} %bitcast.143), calls=%async_computation.3 | async-start | bytes 262144 | tf_op jit(solution)/shard_map/all_to_all | solution.py:145
  105.7 1.8 scatter_custom_fusion.2
  107.6 8.5 %all-to-all-done.3 = bf16[64,8,128]{2,1,0:T(8,128)(2,1)S(1)} async-done(((bf16[64,8,128]{2,1,0:T(8,128)(2,1)}), bf16[64,8,128]{2,1,0:T(8,128)(2,1)S(1)}, u32[]{:S(2)}, u32[]{:S(2)}) %all-to-all-start.3) | async-done | bytes 131104 | tf_op jit(solution)/shard_map/all_to_all | solution.py:145
  116.0 1.8 scatter_custom_fusion.4
  118.1 2.3 collective-permute-start.1
  120.4 3.3 collective-permute-start
  123.6 1.9 collective-permute-start.2
  125.7 0.3 maximum_maximum_fusion.7
  126.5 0.3 maximum_maximum_fusion.5
  126.8 0.8 fusion.230
  127.7 0.8 fusion.231
  128.7 3.8 collective-permute-start.3
  132.5 0.6 pad_slice_fusion.38
  133.1 0.6 pad_slice_fusion.36
  133.7 0.6 pad_slice_fusion.39
  134.5 0.6 fusion.159
  135.2 0.2 maximum_maximum_fusion.2
  135.8 0.2 maximum_maximum_fusion
  136.0 1.1 fusion.227
  137.4 0.9 fusion.102
  141.0 0.2 maximum_maximum_fusion.3
  144.1 2.1 gather_fusion.2
  146.1 8.8 %all-to-all-start.4 = ((bf16[64,8,128]{2,1,0:T(8,128)(2,1)}), bf16[64,8,128]{2,1,0:T(8,128)(2,1)S(1)}, u32[]{:S(2)}, u32[]{:S(2)}) async-start(bf16[64,8,128]{2,1,0:T(8,128)(2,1)} %bitcast.630), calls=%async_computation.4 | async-start | bytes 262144 | tf_op jit(solution)/shard_map/all_to_all | solution.py:181
  155.0 1.2 convolution_add_fusion.51
  156.2 1.1 convolution_add_fusion.50
  157.4 1.1 convolution_add_fusion.49
  160.8 0.2 maximum_maximum_fusion.1
  161.5 0.2 fusion.29
  162.0 0.2 fusion.27
  162.2 0.2 fusion.26
  162.5 0.2 fusion.25
  163.0 0.2 fusion.23
  165.7 0.9 convolution_add_fusion.35
  166.8 0.9 convolution_add_fusion.34
  168.0 0.9 convolution_add_fusion.33
  169.2 0.9 convolution_add_fusion.32
  170.4 0.9 convolution_add_fusion.31
  171.5 0.9 convolution_add_fusion.30
  172.7 1.6 convolution_add_fusion.29
  175.3 1.2 copy-done.2
  176.6 1.1 convolution_add_fusion.28
  178.1 1.9 gather_fusion
  180.0 10.3 %all-to-all-start.2 = ((bf16[64,8,128]{2,1,0:T(8,128)(2,1)}), bf16[64,8,128]{2,1,0:T(8,128)(2,1)S(1)}, u32[]{:S(2)}, u32[]{:S(2)}) async-start(bf16[64,8,128]{2,1,0:T(8,128)(2,1)} %bitcast.139), calls=%async_computation.2 | async-start | bytes 262144 | tf_op jit(solution)/shard_map/all_to_all | solution.py:180
  190.4 1.5 gather_fusion.3
  191.8 8.8 %all-to-all-done.2 = bf16[64,8,128]{2,1,0:T(8,128)(2,1)S(1)} async-done(((bf16[64,8,128]{2,1,0:T(8,128)(2,1)}), bf16[64,8,128]{2,1,0:T(8,128)(2,1)S(1)}, u32[]{:S(2)}, u32[]{:S(2)}) %all-to-all-start.2) | async-done | bytes 131104 | tf_op jit(solution)/shard_map/all_to_all | solution.py:180
  200.7 1.5 gather_fusion.1
  202.1 259.9 %all-reduce.10.cloned.1.call-done = f32[27,128,128]{2,1,0:T(8,128)} async-done(((f32[27,128,128]{2,1,0:T(8,128)}), f32[27,128,128]{2,1,0:T(8,128)}) %all-reduce.10.cloned.1.call-update) | async-done | bytes 1769488 | tf_op jit(solution)/shard_map/psum | solution.py:185
  462.1 2.9 broadcast_multiply_fusion
  (220 shorter events, 15.1 us)
Async XLA Ops:
  7.2 52.9 %copy-start = (bf16[1,256,128]{2,1,0:T(8,128)(2,1)S(1)}, bf16[1,256,128]{2,1,0:T(8,128)(2,1)}, u32[]{:S(2)}) copy-start(bf16[1,256,128]{2,1,0:T(8,128)(2,1)} %param.7) | copy-start | bytes 196612
  10.2 80.3 %copy-start.39 = (s32[256,1]{0,1:T(1,128)}, s32[256,1]{0,1:T(1,128)S(1)}, u32[]{:S(2)}) copy-start(s32[256,1]{0,1:T(1,128)S(1)} %compare_select_fusion.1) | copy-start | bytes 3076
  12.5 67.7 %all-to-all-start = ((s32[64,1,8]{2,1,0:T(1,128)}), s32[64,1,8]{2,1,0:T(1,128)S(1)}, u32[]{:S(2)}, u32[]{:S(2)}) async-start(s32[64,1,8]{2,1,0:T(1,128)} %bitcast.7), calls=%async_computation | async-start | bytes 65536 | tf_op jit(solution)/shard_map/all_to_all | solution.py:146
  80.1 20.7 %all-to-all-start.1 = ((bf16[64,8,128]{2,1,0:T(8,128)(2,1)}), bf16[64,8,128]{2,1,0:T(8,128)(2,1)S(1)}, u32[]{:S(2)}, u32[]{:S(2)}) async-start(bf16[64,8,128]{2,1,0:T(8,128)(2,1)} %bitcast.10), calls=%async_computation.1 | async-start | bytes 262144 | tf_op jit(solution)/shard_map/all_to_all | solution.py:144
  100.8 15.2 %all-to-all-start.3 = ((bf16[64,8,128]{2,1,0:T(8,128)(2,1)}), bf16[64,8,128]{2,1,0:T(8,128)(2,1)S(1)}, u32[]{:S(2)}, u32[]{:S(2)}) async-start(bf16[64,8,128]{2,1,0:T(8,128)(2,1)} %bitcast.143), calls=%async_computation.3 | async-start | bytes 262144 | tf_op jit(solution)/shard_map/all_to_all | solution.py:145
  118.1 14.5 %collective-permute-start.1 = (bf16[1,1,8,8,128]{4,3,2,1,0:T(8,128)(2,1)S(1)}, bf16[1,1,8,8,128]{4,3,2,1,0:T(8,128)(2,1)S(1)}, u32[]{:S(2)}, u32[]{:S(2)}) collective-permute-start(bf16[1,1,8,8,128]{4,3,2,1,0:T(8,128)(2,1)S(1)} %get-tuple-element.639), channel_id=1, source_target_pairs={{8,0},{16,8},{24,16},{32,24},{40,32},{48,40},{56,48},{64,56},{72,6... | collective-permute-start | bytes 49160 | tf_op jit(solution)/shard_map/ppermute | solution.py:31
  120.4 13.9 %collective-permute-start = (bf16[1,1,8,8,128]{4,3,2,1,0:T(8,128)(2,1)S(1)}, bf16[1,1,8,8,128]{4,3,2,1,0:T(8,128)(2,1)S(1)}, u32[]{:S(2)}, u32[]{:S(2)}) collective-permute-start(bf16[1,1,8,8,128]{4,3,2,1,0:T(8,128)(2,1)S(1)} %get-tuple-element.640), channel_id=1, source_target_pairs={{0,8},{8,16},{16,24},{24,32},{32,40},{40,48},{48,56},{56,64},{64,7... | collective-permute-start | bytes 49160 | tf_op jit(solution)/shard_map/ppermute | solution.py:30
  123.6 10.8 %collective-permute-start.2 = (bf16[1,1,8,8,128]{4,3,2,1,0:T(8,128)(2,1)S(1)}, bf16[1,1,8,8,128]{4,3,2,1,0:T(8,128)(2,1)S(1)}, u32[]{:S(2)}, u32[]{:S(2)}) collective-permute-start(bf16[1,1,8,8,128]{4,3,2,1,0:T(8,128)(2,1)S(1)} %get-tuple-element.628), channel_id=1, source_target_pairs={{8,0},{16,8},{24,16},{32,24},{40,32},{48,40},{56,48},{64,56},{72,6... | collective-permute-start | bytes 49160 | tf_op jit(solution)/shard_map/ppermute | solution.py:31
  126.2 9.6 %copy-start.27 = (bf16[1,8,1,1,128]{4,3,2,1,0:T(2,128)(2,1)}, bf16[1,8,1,1,128]{4,3,2,1,0:T(2,128)(2,1)S(1)}, u32[]{:S(2)}) copy-start(bf16[1,8,1,1,128]{4,3,2,1,0:T(2,128)(2,1)S(1)} %get-tuple-element.712) | copy-start | bytes 6148
  126.2 9.5 %copy-start.29 = (bf16[1,8,1,1,128]{4,3,2,1,0:T(2,128)(2,1)}, bf16[1,8,1,1,128]{4,3,2,1,0:T(2,128)(2,1)S(1)}, u32[]{:S(2)}) copy-start(bf16[1,8,1,1,128]{4,3,2,1,0:T(2,128)(2,1)S(1)} %get-tuple-element.709) | copy-start | bytes 6148
  126.2 9.5 %copy-start.31 = (bf16[1,8,1,1,128]{4,3,2,1,0:T(2,128)(2,1)}, bf16[1,8,1,1,128]{4,3,2,1,0:T(2,128)(2,1)S(1)}, u32[]{:S(2)}) copy-start(bf16[1,8,1,1,128]{4,3,2,1,0:T(2,128)(2,1)S(1)} %get-tuple-element.710) | copy-start | bytes 6148
  126.2 9.5 %copy-start.23 = (bf16[1,8,1,8,128]{4,3,2,1,0:T(8,128)(2,1)}, bf16[1,8,1,8,128]{4,3,2,1,0:T(8,128)(2,1)S(1)}, u32[]{:S(2)}) copy-start(bf16[1,8,1,8,128]{4,3,2,1,0:T(8,128)(2,1)S(1)} %get-tuple-element.713) | copy-start | bytes 49156
  126.3 9.5 %copy-start.25 = (bf16[1,8,1,8,128]{4,3,2,1,0:T(8,128)(2,1)}, bf16[1,8,1,8,128]{4,3,2,1,0:T(8,128)(2,1)S(1)}, u32[]{:S(2)}) copy-start(bf16[1,8,1,8,128]{4,3,2,1,0:T(8,128)(2,1)S(1)} %get-tuple-element.714) | copy-start | bytes 49156
  126.4 9.4 %copy-start.21 = (bf16[1,8,8,1,128]{4,3,2,1,0:T(2,128)(2,1)}, bf16[1,8,8,1,128]{4,3,2,1,0:T(2,128)(2,1)S(1)}, u32[]{:S(2)}) copy-start(bf16[1,8,8,1,128]{4,3,2,1,0:T(2,128)(2,1)S(1)} %get-tuple-element.716) | copy-start | bytes 49156
  128.7 5.7 %collective-permute-start.3 = (bf16[1,1,8,8,128]{4,3,2,1,0:T(8,128)(2,1)S(1)}, bf16[1,1,8,8,128]{4,3,2,1,0:T(8,128)(2,1)S(1)}, u32[]{:S(2)}, u32[]{:S(2)}) collective-permute-start(bf16[1,1,8,8,128]{4,3,2,1,0:T(8,128)(2,1)S(1)} %get-tuple-element.627), channel_id=1, source_target_pairs={{0,8},{8,16},{16,24},{24,32},{32,40},{40,48},{48,56},{56,64},{64,7... | collective-permute-start | bytes 49160 | tf_op jit(solution)/shard_map/ppermute | solution.py:30
  135.6 1.7 copy-start.1
  146.1 33.9 %all-to-all-start.4 = ((bf16[64,8,128]{2,1,0:T(8,128)(2,1)}), bf16[64,8,128]{2,1,0:T(8,128)(2,1)S(1)}, u32[]{:S(2)}, u32[]{:S(2)}) async-start(bf16[64,8,128]{2,1,0:T(8,128)(2,1)} %bitcast.630), calls=%async_computation.4 | async-start | bytes 262144 | tf_op jit(solution)/shard_map/all_to_all | solution.py:181
  154.9 307.2 %all-reduce.10.cloned.1.call-start = ((), (), s32[]{:S(2)}) async-start(), calls=%async_computation.5 | async-start | bytes 3538944 | tf_op jit(solution)/shard_map/psum | solution.py:185
  155.0 3.5 copy-start.7
  155.0 3.7 copy-start.6
  155.0 3.9 copy-start.5
  156.2 2.9 copy-start.4
  157.4 1.9 copy-start.3
  158.5 1.1 copy-start.20
  158.7 1.1 copy-start.19
  158.9 1.1 copy-start.18
  159.5 1.1 copy-start.43
  159.5 1.1 copy-start.44
  159.5 1.1 copy-start.41
  159.5 1.1 copy-start.42
  159.5 1.1 copy-start.37
  159.5 1.1 copy-start.38
  159.5 1.2 copy-start.34
  159.5 1.2 copy-start.35
  159.5 1.2 copy-start.22
  159.5 1.2 copy-start.24
  159.6 1.2 copy-start.26
  159.6 1.2 copy-start.28
  159.6 1.2 copy-start.30
  159.6 1.2 copy-start.32
  159.6 1.2 copy-start.33
  160.4 0.9 copy-start.10
  160.5 1.0 copy-start.9
  160.8 1.0 copy-start.8
  161.3 13.3 %copy-start.13 = (bf16[1,8,8,8,128]{4,3,2,1,0:T(8,128)(2,1)}, bf16[1,8,8,8,128]{4,3,2,1,0:T(8,128)(2,1)S(1)}, u32[]{:S(2)}) copy-start(bf16[1,8,8,8,128]{4,3,2,1,0:T(8,128)(2,1)S(1)} %get-tuple-element.595) | copy-start | bytes 393220
  161.3 13.5 %copy-start.11 = (bf16[1,8,8,8,128]{4,3,2,1,0:T(8,128)(2,1)}, bf16[1,8,8,8,128]{4,3,2,1,0:T(8,128)(2,1)S(1)}, u32[]{:S(2)}) copy-start(bf16[1,8,8,8,128]{4,3,2,1,0:T(8,128)(2,1)S(1)} %get-tuple-element.594) | copy-start | bytes 393220
  162.7 2.1 copy-start.17
  163.4 1.8 copy-start.16
  164.2 1.5 copy-start.15
  174.8 1.7 copy-start.14
  175.1 2.6 copy-start.12
  175.3 1.2 copy-start.2
  175.3 2.8 copy-start.36
  176.5 13.8 %copy-start.40 = (s32[256,1]{0,1:T(1,128)S(1)}, s32[256,1]{0,1:T(1,128)}, u32[]{:S(2)}) copy-start(s32[256,1]{0,1:T(1,128)} %copy-done.39) | copy-start | bytes 3076
  180.0 20.7 %all-to-all-start.2 = ((bf16[64,8,128]{2,1,0:T(8,128)(2,1)}), bf16[64,8,128]{2,1,0:T(8,128)(2,1)S(1)}, u32[]{:S(2)}, u32[]{:S(2)}) async-start(bf16[64,8,128]{2,1,0:T(8,128)(2,1)} %bitcast.139), calls=%async_computation.2 | async-start | bytes 262144 | tf_op jit(solution)/shard_map/all_to_all | solution.py:180
Sparse Core Ops, SparseCore 0:
  176.7 285.3 all-reduce.9
where the time goes:
time: 474 us; the launch traced here: 472 us
  waiting for transfers between devices  286 us (60%)
  between operations  64.3 us (14%)
  starting transfers between devices  57.3 us (12%)
  local copies, waits for them, and re-layouts  29.1 us (6%)
  matrix products  26.5 us (6%)
  other arithmetic  8.99 us (2%)
    psum x1, waiting for transfers between devices, local(): summed = lax.psum(grad_part, ('space', 'rep'))  260 us
    dot_general x27, matrix products, local_section(): jnp.dot(view_h, tap_weight, preferred_element_type=jnp.float32)  15.2 us
    all_to_all x1, starting transfers between devices, local(): lax.all_to_all(send_slot, 'space', split_axis=0, concat_axis=0, tiled=True)  11.6 us
    all_to_all x1, starting transfers between devices, local(): lax.all_to_all(ret_x, 'space', split_axis=0, concat_axis=0, tiled=True)  10.3 us
    all_to_all x1, starting transfers between devices, local(): lax.all_to_all(send_x, 'space', split_axis=0, concat_axis=0, tiled=True)  10.3 us
  transfers between devices with their start and end apart: 10, of which 4 were waited for; matrix products, arithmetic and copies ran while one was open for 9% of the time, Pallas kernels for 0%

commit v1 on v0

v1 whole, which is shorter than its diff:
```python
import math

import jax
import jax.numpy as jnp
import numpy as np
from jax import lax
from jax.sharding import Mesh
from jax.sharding import PartitionSpec as P

NEIGHBOR_OFFSETS = [
    (shift_x, shift_y, shift_z)
    for shift_x in (-1, 0, 1)
    for shift_y in (-1, 0, 1)
    for shift_z in (-1, 0, 1)
    if (shift_x, shift_y, shift_z) != (0, 0, 0)
]
ALL_TAPS = [
    (shift_x, shift_y, shift_z)
    for shift_x in (-1, 0, 1)
    for shift_y in (-1, 0, 1)
    for shift_z in (-1, 0, 1)
]
SPACE_AXES = ("sx", "sy", "sc")
REDUCE_ORDER = ("sc", "sx", "sy", "rep")


def extent(offset):
    if offset < 0:
        return (7, 8)
    if offset == 0:
        return (0, 8)
    return (0, 1)


def pad_blocks(blocks, low_faces, high_faces, slab_links):
    zero_block = jnp.zeros((1,) + blocks.shape[1:], blocks.dtype)
    zero_face = jnp.zeros((1,) + low_faces.shape[1:], low_faces.dtype)
    own_table = jnp.concatenate([blocks, zero_block], 0)
    low_table = jnp.concatenate([low_faces, zero_face], 0)
    high_table = jnp.concatenate([high_faces, zero_face], 0)
    slab_parts = []
    for shift_x in (-1, 0, 1):
        layers = []
        for shift_y in (-1, 0, 1):
            lower_y, upper_y = extent(shift_y)
            pieces = []
            for shift_z in (-1, 0, 1):
                lower_z, upper_z = extent(shift_z)
                if shift_x == 0 and shift_y == 0 and (shift_z == 0):
                    portion = blocks
                else:
                    column = slab_links[:, NEIGHBOR_OFFSETS.index((shift_x, shift_y, shift_z))]
                    if shift_x == 0:
                        portion = own_table[:, :, lower_y:upper_y, lower_z:upper_z][column]
                    elif shift_x < 0:
                        portion = low_table[:, lower_y:upper_y, lower_z:upper_z][column][:, None]
                    else:
                        portion = high_table[:, lower_y:upper_y, lower_z:upper_z][column][:, None]
                pieces.append(portion)
            layers.append(jnp.concatenate(pieces, 3))
        slab_parts.append(jnp.concatenate(layers, 2))
    return jnp.concatenate(slab_parts, 1)


def patch_columns(padded, direction):
    block_count = padded.shape[0]
    channels = padded.shape[-1]
    pieces = []
    for shift_x, shift_y, shift_z in ALL_TAPS:
        start_x = 1 + direction * shift_x
        start_y = 1 + direction * shift_y
        start_z = 1 + direction * shift_z
        pieces.append(
            padded[:, start_x : start_x + 8, start_y : start_y + 8, start_z : start_z + 8, :]
        )
    return jnp.concatenate(pieces, -1).reshape(block_count * 512, 27 * channels)


def reduce_everywhere(value, sizes):
    flat = value.reshape(-1)
    for axis in REDUCE_ORDER:
        count = sizes[axis]
        lanes = 128 if flat.shape[0] % (count * 128) == 0 else flat.shape[0] // count
        parts = lax.all_to_all(flat.reshape(count, -1, lanes), axis, 0, 0, tiled=True)
        flat = jnp.sum(parts, 0).reshape(-1)
    for axis in reversed(REDUCE_ORDER):
        count = sizes[axis]
        lanes = 128 if flat.shape[0] % 128 == 0 else flat.shape[0]
        spread = jnp.broadcast_to(flat.reshape(1, -1, lanes), (count, flat.shape[0] // lanes, lanes))
        flat = lax.all_to_all(spread, axis, 0, 0, tiled=True).reshape(-1)
    return flat.reshape(value.shape)


def make_local(sizes):
    def local(features, cotangent, point_owner, point_slot, block_links, weights):
        peer_count = sizes["sx"] * sizes["sy"] * sizes["sc"]
        rep_count = sizes["rep"]
        channels = features.shape[-1]
        data_type = features.dtype
        links_here = block_links[0]
        blocks_here = links_here.shape[0]
        voxels = blocks_here * 512
        capacity = voxels // peer_count
        owners = point_owner[0]
        slots_here = point_slot[0]
        matches = (owners[:, None] == jnp.arange(peer_count, dtype=jnp.int32)[None, :]).astype(
            jnp.int32
        )
        earlier = jnp.cumsum(matches, axis=0) - matches
        within = jnp.sum(earlier * matches, axis=1)
        bucket = owners * capacity + within
        payload = jnp.concatenate([features[0], cotangent[0]], -1)
        rows = (
            jnp.zeros((peer_count * capacity, 2 * channels), data_type)
            .at[bucket]
            .set(payload)
            .reshape(peer_count, capacity * 2 * channels)
        )
        slot_full = (
            jnp.full((peer_count * capacity,), voxels, jnp.int32)
            .at[bucket]
            .set(slots_here)
            .reshape(peer_count, capacity)
        )
        slot_hi = (slot_full // 32).astype(data_type)
        slot_lo = (slot_full % 32).astype(data_type)
        slot_row = jnp.concatenate(
            [
                slot_hi,
                slot_lo,
                jnp.zeros((peer_count, 2 * channels - 2 * capacity), data_type),
            ],
            -1,
        )
        send = jnp.concatenate([rows, slot_row], -1)
        recv = lax.all_to_all(send, SPACE_AXES, 0, 0, tiled=True)
        recv_rows = recv[:, : capacity * 2 * channels].reshape(peer_count * capacity, 2 * channels)
        recv_slot = recv[:, capacity * 2 * channels :]
        arrived = (
            recv_slot[:, :capacity].astype(jnp.int32) * 32
            + recv_slot[:, capacity : 2 * capacity].astype(jnp.int32)
        ).reshape(-1)
        dense = (
            jnp.zeros((voxels + 1, 2 * channels), data_type).at[arrived].set(recv_rows)[:voxels]
        )
        dense_x = dense[:, :channels]
        dense_g = dense[:, channels:]
        block_shape = (blocks_here, 8, 8, 8, channels)
        blocks_x = dense_x.reshape(block_shape)
        blocks_h = jnp.maximum(blocks_x, 0)
        blocks_g = dense_g.reshape(block_shape)
        faces = jnp.concatenate(
            [blocks_h[:, 0], blocks_g[:, 0], blocks_h[:, 7], blocks_g[:, 7]], -1
        )
        up = [(i, (i + 1) % peer_count) for i in range(peer_count - 1)]
        down = [(j, i) for i, j in up]
        from_below = lax.ppermute(faces[..., 2 * channels :], SPACE_AXES, up)
        from_above = lax.ppermute(faces[..., : 2 * channels], SPACE_AXES, down)
        low_h, low_g = from_below[..., :channels], from_below[..., channels:]
        high_h, high_g = from_above[..., :channels], from_above[..., channels:]
        columns_h = patch_columns(pad_blocks(blocks_h, low_h, high_h, links_here), 1)
        columns_g = patch_columns(pad_blocks(blocks_g, low_g, high_g, links_here), -1)
        grads_flat = dense_g
        grad_part = lax.dot_general(
            columns_h, grads_flat, (((0,), (0,)), ((), ())), preferred_element_type=jnp.float32
        )
        convolved = jnp.dot(
            columns_h,
            weights.reshape(27 * channels, channels),
            preferred_element_type=jnp.float32,
        )
        flipped = jnp.transpose(weights, (0, 2, 1)).reshape(27 * channels, channels)
        backward = jnp.dot(columns_g, flipped, preferred_element_type=jnp.float32)
        out_x = (dense_x.astype(jnp.float32) + convolved).astype(data_type)
        out_dx = (dense_g.astype(jnp.float32) + jnp.where(dense_x > 0, backward, 0.0)).astype(
            data_type
        )
        out_both = jnp.concatenate(
            [jnp.concatenate([out_x, out_dx], -1), jnp.zeros((1, 2 * channels), data_type)], 0
        )
        ret = out_both[arrived].reshape(peer_count, capacity * 2 * channels)
        home = lax.all_to_all(ret, SPACE_AXES, 0, 0, tiled=True).reshape(-1, 2 * channels)
        final = home[bucket]
        final_x = final[:, :channels]
        final_dx = final[:, channels:]
        summed = reduce_everywhere(grad_part, sizes)
        norm_scale = 1.0 / math.sqrt(peer_count * rep_count * owners.shape[0])
        weight_grad = (summed * norm_scale).reshape(27, channels, channels)
        return (final_x[None], final_dx[None], weight_grad)

    return local


def split_space(mesh):
    grid = np.asarray(mesh.devices)
    space_count = grid.shape[0]
    try:
        column = grid[:, 0]
        xs = len({int(d.coords[0]) for d in column})
        cores = len({int(d.core_on_chip) for d in column})
    except Exception:
        cores = 2
        xs = 4
    ys = space_count // (xs * cores)
    return xs, ys, cores


def solution(mesh):
    xs, ys, cores = split_space(mesh)
    grid = np.asarray(mesh.devices)
    rep_count = grid.shape[1]
    fine = Mesh(grid.reshape(xs, ys, cores, rep_count), ("sx", "sy", "sc", "rep"))
    sizes = {"sx": xs, "sy": ys, "sc": cores, "rep": rep_count}
    space = SPACE_AXES
    in_specs = (
        P("rep", space, None),
        P("rep", space, None),
        P("rep", space),
        P("rep", space),
        P("rep", space, None),
        P(),
    )
    out_specs = (P("rep", space, None), P("rep", space, None), P())
    return jax.shard_map(
        make_local(sizes), mesh=fine, in_specs=in_specs, out_specs=out_specs, check_vma=False
    )
```

time: 474 us -> 296 us (0.62)
  waiting for transfers between devices: 286 us -> 35.2 us
  local copies, waits for them, and re-layouts: 29.1 us -> 109 us
  matrix products: 26.5 us -> 7.56 us
  between operations: 64.3 us -> 49.4 us
  blocking collectives: 0 us -> 11.2 us
  other arithmetic: 8.99 us -> 17.4 us
  starting transfers between devices: 57.3 us -> 63.7 us
    psum x1 -> x0, waiting for transfers between devices: 260 us -> none  [local(): summed = lax.psum(grad_part, ('space', 'rep'))]
    unnamed x90 -> x120, local copies, waits for them, and re-layouts: 1.41 us -> 47.2 us
    concatenate x2 -> x56, local copies, waits for them, and re-layouts: 0.02 us -> 39.8 us  [the longest x54 39.7 us: patch_columns(): return jnp.concatenate(pieces, -1).reshape(block_count * 512, 27 * channels)]
    dot_general x81 -> x3, matrix products: 26.5 us -> 7.56 us  [the longest x1 3.66 us: local(): backward = jnp.dot(columns_g, flipped, preferred_element_type=jnp.float32)]
    all_to_all x5 -> x8, starting transfers between devices: 46 us -> 58 us  [the longest x3 20.8 us: reduce_everywhere(): lax.all_to_all(flat.reshape(count, -1, lanes), axis, 0, 0, tiled=True)]
    all_to_all x0 -> x2, blocking collectives: none -> 11.2 us  [the longest x1 6.3 us: reduce_everywhere(): flat = lax.all_to_all(spread, axis, 0, 0, tiled=True).reshape(-1)]
    all_to_all x5 -> x8, waiting for transfers between devices: 25.7 us -> 35.2 us  [the longest x3 13.7 us: reduce_everywhere(): flat = lax.all_to_all(spread, axis, 0, 0, tiled=True).reshape(-1)]
    broadcast_in_dim x0 -> x8, local copies, waits for them, and re-layouts: none -> 6.22 us  [the longest x6 5.55 us: reduce_everywhere(): jnp.broadcast_to(flat.reshape(1, -1, lanes), (count, flat.shape[0] // lan...]
  transfers between devices with their start and end apart: 10 -> 10, of which waited for: 4 -> 6; matrix products, arithmetic and copies ran while one was open for 9% -> 18% of each run, Pallas kernels for 0% -> 0%
where the time goes in v1:
time: 296 us; the launch traced here: 294 us
  local copies, waits for them, and re-layouts  109 us (37%)
  starting transfers between devices  63.7 us (22%)
  between operations  49.4 us (17%)
  waiting for transfers between devices  35.2 us (12%)
  other arithmetic  17.4 us (6%)
  blocking collectives  11.2 us (4%)
  matrix products  7.56 us (3%)
    unnamed x120, local copies, waits for them, and re-layouts  47.2 us
    concatenate x54, local copies, waits for them, and re-layouts, patch_columns(): return jnp.concatenate(pieces, -1).reshape(block_count * 512, 27 * channels)  39.7 us
    all_to_all x3, starting transfers between devices, reduce_everywhere(): lax.all_to_all(flat.reshape(count, -1, lanes), axis, 0, 0, tiled=True)  20.8 us
    all_to_all x3, waiting for transfers between devices, reduce_everywhere(): flat = lax.all_to_all(spread, axis, 0, 0, tiled=True).reshape(-1)  13.7 us
    all_to_all x1, starting transfers between devices, local(): lax.all_to_all(ret, SPACE_AXES, 0, 0, tiled=True).reshape(-1, 2 * channels)  13.5 us
    all_to_all x3, starting transfers between devices, reduce_everywhere(): flat = lax.all_to_all(spread, axis, 0, 0, tiled=True).reshape(-1)  12 us
    all_to_all x1, starting transfers between devices, local(): recv = lax.all_to_all(send, SPACE_AXES, 0, 0, tiled=True)  11.6 us
    all_to_all x1, waiting for transfers between devices, local(): lax.all_to_all(ret, SPACE_AXES, 0, 0, tiled=True).reshape(-1, 2 * channels)  11 us
  transfers between devices with their start and end apart: 10, of which 6 were waited for; matrix products, arithmetic and copies ran while one was open for 18% of the time, Pallas kernels for 0%

profile of v1, /device:TPU:1, one launch (start us, length us, event | category | flops | bytes accessed | tf_op | source)
XLA Modules:
  0.0 293.7 jit_solution(6341310483252780171)
XLA Ops:
  3.7 1.9 scatter_custom_fusion
  5.7 1.6 scatter_custom_fusion.1
  9.6 11.6 %all-to-all-start = ((bf16[64,2,1152]{2,1,0:T(2,128)(2,1)}), bf16[64,2,1152]{2,1,0:T(2,128)(2,1)S(1)}, u32[]{:S(2)}, u32[]{:S(2)}) async-start(bf16[64,2,1152]{2,1,0:T(2,128)(2,1)} %reshape.1508), calls=%async_computation | async-start | bytes 589824 | tf_op jit(solution)/shard_map/all_to_all | solution.py:136
  54.3 1.6 copy.304
  72.5 2.4 scatter_custom_fusion.2
  76.2 2.4 collective-permute-start.1
  85.6 3.4 %collective-permute-start = (bf16[1,8,8,256]{3,2,1,0:T(8,128)(2,1)S(1)}, bf16[1,8,8,256]{3,2,1,0:T(8,128)(2,1)S(1)}, u32[]{:S(2)}, u32[]{:S(2)}) collective-permute-start(bf16[1,8,8,256]{3,2,1,0:T(8,128)(2,1)S(1)} %pad_maximum_fusion.5), channel_id=1, source_target_pairs={{0,8},{8,16},{16,24},{24,32},{32,40},{40,48},{48,56},{56,64},{64,7... | collective-permute-start | bytes 98312 | tf_op jit(solution)/shard_map/ppermute | solution.py:157
  101.5 0.9 fusion.61
  117.7 1.2 fusion.59
  118.8 2.0 copy.265
  120.8 1.7 copy.266
  122.5 1.7 copy.267
  124.1 1.7 copy.268
  125.8 1.7 copy.269
  127.4 1.7 copy.270
  129.1 1.7 copy.271
  130.8 1.7 copy.272
  132.4 1.7 copy.273
  135.0 0.9 constant_dynamic-update-slice_fusion.11
  135.9 0.9 constant_dynamic-update-slice_fusion.10
  136.9 0.9 constant_dynamic-update-slice_fusion.9
  137.8 0.9 constant_dynamic-update-slice_fusion.8
  138.7 0.9 constant_dynamic-update-slice_fusion.7
  139.6 0.9 constant_dynamic-update-slice_fusion.6
  140.5 0.9 constant_dynamic-update-slice_fusion.5
  141.4 0.9 constant_dynamic-update-slice_fusion.4
  142.4 0.9 constant_dynamic-update-slice_fusion.3
  144.2 0.9 constant_dynamic-update-slice_fusion.1
  146.0 1.8 copy-done.1
  147.8 2.0 fusion.9
  149.8 4.9 %all_to_all.62 = f32[2,1728,128]{2,1,0:T(8,128)S(1)} all-to-all(f32[2,1728,128]{2,1,0:T(8,128)S(1)} %fusion.9), channel_id=1, replica_groups=mesh['sx'=4,'sy'=8,'sc'=2,'rep'=8] {'sc'}, dimensions={0} | all-to-all | bytes 3538944 | tf_op jit(solution)/shard_map/all_to_all | solution.py:84
  154.8 1.2 reduce_sum.49
  156.0 6.3 %all-to-all-start.3 = ((f32[4,432,128]{2,1,0:T(8,128)}), f32[4,432,128]{2,1,0:T(8,128)S(1)}, u32[]{:S(2)}, u32[]{:S(2)}) async-start(f32[4,432,128]{2,1,0:T(8,128)} %bitcast.166), calls=%async_computation.3 | async-start | bytes 1769472 | tf_op jit(solution)/shard_map/all_to_all | solution.py:84
  162.3 1.6 constant_dynamic-update-slice_fusion.52
  164.0 1.6 constant_dynamic-update-slice_fusion.51
  165.5 1.6 constant_dynamic-update-slice_fusion.50
  179.8 4.5 %all-to-all-start.4 = ((f32[8,54,128]{2,1,0:T(8,128)}), f32[8,54,128]{2,1,0:T(8,128)S(1)}, u32[]{:S(2)}, u32[]{:S(2)}) async-start(f32[8,54,128]{2,1,0:T(8,128)} %reshape_reshape.7), calls=%async_computation.4 | async-start | bytes 458752 | tf_op jit(solution)/shard_map/all_to_all | solution.py:84
  184.3 1.6 constant_dynamic-update-slice_fusion.31
  189.0 5.1 %all-to-all-done.4 = f32[8,54,128]{2,1,0:T(8,128)S(1)} async-done(((f32[8,54,128]{2,1,0:T(8,128)}), f32[8,54,128]{2,1,0:T(8,128)S(1)}, u32[]{:S(2)}, u32[]{:S(2)}) %all-to-all-start.4) | async-done | bytes 221216 | tf_op jit(solution)/shard_map/all_to_all | solution.py:84
  194.8 1.6 reshape_reshape.8
  196.4 10.0 %all-to-all-start.5 = ((f32[8,1,864]{2,1,0:T(1,128)}), f32[8,1,864]{2,1,0:T(1,128)}, u32[]{:S(2)}, u32[]{:S(2)}) async-start(f32[8,1,864]{2,1,0:T(1,128)} %reshape_reshape.8), calls=%async_computation.5 | async-start | bytes 57344 | tf_op jit(solution)/shard_map/all_to_all | solution.py:84
  206.4 1.6 constant_dynamic-update-slice_fusion.27
  208.0 5.4 %all-to-all-done.5 = f32[8,1,864]{2,1,0:T(1,128)} async-done(((f32[8,1,864]{2,1,0:T(1,128)}), f32[8,1,864]{2,1,0:T(1,128)}, u32[]{:S(2)}, u32[]{:S(2)}) %all-to-all-start.5) | async-done | bytes 27680 | tf_op jit(solution)/shard_map/all_to_all | solution.py:84
  214.8 3.9 %all-to-all-start.6 = ((f32[8,1,864]{2,1,0:T(1,128)}), f32[8,1,864]{2,1,0:T(1,128)}, u32[]{:S(2)}, u32[]{:S(2)}) async-start(f32[8,1,864]{2,1,0:T(1,128)} %broadcast_in_dim.336), calls=%async_computation.6 | async-start | bytes 57344 | tf_op jit(solution)/shard_map/all_to_all | solution.py:90
  218.7 3.7 %fusion.2 = bf16[512,128]{0,1:T(8,128)(2,1)} fusion(bf16[512,3456]{0,1:T(8,128)(2,1)} %constant_dynamic-update-slice_fusion.27, bf16[3456,128]{1,0:T(8,128)(2,1)} %bitcast.268, bf16[512,128]{0,1:T(8,128)(2,1)} %copy.312, bf16[512,128]{0,1:T(8,128)(2,1)} %copy-done.4), kind=kOutput, calls=%fused_computation.9 | convolution fusion | flops 453312512 | bytes 4816896 | tf_op jit(solution)/shard_map/dot_general | solution.py:173
  222.4 3.2 %all-to-all-done.6 = f32[8,1,864]{2,1,0:T(1,128)} async-done(((f32[8,1,864]{2,1,0:T(1,128)}), f32[8,1,864]{2,1,0:T(1,128)}, u32[]{:S(2)}, u32[]{:S(2)}) %all-to-all-start.6) | async-done | bytes 27680 | tf_op jit(solution)/shard_map/all_to_all | solution.py:90
  225.5 1.4 reduce.3
  227.0 1.4 broadcast_in_dim.337
  228.4 1.4 broadcast_in_dim.338
  229.8 4.3 %all-to-all-start.7 = ((f32[8,54,128]{2,1,0:T(8,128)}), f32[8,54,128]{2,1,0:T(8,128)}, u32[]{:S(2)}, u32[]{:S(2)}) async-start(f32[8,54,128]{2,1,0:T(8,128)} %broadcast_in_dim.338), calls=%async_computation.7 | async-start | bytes 458752 | tf_op jit(solution)/shard_map/all_to_all | solution.py:90
  234.1 1.9 fusion.1
  236.3 2.0 gather_fusion
  238.4 2.1 reduce.6
  241.4 1.5 all-to-all-done.7
  242.9 13.5 %all-to-all-start.1 = ((bf16[64,2,1024]{2,1,0:T(2,128)(2,1)}), bf16[64,2,1024]{2,1,0:T(2,128)(2,1)S(1)}, u32[]{:S(2)}, u32[]{:S(2)}) async-start(bf16[64,2,1024]{2,1,0:T(2,128)(2,1)} %reshape.1510), calls=%async_computation.1 | async-start | bytes 524288 | tf_op jit(solution)/shard_map/all_to_all | solution.py:182
  256.4 1.0 broadcast_in_dim.339
  257.4 11.0 %all-to-all-done.1 = bf16[64,2,1024]{2,1,0:T(2,128)(2,1)S(1)} async-done(((bf16[64,2,1024]{2,1,0:T(2,128)(2,1)}), bf16[64,2,1024]{2,1,0:T(2,128)(2,1)S(1)}, u32[]{:S(2)}, u32[]{:S(2)}) %all-to-all-start.1) | async-done | bytes 262176 | tf_op jit(solution)/shard_map/all_to_all | solution.py:182
  268.4 1.0 broadcast_in_dim.340
  269.3 3.8 %all-to-all-start.8 = ((f32[4,432,128]{2,1,0:T(8,128)}), f32[4,432,128]{2,1,0:T(8,128)S(1)}, u32[]{:S(2)}, u32[]{:S(2)}) async-start(f32[4,432,128]{2,1,0:T(8,128)} %broadcast_in_dim.340), calls=%async_computation.8 | async-start | bytes 1769472 | tf_op jit(solution)/shard_map/all_to_all | solution.py:90
  273.4 1.5 reduce.2
  275.1 1.2 gather_fusion.1
  276.9 9.1 %all-to-all-done.8 = f32[4,432,128]{2,1,0:T(8,128)S(1)} async-done(((f32[4,432,128]{2,1,0:T(8,128)}), f32[4,432,128]{2,1,0:T(8,128)S(1)}, u32[]{:S(2)}, u32[]{:S(2)}) %all-to-all-start.8) | async-done | bytes 884768 | tf_op jit(solution)/shard_map/all_to_all | solution.py:90
  286.0 6.3 %all_to_all.63 = f32[2,1728,128]{2,1,0:T(8,128)S(1)} all-to-all(f32[2,1728,128]{2,1,0:T(8,128)S(1)} %broadcast_in_dim.342), channel_id=1, replica_groups=mesh['sx'=4,'sy'=8,'sc'=2,'rep'=8] {'sc'}, dimensions={0} | all-to-all | bytes 3538944 | tf_op jit(solution)/shard_map/all_to_all | solution.py:90
  292.3 1.4 broadcast_multiply_fusion
  (271 shorter events, 65.9 us)
Async XLA Ops:
  0.6 20.6 %copy-start.28 = (s32[1,1,26]{2,1,0:T(1,128)S(1)}, s32[1,1,26]{2,1,0:T(1,128)}, u32[]{:S(2)}) copy-start(s32[1,1,26]{2,1,0:T(1,128)} %param.10) | copy-start | bytes 316
  0.6 53.7 %copy-start.5 = (bf16[27,128,128]{2,1,0:T(8,128)(2,1)S(1)}, bf16[27,128,128]{2,1,0:T(8,128)(2,1)}, u32[]{:S(2)}) copy-start(bf16[27,128,128]{2,1,0:T(8,128)(2,1)} %param.11) | copy-start | bytes 2654212
  9.6 62.2 %all-to-all-start = ((bf16[64,2,1152]{2,1,0:T(2,128)(2,1)}), bf16[64,2,1152]{2,1,0:T(2,128)(2,1)S(1)}, u32[]{:S(2)}, u32[]{:S(2)}) async-start(bf16[64,2,1152]{2,1,0:T(2,128)(2,1)} %reshape.1508), calls=%async_computation | async-start | bytes 589824 | tf_op jit(solution)/shard_map/all_to_all | solution.py:136
  74.9 8.4 %copy-start.3 = (bf16[513,256]{1,0:T(8,128)(2,1)}, bf16[513,256]{1,0:T(8,128)(2,1)S(1)}, u32[]{:S(2)}) copy-start(bf16[513,256]{1,0:T(8,128)(2,1)S(1)} %scatter_custom_fusion.2) | copy-start | bytes 787972
  75.9 40.7 %copy-start.4 = (bf16[512,128]{0,1:T(8,128)(2,1)}, bf16[512,128]{0,1:T(8,128)(2,1)S(1)}, u32[]{:S(2)}) copy-start(bf16[512,128]{0,1:T(8,128)(2,1)S(1)} %copy.311) | copy-start | bytes 393220
  76.2 17.1 %collective-permute-start.1 = (bf16[1,8,8,256]{3,2,1,0:T(8,128)(2,1)S(1)}, bf16[1,8,8,256]{3,2,1,0:T(8,128)(2,1)S(1)}, u32[]{:S(2)}, u32[]{:S(2)}) collective-permute-start(bf16[1,8,8,256]{3,2,1,0:T(8,128)(2,1)S(1)} %pad_maximum_fusion.6), channel_id=1, source_target_pairs={{8,0},{16,8},{24,16},{32,24},{40,32},{48,40},{56,48},{64,56},{72,6... | collective-permute-start | bytes 98312 | tf_op jit(solution)/shard_map/ppermute | solution.py:158
  85.6 7.8 %collective-permute-start = (bf16[1,8,8,256]{3,2,1,0:T(8,128)(2,1)S(1)}, bf16[1,8,8,256]{3,2,1,0:T(8,128)(2,1)S(1)}, u32[]{:S(2)}, u32[]{:S(2)}) collective-permute-start(bf16[1,8,8,256]{3,2,1,0:T(8,128)(2,1)S(1)} %pad_maximum_fusion.5), channel_id=1, source_target_pairs={{0,8},{8,16},{16,24},{24,32},{32,40},{40,48},{48,56},{56,64},{64,7... | collective-permute-start | bytes 98312 | tf_op jit(solution)/shard_map/ppermute | solution.py:157
  117.6 16.5 %copy-start = (bf16[512,3456]{0,1:T(8,128)(2,1)S(1)}, bf16[512,3456]{0,1:T(8,128)(2,1)}, u32[]{:S(2)}) copy-start(bf16[512,3456]{0,1:T(8,128)(2,1)} %constant_dynamic-update-slice_fusion.13) | copy-start | bytes 10616836
  146.0 1.8 copy-start.1
  149.8 17.3 %copy-start.23 = (bf16[512,128]{0,1:T(8,128)(2,1)S(1)}, bf16[512,128]{0,1:T(8,128)(2,1)}, u32[]{:S(2)}) copy-start(bf16[512,128]{0,1:T(8,128)(2,1)} %copy.282) | copy-start | bytes 393220
  154.7 13.0 %copy-start.22 = (bf16[512,128]{0,1:T(8,128)(2,1)S(1)}, bf16[512,128]{0,1:T(8,128)(2,1)}, u32[]{:S(2)}) copy-start(bf16[512,128]{0,1:T(8,128)(2,1)} %copy.283) | copy-start | bytes 393220
  154.7 13.7 %copy-start.21 = (bf16[512,128]{0,1:T(8,128)(2,1)S(1)}, bf16[512,128]{0,1:T(8,128)(2,1)}, u32[]{:S(2)}) copy-start(bf16[512,128]{0,1:T(8,128)(2,1)} %copy.284) | copy-start | bytes 393220
  154.7 14.3 %copy-start.19 = (bf16[512,128]{0,1:T(8,128)(2,1)S(1)}, bf16[512,128]{0,1:T(8,128)(2,1)}, u32[]{:S(2)}) copy-start(bf16[512,128]{0,1:T(8,128)(2,1)} %copy.285) | copy-start | bytes 393220
  154.7 15.0 %copy-start.20 = (bf16[512,128]{0,1:T(8,128)(2,1)S(1)}, bf16[512,128]{0,1:T(8,128)(2,1)}, u32[]{:S(2)}) copy-start(bf16[512,128]{0,1:T(8,128)(2,1)} %copy.286) | copy-start | bytes 393220
  154.7 15.7 %copy-start.15 = (bf16[512,128]{0,1:T(8,128)(2,1)S(1)}, bf16[512,128]{0,1:T(8,128)(2,1)}, u32[]{:S(2)}) copy-start(bf16[512,128]{0,1:T(8,128)(2,1)} %copy.287) | copy-start | bytes 393220
  154.7 16.3 %copy-start.13 = (bf16[512,128]{0,1:T(8,128)(2,1)S(1)}, bf16[512,128]{0,1:T(8,128)(2,1)}, u32[]{:S(2)}) copy-start(bf16[512,128]{0,1:T(8,128)(2,1)} %copy.288) | copy-start | bytes 393220
  154.8 17.0 %copy-start.14 = (bf16[512,128]{0,1:T(8,128)(2,1)S(1)}, bf16[512,128]{0,1:T(8,128)(2,1)}, u32[]{:S(2)}) copy-start(bf16[512,128]{0,1:T(8,128)(2,1)} %copy.289) | copy-start | bytes 393220
  154.8 17.6 %copy-start.12 = (bf16[512,128]{0,1:T(8,128)(2,1)S(1)}, bf16[512,128]{0,1:T(8,128)(2,1)}, u32[]{:S(2)}) copy-start(bf16[512,128]{0,1:T(8,128)(2,1)} %copy.290) | copy-start | bytes 393220
  154.8 18.3 %copy-start.10 = (bf16[512,128]{0,1:T(8,128)(2,1)S(1)}, bf16[512,128]{0,1:T(8,128)(2,1)}, u32[]{:S(2)}) copy-start(bf16[512,128]{0,1:T(8,128)(2,1)} %copy.312) | copy-start | bytes 393220
  154.8 18.9 %copy-start.11 = (bf16[512,128]{0,1:T(8,128)(2,1)S(1)}, bf16[512,128]{0,1:T(8,128)(2,1)}, u32[]{:S(2)}) copy-start(bf16[512,128]{0,1:T(8,128)(2,1)} %copy.291) | copy-start | bytes 393220
  154.8 19.6 %copy-start.18 = (bf16[512,128]{0,1:T(8,128)(2,1)S(1)}, bf16[512,128]{0,1:T(8,128)(2,1)}, u32[]{:S(2)}) copy-start(bf16[512,128]{0,1:T(8,128)(2,1)} %copy.292) | copy-start | bytes 393220
  154.8 20.2 %copy-start.16 = (bf16[512,128]{0,1:T(8,128)(2,1)S(1)}, bf16[512,128]{0,1:T(8,128)(2,1)}, u32[]{:S(2)}) copy-start(bf16[512,128]{0,1:T(8,128)(2,1)} %copy.293) | copy-start | bytes 393220
  156.0 19.7 %copy-start.17 = (bf16[512,128]{0,1:T(8,128)(2,1)S(1)}, bf16[512,128]{0,1:T(8,128)(2,1)}, u32[]{:S(2)}) copy-start(bf16[512,128]{0,1:T(8,128)(2,1)} %copy.294) | copy-start | bytes 393220
  156.0 22.3 %copy-start.24 = (bf16[512,128]{0,1:T(8,128)(2,1)S(1)}, bf16[512,128]{0,1:T(8,128)(2,1)}, u32[]{:S(2)}) copy-start(bf16[512,128]{0,1:T(8,128)(2,1)} %copy.298) | copy-start | bytes 393220
  156.0 23.0 %all-to-all-start.3 = ((f32[4,432,128]{2,1,0:T(8,128)}), f32[4,432,128]{2,1,0:T(8,128)S(1)}, u32[]{:S(2)}, u32[]{:S(2)}) async-start(f32[4,432,128]{2,1,0:T(8,128)} %bitcast.166), calls=%async_computation.3 | async-start | bytes 1769472 | tf_op jit(solution)/shard_map/all_to_all | solution.py:84
  162.3 14.1 %copy-start.27 = (bf16[512,128]{0,1:T(8,128)(2,1)S(1)}, bf16[512,128]{0,1:T(8,128)(2,1)}, u32[]{:S(2)}) copy-start(bf16[512,128]{0,1:T(8,128)(2,1)} %copy.295) | copy-start | bytes 393220
  162.3 14.7 %copy-start.26 = (bf16[512,128]{0,1:T(8,128)(2,1)S(1)}, bf16[512,128]{0,1:T(8,128)(2,1)}, u32[]{:S(2)}) copy-start(bf16[512,128]{0,1:T(8,128)(2,1)} %copy.296) | copy-start | bytes 393220
  162.3 15.4 %copy-start.25 = (bf16[512,128]{0,1:T(8,128)(2,1)S(1)}, bf16[512,128]{0,1:T(8,128)(2,1)}, u32[]{:S(2)}) copy-start(bf16[512,128]{0,1:T(8,128)(2,1)} %copy.297) | copy-start | bytes 393220
  167.1 18.8 %copy-start.9 = (bf16[1,8,8,8,128]{4,3,2,1,0:T(8,128)(2,1)S(1)}, bf16[1,8,8,8,128]{4,3,2,1,0:T(8,128)(2,1)}, u32[]{:S(2)}) copy-start(bf16[1,8,8,8,128]{4,3,2,1,0:T(8,128)(2,1)} %get-tuple-element.596) | copy-start | bytes 393220
  167.7 18.3 %copy-start.8 = (bf16[1,8,8,8,128]{4,3,2,1,0:T(8,128)(2,1)S(1)}, bf16[1,8,8,8,128]{4,3,2,1,0:T(8,128)(2,1)}, u32[]{:S(2)}) copy-start(bf16[1,8,8,8,128]{4,3,2,1,0:T(8,128)(2,1)} %get-tuple-element.595) | copy-start | bytes 393220
  168.4 17.7 %copy-start.7 = (bf16[1,8,8,8,128]{4,3,2,1,0:T(8,128)(2,1)S(1)}, bf16[1,8,8,8,128]{4,3,2,1,0:T(8,128)(2,1)}, u32[]{:S(2)}) copy-start(bf16[1,8,8,8,128]{4,3,2,1,0:T(8,128)(2,1)} %get-tuple-element.594) | copy-start | bytes 393220
  169.1 17.2 %copy-start.6 = (bf16[1,8,8,8,128]{4,3,2,1,0:T(8,128)(2,1)S(1)}, bf16[1,8,8,8,128]{4,3,2,1,0:T(8,128)(2,1)}, u32[]{:S(2)}) copy-start(bf16[1,8,8,8,128]{4,3,2,1,0:T(8,128)(2,1)} %get-tuple-element.593) | copy-start | bytes 393220
  179.8 14.3 %all-to-all-start.4 = ((f32[8,54,128]{2,1,0:T(8,128)}), f32[8,54,128]{2,1,0:T(8,128)S(1)}, u32[]{:S(2)}, u32[]{:S(2)}) async-start(f32[8,54,128]{2,1,0:T(8,128)} %reshape_reshape.7), calls=%async_computation.4 | async-start | bytes 458752 | tf_op jit(solution)/shard_map/all_to_all | solution.py:84
  194.8 39.3 %copy-start.2 = (bf16[512,3456]{0,1:T(8,128)(2,1)S(1)}, bf16[512,3456]{0,1:T(8,128)(2,1)}, u32[]{:S(2)}) copy-start(bf16[512,3456]{0,1:T(8,128)(2,1)} %copy-done.1) | copy-start | bytes 10616836
  196.4 17.0 %all-to-all-start.5 = ((f32[8,1,864]{2,1,0:T(1,128)}), f32[8,1,864]{2,1,0:T(1,128)}, u32[]{:S(2)}, u32[]{:S(2)}) async-start(f32[8,1,864]{2,1,0:T(1,128)} %reshape_reshape.8), calls=%async_computation.5 | async-start | bytes 57344 | tf_op jit(solution)/shard_map/all_to_all | solution.py:84
  214.8 10.8 %all-to-all-start.6 = ((f32[8,1,864]{2,1,0:T(1,128)}), f32[8,1,864]{2,1,0:T(1,128)}, u32[]{:S(2)}, u32[]{:S(2)}) async-start(f32[8,1,864]{2,1,0:T(1,128)} %broadcast_in_dim.336), calls=%async_computation.6 | async-start | bytes 57344 | tf_op jit(solution)/shard_map/all_to_all | solution.py:90
  229.8 13.0 %all-to-all-start.7 = ((f32[8,54,128]{2,1,0:T(8,128)}), f32[8,54,128]{2,1,0:T(8,128)}, u32[]{:S(2)}, u32[]{:S(2)}) async-start(f32[8,54,128]{2,1,0:T(8,128)} %broadcast_in_dim.338), calls=%async_computation.7 | async-start | bytes 458752 | tf_op jit(solution)/shard_map/all_to_all | solution.py:90
  234.1 2.0 copy-start.29
  242.9 25.5 %all-to-all-start.1 = ((bf16[64,2,1024]{2,1,0:T(2,128)(2,1)}), bf16[64,2,1024]{2,1,0:T(2,128)(2,1)S(1)}, u32[]{:S(2)}, u32[]{:S(2)}) async-start(bf16[64,2,1024]{2,1,0:T(2,128)(2,1)} %reshape.1510), calls=%async_computation.1 | async-start | bytes 524288 | tf_op jit(solution)/shard_map/all_to_all | solution.py:182
  269.3 16.6 %all-to-all-start.8 = ((f32[4,432,128]{2,1,0:T(8,128)}), f32[4,432,128]{2,1,0:T(8,128)S(1)}, u32[]{:S(2)}, u32[]{:S(2)}) async-start(f32[4,432,128]{2,1,0:T(8,128)} %broadcast_in_dim.340), calls=%async_computation.8 | async-start | bytes 1769472 | tf_op jit(solution)/shard_map/all_to_all | solution.py:90

commit v2 on v1

--- a/solution.py
+++ b/solution.py
@@ -76,6 +76,16 @@
     return jnp.concatenate(pieces, -1).reshape(block_count * 512, 27 * channels)
 
 
+def tap_view(padded, shift_x, shift_y, shift_z, direction):
+    channels = padded.shape[-1]
+    start_x = 1 + direction * shift_x
+    start_y = 1 + direction * shift_y
+    start_z = 1 + direction * shift_z
+    return padded[
+        :, start_x : start_x + 8, start_y : start_y + 8, start_z : start_z + 8, :
+    ].reshape(-1, channels)
+
+
 def reduce_everywhere(value, sizes):
     flat = value.reshape(-1)
     for axis in REDUCE_ORDER:
@@ -158,19 +168,28 @@
         from_above = lax.ppermute(faces[..., : 2 * channels], SPACE_AXES, down)
         low_h, low_g = from_below[..., :channels], from_below[..., channels:]
         high_h, high_g = from_above[..., :channels], from_above[..., channels:]
-        columns_h = patch_columns(pad_blocks(blocks_h, low_h, high_h, links_here), 1)
-        columns_g = patch_columns(pad_blocks(blocks_g, low_g, high_g, links_here), -1)
+        padded_h = pad_blocks(blocks_h, low_h, high_h, links_here)
+        padded_g = pad_blocks(blocks_g, low_g, high_g, links_here)
         grads_flat = dense_g
-        grad_part = lax.dot_general(
-            columns_h, grads_flat, (((0,), (0,)), ((), ())), preferred_element_type=jnp.float32
-        )
-        convolved = jnp.dot(
-            columns_h,
-            weights.reshape(27 * channels, channels),
-            preferred_element_type=jnp.float32,
-        )
-        flipped = jnp.transpose(weights, (0, 2, 1)).reshape(27 * channels, channels)
-        backward = jnp.dot(columns_g, flipped, preferred_element_type=jnp.float32)
+        tap_grads = []
+        for shift_x, shift_y, shift_z in ALL_TAPS:
+            view_h = tap_view(padded_h, shift_x, shift_y, shift_z, 1)
+            tap_grads.append(
+                lax.dot_general(
+                    view_h, grads_flat, (((0,), (0,)), ((), ())), preferred_element_type=jnp.float32
+                )
+            )
+        grad_part = jnp.stack(tap_grads, 0)
+        convolved = jnp.zeros((voxels, channels), jnp.float32)
+        backward = jnp.zeros((voxels, channels), jnp.float32)
+        for tap_index, (shift_x, shift_y, shift_z) in enumerate(ALL_TAPS):
+            view_h = tap_view(padded_h, shift_x, shift_y, shift_z, 1)
+            view_g = tap_view(padded_g, shift_x, shift_y, shift_z, -1)
+            tap_weight = weights[tap_index]
+            convolved = convolved + jnp.dot(view_h, tap_weight, preferred_element_type=jnp.float32)
+            backward = backward + lax.dot_general(
+                view_g, tap_weight, (((1,), (1,)), ((), ())), preferred_element_type=jnp.float32
+            )
         out_x = (dense_x.astype(jnp.float32) + convolved).astype(data_type)
         out_dx = (dense_g.astype(jnp.float32) + jnp.where(dense_x > 0, backward, 0.0)).astype(
             data_type

time: 296 us -> 258 us (0.87)
  local copies, waits for them, and re-layouts: 109 us -> 25.1 us
  matrix products: 7.56 us -> 35.1 us
  waiting for transfers between devices: 35.2 us -> 54.1 us
    unnamed x120 -> x108, local copies, waits for them, and re-layouts: 47.2 us -> 3.59 us
    concatenate x54 -> x0, local copies, waits for them, and re-layouts: 39.7 us -> none  [patch_columns(): return jnp.concatenate(pieces, -1).reshape(block_count * 512, 27 * channels)]
    dot_general x3 -> x81, matrix products: 7.56 us -> 35.1 us  [the longest x27 14.3 us: local(): lax.dot_general(view_h, grads_flat, (((0,), (0,)), ((), ())), preferred_e...]
    all_to_all x3, waiting for transfers between devices: 10.5 us -> 23.7 us  [reduce_everywhere(): lax.all_to_all(flat.reshape(count, -1, lanes), axis, 0, 0, tiled=True)]
    all_to_all x3, waiting for transfers between devices: 13.7 us -> 18.4 us  [reduce_everywhere(): flat = lax.all_to_all(spread, axis, 0, 0, tiled=True).reshape(-1)]
    broadcast_in_dim x6, local copies, waits for them, and re-layouts: 5.55 us -> 2.52 us  [reduce_everywhere(): jnp.broadcast_to(flat.reshape(1, -1, lanes), (count, flat.shape[0] // lan...]
  transfers between devices with their start and end apart: 10 -> 10, of which waited for: 6 -> 7; matrix products, arithmetic and copies ran while one was open for 18% -> 9% of each run, Pallas kernels for 0% -> 0%
where the time goes in v2:
time: 258 us; the launch traced here: 255 us
  starting transfers between devices  62.7 us (24%)
  waiting for transfers between devices  54.1 us (21%)
  between operations  51.3 us (20%)
  matrix products  35.1 us (14%)
  local copies, waits for them, and re-layouts  25.1 us (10%)
  other arithmetic  15.6 us (6%)
  blocking collectives  11.1 us (4%)
    all_to_all x3, waiting for transfers between devices, reduce_everywhere(): lax.all_to_all(flat.reshape(count, -1, lanes), axis, 0, 0, tiled=True)  23.7 us
    all_to_all x3, starting transfers between devices, reduce_everywhere(): lax.all_to_all(flat.reshape(count, -1, lanes), axis, 0, 0, tiled=True)  23.3 us
    all_to_all x3, waiting for transfers between devices, reduce_everywhere(): flat = lax.all_to_all(spread, axis, 0, 0, tiled=True).reshape(-1)  18.4 us
    dot_general x27, matrix products, local(): lax.dot_general(view_h, grads_flat, (((0,), (0,)), ((), ())), preferred_e...  14.3 us
    dot_general x27, matrix products, local(): jnp.dot(view_h, tap_weight, preferred_element_type=jnp.float32)  13.6 us
    all_to_all x1, waiting for transfers between devices, local(): lax.all_to_all(ret, SPACE_AXES, 0, 0, tiled=True).reshape(-1, 2 * channels)  12 us
    all_to_all x1, starting transfers between devices, local(): recv = lax.all_to_all(send, SPACE_AXES, 0, 0, tiled=True)  11.6 us
    all_to_all x1, starting transfers between devices, local(): lax.all_to_all(ret, SPACE_AXES, 0, 0, tiled=True).reshape(-1, 2 * channels)  11.1 us
  transfers between devices with their start and end apart: 10, of which 7 were waited for; matrix products, arithmetic and copies ran while one was open for 9% of the time, Pallas kernels for 0%

profile of v2, /device:TPU:1, one launch (start us, length us, event | category | flops | bytes accessed | tf_op | source)
XLA Modules:
  0.0 255.1 jit_solution(4986567351906470121)
XLA Ops:
  2.2 0.8 fusion.43
  3.6 1.6 scatter_custom_fusion.1
  5.3 1.9 scatter_custom_fusion
  8.0 0.8 reduce.5
  8.8 0.8 reshape.1675
  9.6 11.6 %all-to-all-start = ((bf16[64,2,1152]{2,1,0:T(2,128)(2,1)}), bf16[64,2,1152]{2,1,0:T(2,128)(2,1)S(1)}, u32[]{:S(2)}, u32[]{:S(2)}) async-start(bf16[64,2,1152]{2,1,0:T(2,128)(2,1)} %reshape.1675), calls=%async_computation | async-start | bytes 589824 | tf_op jit(solution)/shard_map/all_to_all | solution.py:146
  30.6 0.7 fusion.238
  71.9 2.4 scatter_custom_fusion.2
  75.5 2.4 collective-permute-start.1
  78.8 0.8 pad_maximum_fusion.2
  79.9 0.8 fusion.234
  80.8 0.7 fusion.233
  81.5 0.9 fusion.72
  82.4 0.9 fusion.69
  83.3 0.8 fusion.232
  84.7 0.8 copy.93
  85.5 3.4 %collective-permute-start = (bf16[1,8,8,256]{3,2,1,0:T(8,128)(2,1)S(1)}, bf16[1,8,8,256]{3,2,1,0:T(8,128)(2,1)S(1)}, u32[]{:S(2)}, u32[]{:S(2)}) collective-permute-start(bf16[1,8,8,256]{3,2,1,0:T(8,128)(2,1)S(1)} %pad_maximum_fusion.5), channel_id=1, source_target_pairs={{0,8},{8,16},{16,24},{24,32},{32,40},{40,48},{48,56},{56,64},{64,7... | collective-permute-start | bytes 98312 | tf_op jit(solution)/shard_map/ppermute | solution.py:167
  88.9 0.7 fusion.236
  95.3 1.0 fusion.230
  96.3 0.9 fusion.101
  97.5 1.1 fusion.229
  103.0 1.0 convolution_add_fusion.33
  104.0 1.1 fusion.16
  105.1 1.0 convolution_add_fusion.32
  106.1 1.1 fusion.15
  107.2 1.0 convolution_add_fusion.31
  108.2 1.1 fusion.14
  109.4 1.0 convolution_add_fusion.30
  110.4 1.1 fusion.13
  111.5 1.0 convolution_add_fusion.29
  112.5 1.1 fusion.12
  113.6 1.0 convolution_add_fusion.28
  114.6 1.1 fusion.11
  115.8 1.0 convolution_add_fusion.27
  116.8 1.1 fusion.10
  118.0 1.0 convolution_add_fusion.26
  119.0 1.1 fusion.9
  120.1 1.0 convolution_add_fusion.25
  121.1 1.1 fusion.8
  122.2 0.9 fusion.5
  123.4 4.8 %all_to_all.62 = f32[2,1728,128]{2,1,0:T(8,128)S(1)} all-to-all(f32[2,1728,128]{2,1,0:T(8,128)S(1)} %bitcast.571), channel_id=1, replica_groups=mesh['sx'=4,'sy'=8,'sc'=2,'rep'=8] {'sc'}, dimensions={0} | all-to-all | bytes 3538944 | tf_op jit(solution)/shard_map/all_to_all | solution.py:94
  128.2 1.1 reduce_sum.49
  129.3 9.8 %all-to-all-start.3 = ((f32[4,432,128]{2,1,0:T(8,128)}), f32[4,432,128]{2,1,0:T(8,128)S(1)}, u32[]{:S(2)}, u32[]{:S(2)}) async-start(f32[4,432,128]{2,1,0:T(8,128)} %bitcast.215), calls=%async_computation.3 | async-start | bytes 1769472 | tf_op jit(solution)/shard_map/all_to_all | solution.py:94
  143.1 8.8 %all-to-all-done.3 = f32[4,432,128]{2,1,0:T(8,128)S(1)} async-done(((f32[4,432,128]{2,1,0:T(8,128)}), f32[4,432,128]{2,1,0:T(8,128)S(1)}, u32[]{:S(2)}, u32[]{:S(2)}) %all-to-all-start.3) | async-done | bytes 884768 | tf_op jit(solution)/shard_map/all_to_all | solution.py:94
  152.7 3.4 %all-to-all-start.4 = ((f32[8,54,128]{2,1,0:T(8,128)}), f32[8,54,128]{2,1,0:T(8,128)S(1)}, u32[]{:S(2)}, u32[]{:S(2)}) async-start(f32[8,54,128]{2,1,0:T(8,128)} %reshape_reshape.19), calls=%async_computation.4 | async-start | bytes 458752 | tf_op jit(solution)/shard_map/all_to_all | solution.py:94
  156.5 8.3 %all-to-all-done.4 = f32[8,54,128]{2,1,0:T(8,128)S(1)} async-done(((f32[8,54,128]{2,1,0:T(8,128)}), f32[8,54,128]{2,1,0:T(8,128)S(1)}, u32[]{:S(2)}, u32[]{:S(2)}) %all-to-all-start.4) | async-done | bytes 221216 | tf_op jit(solution)/shard_map/all_to_all | solution.py:94
  165.6 10.0 %all-to-all-start.5 = ((f32[8,1,864]{2,1,0:T(1,128)}), f32[8,1,864]{2,1,0:T(1,128)S(1)}, u32[]{:S(2)}, u32[]{:S(2)}) async-start(f32[8,1,864]{2,1,0:T(1,128)} %reshape_reshape.20), calls=%async_computation.5 | async-start | bytes 57344 | tf_op jit(solution)/shard_map/all_to_all | solution.py:94
  175.9 6.6 %all-to-all-done.5 = f32[8,1,864]{2,1,0:T(1,128)S(1)} async-done(((f32[8,1,864]{2,1,0:T(1,128)}), f32[8,1,864]{2,1,0:T(1,128)S(1)}, u32[]{:S(2)}, u32[]{:S(2)}) %all-to-all-start.5) | async-done | bytes 27680 | tf_op jit(solution)/shard_map/all_to_all | solution.py:94
  183.1 3.3 %all-to-all-start.6 = ((f32[8,1,864]{2,1,0:T(1,128)}), f32[8,1,864]{2,1,0:T(1,128)S(1)}, u32[]{:S(2)}, u32[]{:S(2)}) async-start(f32[8,1,864]{2,1,0:T(1,128)} %broadcast_in_dim.336), calls=%async_computation.6 | async-start | bytes 57344 | tf_op jit(solution)/shard_map/all_to_all | solution.py:100
  186.7 6.5 %all-to-all-done.6 = f32[8,1,864]{2,1,0:T(1,128)S(1)} async-done(((f32[8,1,864]{2,1,0:T(1,128)}), f32[8,1,864]{2,1,0:T(1,128)S(1)}, u32[]{:S(2)}, u32[]{:S(2)}) %all-to-all-start.6) | async-done | bytes 27680 | tf_op jit(solution)/shard_map/all_to_all | solution.py:100
  194.1 3.8 %all-to-all-start.7 = ((f32[8,54,128]{2,1,0:T(8,128)}), f32[8,54,128]{2,1,0:T(8,128)S(1)}, u32[]{:S(2)}, u32[]{:S(2)}) async-start(f32[8,54,128]{2,1,0:T(8,128)} %broadcast_in_dim.338), calls=%async_computation.7 | async-start | bytes 458752 | tf_op jit(solution)/shard_map/all_to_all | solution.py:100
  198.5 2.0 gather_fusion
  200.6 2.1 reduce.6
  202.8 0.9 reshape.1677
  203.6 2.9 %all-to-all-done.7 = f32[8,54,128]{2,1,0:T(8,128)S(1)} async-done(((f32[8,54,128]{2,1,0:T(8,128)}), f32[8,54,128]{2,1,0:T(8,128)S(1)}, u32[]{:S(2)}, u32[]{:S(2)}) %all-to-all-start.7) | async-done | bytes 221216 | tf_op jit(solution)/shard_map/all_to_all | solution.py:100
  206.5 11.1 %all-to-all-start.1 = ((bf16[64,2,1024]{2,1,0:T(2,128)(2,1)}), bf16[64,2,1024]{2,1,0:T(2,128)(2,1)S(1)}, u32[]{:S(2)}, u32[]{:S(2)}) async-start(bf16[64,2,1024]{2,1,0:T(2,128)(2,1)} %reshape.1677), calls=%async_computation.1 | async-start | bytes 524288 | tf_op jit(solution)/shard_map/all_to_all | solution.py:201
  217.7 12.0 %all-to-all-done.1 = bf16[64,2,1024]{2,1,0:T(2,128)(2,1)S(1)} async-done(((bf16[64,2,1024]{2,1,0:T(2,128)(2,1)}), bf16[64,2,1024]{2,1,0:T(2,128)(2,1)S(1)}, u32[]{:S(2)}, u32[]{:S(2)}) %all-to-all-start.1) | async-done | bytes 262176 | tf_op jit(solution)/shard_map/all_to_all | solution.py:201
  229.7 1.0 broadcast_in_dim.340
  230.6 3.9 %all-to-all-start.8 = ((f32[4,432,128]{2,1,0:T(8,128)}), f32[4,432,128]{2,1,0:T(8,128)S(1)}, u32[]{:S(2)}, u32[]{:S(2)}) async-start(f32[4,432,128]{2,1,0:T(8,128)} %broadcast_in_dim.340), calls=%async_computation.8 | async-start | bytes 1769472 | tf_op jit(solution)/shard_map/all_to_all | solution.py:100
  234.7 1.5 reduce.2
  236.4 1.3 gather_fusion.1
  238.3 8.9 %all-to-all-done.8 = f32[4,432,128]{2,1,0:T(8,128)S(1)} async-done(((f32[4,432,128]{2,1,0:T(8,128)}), f32[4,432,128]{2,1,0:T(8,128)S(1)}, u32[]{:S(2)}, u32[]{:S(2)}) %all-to-all-start.8) | async-done | bytes 884768 | tf_op jit(solution)/shard_map/all_to_all | solution.py:100
  247.4 6.3 %all_to_all.63 = f32[2,1728,128]{2,1,0:T(8,128)S(1)} all-to-all(f32[2,1728,128]{2,1,0:T(8,128)S(1)} %broadcast_in_dim.342), channel_id=1, replica_groups=mesh['sx'=4,'sy'=8,'sc'=2,'rep'=8] {'sc'}, dimensions={0} | all-to-all | bytes 3538944 | tf_op jit(solution)/shard_map/all_to_all | solution.py:100
  253.7 1.4 broadcast_multiply_fusion
  (281 shorter events, 26.4 us)
Async XLA Ops:
  2.2 19.0 %copy-start.34 = (s32[1,1,26]{2,1,0:T(1,128)S(1)}, s32[1,1,26]{2,1,0:T(1,128)}, u32[]{:S(2)}) copy-start(s32[1,1,26]{2,1,0:T(1,128)} %param.10) | copy-start | bytes 316
  3.6 5.9 %copy-start.48 = (s32[256,1]{0,1:T(1,128)}, s32[256,1]{0,1:T(1,128)S(1)}, u32[]{:S(2)}) copy-start(s32[256,1]{0,1:T(1,128)S(1)} %compare_select_fusion.1) | copy-start | bytes 3076
  9.6 61.7 %all-to-all-start = ((bf16[64,2,1152]{2,1,0:T(2,128)(2,1)}), bf16[64,2,1152]{2,1,0:T(2,128)(2,1)S(1)}, u32[]{:S(2)}, u32[]{:S(2)}) async-start(bf16[64,2,1152]{2,1,0:T(2,128)(2,1)} %reshape.1675), calls=%async_computation | async-start | bytes 589824 | tf_op jit(solution)/shard_map/all_to_all | solution.py:146
  71.8 2.6 %copy-start.46 = (s32[512,1]{0,1:T(1,128)}, s32[512,1]{0,1:T(1,128)S(1)}, u32[]{:S(2)}) copy-start(s32[512,1]{0,1:T(1,128)S(1)} %compare_select_fusion) | copy-start | bytes 6148
  74.3 28.5 %copy-start = (bf16[513,256]{1,0:T(8,128)(2,1)}, bf16[513,256]{1,0:T(8,128)(2,1)S(1)}, u32[]{:S(2)}) copy-start(bf16[513,256]{1,0:T(8,128)(2,1)S(1)} %scatter_custom_fusion.2) | copy-start | bytes 787972
  75.5 13.4 %collective-permute-start.1 = (bf16[1,8,8,256]{3,2,1,0:T(8,128)(2,1)}, bf16[1,8,8,256]{3,2,1,0:T(8,128)(2,1)}, u32[]{:S(2)}, u32[]{:S(2)}) collective-permute-start(bf16[1,8,8,256]{3,2,1,0:T(8,128)(2,1)} %pad_maximum_fusion.6), channel_id=1, source_target_pairs={{8,0},{16,8},{24,16},{32,24},{40,32},{48,40},{56,48},{64,56},{72,6... | collective-permute-start | bytes 98312 | tf_op jit(solution)/shard_map/ppermute | solution.py:168
  78.1 0.6 copy-start.37
  78.1 2.6 %copy-start.39 = (bf16[1,8,1,1,128]{4,3,2,1,0:T(2,128)(2,1)}, bf16[1,8,1,1,128]{4,3,2,1,0:T(2,128)(2,1)S(1)}, u32[]{:S(2)}) copy-start(bf16[1,8,1,1,128]{4,3,2,1,0:T(2,128)(2,1)S(1)} %get-tuple-element.732) | copy-start | bytes 6148
  78.1 2.6 %copy-start.41 = (bf16[1,8,1,1,128]{4,3,2,1,0:T(2,128)(2,1)}, bf16[1,8,1,1,128]{4,3,2,1,0:T(2,128)(2,1)S(1)}, u32[]{:S(2)}) copy-start(bf16[1,8,1,1,128]{4,3,2,1,0:T(2,128)(2,1)S(1)} %get-tuple-element.729) | copy-start | bytes 6148
  78.1 2.6 %copy-start.43 = (bf16[1,8,1,1,128]{4,3,2,1,0:T(2,128)(2,1)}, bf16[1,8,1,1,128]{4,3,2,1,0:T(2,128)(2,1)S(1)}, u32[]{:S(2)}) copy-start(bf16[1,8,1,1,128]{4,3,2,1,0:T(2,128)(2,1)S(1)} %get-tuple-element.730) | copy-start | bytes 6148
  78.5 3.0 %copy-start.2 = (bf16[27,128,128]{2,1,0:T(8,128)(2,1)S(1)}, bf16[27,128,128]{2,1,0:T(8,128)(2,1)}, u32[]{:S(2)}) copy-start(bf16[27,128,128]{2,1,0:T(8,128)(2,1)} %param.11) | copy-start | bytes 2654212
  78.7 2.0 copy-start.35
  79.9 4.2 %copy-start.47 = (s32[512,1]{0,1:T(1,128)S(1)}, s32[512,1]{0,1:T(1,128)}, u32[]{:S(2)}) copy-start(s32[512,1]{0,1:T(1,128)} %copy-done.46) | copy-start | bytes 6148
  79.9 4.2 %copy-start.49 = (s32[256,1]{0,1:T(1,128)S(1)}, s32[256,1]{0,1:T(1,128)}, u32[]{:S(2)}) copy-start(s32[256,1]{0,1:T(1,128)} %copy-done.48) | copy-start | bytes 3076
  80.7 9.4 %copy-start.38 = (bf16[1,8,1,1,128]{4,3,2,1,0:T(2,128)(2,1)S(1)}, bf16[1,8,1,1,128]{4,3,2,1,0:T(2,128)(2,1)}, u32[]{:S(2)}) copy-start(bf16[1,8,1,1,128]{4,3,2,1,0:T(2,128)(2,1)} %copy-done.37) | copy-start | bytes 6148
  80.7 9.4 %copy-start.40 = (bf16[1,8,1,1,128]{4,3,2,1,0:T(2,128)(2,1)S(1)}, bf16[1,8,1,1,128]{4,3,2,1,0:T(2,128)(2,1)}, u32[]{:S(2)}) copy-start(bf16[1,8,1,1,128]{4,3,2,1,0:T(2,128)(2,1)} %copy-done.39) | copy-start | bytes 6148
  80.8 9.4 %copy-start.42 = (bf16[1,8,1,1,128]{4,3,2,1,0:T(2,128)(2,1)S(1)}, bf16[1,8,1,1,128]{4,3,2,1,0:T(2,128)(2,1)}, u32[]{:S(2)}) copy-start(bf16[1,8,1,1,128]{4,3,2,1,0:T(2,128)(2,1)} %copy-done.41) | copy-start | bytes 6148
  80.8 9.4 %copy-start.44 = (bf16[1,8,1,1,128]{4,3,2,1,0:T(2,128)(2,1)S(1)}, bf16[1,8,1,1,128]{4,3,2,1,0:T(2,128)(2,1)}, u32[]{:S(2)}) copy-start(bf16[1,8,1,1,128]{4,3,2,1,0:T(2,128)(2,1)} %copy-done.43) | copy-start | bytes 6148
  85.5 4.3 %collective-permute-start = (bf16[1,8,8,256]{3,2,1,0:T(8,128)(2,1)S(1)}, bf16[1,8,8,256]{3,2,1,0:T(8,128)(2,1)S(1)}, u32[]{:S(2)}, u32[]{:S(2)}) collective-permute-start(bf16[1,8,8,256]{3,2,1,0:T(8,128)(2,1)S(1)} %pad_maximum_fusion.5), channel_id=1, source_target_pairs={{0,8},{8,16},{16,24},{24,32},{32,40},{40,48},{48,56},{56,64},{64,7... | collective-permute-start | bytes 98312 | tf_op jit(solution)/shard_map/ppermute | solution.py:167
  92.2 1.2 copy-start.5
  92.4 1.2 copy-start.4
  92.7 1.2 copy-start.3
  94.3 0.7 copy-start.36
  115.8 7.3 %copy-start.1 = (bf16[513,256]{1,0:T(8,128)(2,1)S(1)}, bf16[513,256]{1,0:T(8,128)(2,1)}, u32[]{:S(2)}) copy-start(bf16[513,256]{1,0:T(8,128)(2,1)} %copy-done) | copy-start | bytes 787972
  128.2 11.0 %copy-start.8 = (f32[512,128]{0,1:T(8,128)S(1)}, f32[512,128]{0,1:T(8,128)}, u32[]{:S(2)}) copy-start(f32[512,128]{0,1:T(8,128)} %fusion.101) | copy-start | bytes 786436
  129.3 9.9 %copy-start.27 = (bf16[1,8,8,8,128]{4,3,2,1,0:T(8,128)(2,1)S(1)}, bf16[1,8,8,8,128]{4,3,2,1,0:T(8,128)(2,1)}, u32[]{:S(2)}) copy-start(bf16[1,8,8,8,128]{4,3,2,1,0:T(8,128)(2,1)} %get-tuple-element.609) | copy-start | bytes 393220
  129.3 10.1 %copy-start.26 = (bf16[1,8,8,8,128]{4,3,2,1,0:T(8,128)(2,1)S(1)}, bf16[1,8,8,8,128]{4,3,2,1,0:T(8,128)(2,1)}, u32[]{:S(2)}) copy-start(bf16[1,8,8,8,128]{4,3,2,1,0:T(8,128)(2,1)} %get-tuple-element.608) | copy-start | bytes 393220
  129.3 10.3 %copy-start.25 = (bf16[1,8,8,8,128]{4,3,2,1,0:T(8,128)(2,1)S(1)}, bf16[1,8,8,8,128]{4,3,2,1,0:T(8,128)(2,1)}, u32[]{:S(2)}) copy-start(bf16[1,8,8,8,128]{4,3,2,1,0:T(8,128)(2,1)} %get-tuple-element.607) | copy-start | bytes 393220
  129.3 10.5 %copy-start.24 = (bf16[1,8,8,8,128]{4,3,2,1,0:T(8,128)(2,1)S(1)}, bf16[1,8,8,8,128]{4,3,2,1,0:T(8,128)(2,1)}, u32[]{:S(2)}) copy-start(bf16[1,8,8,8,128]{4,3,2,1,0:T(8,128)(2,1)} %get-tuple-element.606) | copy-start | bytes 393220
  129.3 22.6 %all-to-all-start.3 = ((f32[4,432,128]{2,1,0:T(8,128)}), f32[4,432,128]{2,1,0:T(8,128)S(1)}, u32[]{:S(2)}, u32[]{:S(2)}) async-start(f32[4,432,128]{2,1,0:T(8,128)} %bitcast.215), calls=%async_computation.3 | async-start | bytes 1769472 | tf_op jit(solution)/shard_map/all_to_all | solution.py:94
  139.1 0.9 copy-start.23
  139.1 1.1 copy-start.22
  139.3 1.1 copy-start.21
  139.6 1.1 copy-start.20
  139.8 1.1 copy-start.32
  140.0 1.1 copy-start.31
  140.2 1.1 copy-start.30
  140.4 1.1 copy-start.11
  140.7 1.1 copy-start.6
  140.7 1.1 copy-start.7
  141.1 1.0 copy-start.29
  141.3 1.0 copy-start.28
  141.5 1.0 copy-start.19
  141.8 0.9 copy-start.18
  141.8 1.1 copy-start.17
  142.7 13.4 %copy-start.16 = (bf16[1,8,8,8,128]{4,3,2,1,0:T(8,128)(2,1)S(1)}, bf16[1,8,8,8,128]{4,3,2,1,0:T(8,128)(2,1)}, u32[]{:S(2)}) copy-start(bf16[1,8,8,8,128]{4,3,2,1,0:T(8,128)(2,1)} %get-tuple-element.598) | copy-start | bytes 393220
  142.9 13.4 %copy-start.15 = (bf16[1,8,8,8,128]{4,3,2,1,0:T(8,128)(2,1)S(1)}, bf16[1,8,8,8,128]{4,3,2,1,0:T(8,128)(2,1)}, u32[]{:S(2)}) copy-start(bf16[1,8,8,8,128]{4,3,2,1,0:T(8,128)(2,1)} %get-tuple-element.597) | copy-start | bytes 393220
  143.1 32.5 %copy-start.14 = (bf16[1,8,8,8,128]{4,3,2,1,0:T(8,128)(2,1)S(1)}, bf16[1,8,8,8,128]{4,3,2,1,0:T(8,128)(2,1)}, u32[]{:S(2)}) copy-start(bf16[1,8,8,8,128]{4,3,2,1,0:T(8,128)(2,1)} %get-tuple-element.596) | copy-start | bytes 393220
  152.0 34.5 %copy-start.13 = (bf16[1,8,8,8,128]{4,3,2,1,0:T(8,128)(2,1)S(1)}, bf16[1,8,8,8,128]{4,3,2,1,0:T(8,128)(2,1)}, u32[]{:S(2)}) copy-start(bf16[1,8,8,8,128]{4,3,2,1,0:T(8,128)(2,1)} %get-tuple-element.595) | copy-start | bytes 393220
  152.7 12.2 %all-to-all-start.4 = ((f32[8,54,128]{2,1,0:T(8,128)}), f32[8,54,128]{2,1,0:T(8,128)S(1)}, u32[]{:S(2)}, u32[]{:S(2)}) async-start(f32[8,54,128]{2,1,0:T(8,128)} %reshape_reshape.19), calls=%async_computation.4 | async-start | bytes 458752 | tf_op jit(solution)/shard_map/all_to_all | solution.py:94
  156.3 41.6 %copy-start.12 = (bf16[1,8,8,8,128]{4,3,2,1,0:T(8,128)(2,1)S(1)}, bf16[1,8,8,8,128]{4,3,2,1,0:T(8,128)(2,1)}, u32[]{:S(2)}) copy-start(bf16[1,8,8,8,128]{4,3,2,1,0:T(8,128)(2,1)} %get-tuple-element.594) | copy-start | bytes 393220
  156.5 41.6 %copy-start.9 = (bf16[1,8,8,8,128]{4,3,2,1,0:T(8,128)(2,1)S(1)}, bf16[1,8,8,8,128]{4,3,2,1,0:T(8,128)(2,1)}, u32[]{:S(2)}) copy-start(bf16[1,8,8,8,128]{4,3,2,1,0:T(8,128)(2,1)} %get-tuple-element.593) | copy-start | bytes 393220
  156.5 41.6 %copy-start.10 = (bf16[512,128]{0,1:T(8,128)(2,1)S(1)}, bf16[512,128]{0,1:T(8,128)(2,1)}, u32[]{:S(2)}) copy-start(bf16[512,128]{0,1:T(8,128)(2,1)} %copy.93) | copy-start | bytes 393220
  165.6 16.9 %all-to-all-start.5 = ((f32[8,1,864]{2,1,0:T(1,128)}), f32[8,1,864]{2,1,0:T(1,128)S(1)}, u32[]{:S(2)}, u32[]{:S(2)}) async-start(f32[8,1,864]{2,1,0:T(1,128)} %reshape_reshape.20), calls=%async_computation.5 | async-start | bytes 57344 | tf_op jit(solution)/shard_map/all_to_all | solution.py:94
  175.7 22.7 %copy-start.33 = (bf16[512,128]{0,1:T(8,128)(2,1)S(1)}, bf16[512,128]{0,1:T(8,128)(2,1)}, u32[]{:S(2)}) copy-start(bf16[512,128]{0,1:T(8,128)(2,1)} %fusion.5) | copy-start | bytes 393220
  183.1 10.1 %all-to-all-start.6 = ((f32[8,1,864]{2,1,0:T(1,128)}), f32[8,1,864]{2,1,0:T(1,128)S(1)}, u32[]{:S(2)}, u32[]{:S(2)}) async-start(f32[8,1,864]{2,1,0:T(1,128)} %broadcast_in_dim.336), calls=%async_computation.6 | async-start | bytes 57344 | tf_op jit(solution)/shard_map/all_to_all | solution.py:100
  194.1 4.4 %copy-start.45 = (s32[1024]{0:T(1024)S(1)}, s32[1024]{0:T(1024)}, u32[]{:S(2)}) copy-start(s32[1024]{0:T(1024)} %get-tuple-element.738) | copy-start | bytes 12292
  194.1 12.4 %all-to-all-start.7 = ((f32[8,54,128]{2,1,0:T(8,128)}), f32[8,54,128]{2,1,0:T(8,128)S(1)}, u32[]{:S(2)}, u32[]{:S(2)}) async-start(f32[8,54,128]{2,1,0:T(8,128)} %broadcast_in_dim.338), calls=%async_computation.7 | async-start | bytes 458752 | tf_op jit(solution)/shard_map/all_to_all | solution.py:100
  206.5 23.1 %all-to-all-start.1 = ((bf16[64,2,1024]{2,1,0:T(2,128)(2,1)}), bf16[64,2,1024]{2,1,0:T(2,128)(2,1)S(1)}, u32[]{:S(2)}, u32[]{:S(2)}) async-start(bf16[64,2,1024]{2,1,0:T(2,128)(2,1)} %reshape.1677), calls=%async_computation.1 | async-start | bytes 524288 | tf_op jit(solution)/shard_map/all_to_all | solution.py:201
  230.6 16.7 %all-to-all-start.8 = ((f32[4,432,128]{2,1,0:T(8,128)}), f32[4,432,128]{2,1,0:T(8,128)S(1)}, u32[]{:S(2)}, u32[]{:S(2)}) async-start(f32[4,432,128]{2,1,0:T(8,128)} %broadcast_in_dim.340), calls=%async_computation.8 | async-start | bytes 1769472 | tf_op jit(solution)/shard_map/all_to_all | solution.py:100

commit v3 on v2

--- a/solution.py
+++ b/solution.py
@@ -86,9 +86,11 @@
     ].reshape(-1, channels)
 
 
-def reduce_everywhere(value, sizes):
+def reduce_everywhere(value, sizes, held=None):
     flat = value.reshape(-1)
-    for axis in REDUCE_ORDER:
+    for stage, axis in enumerate(REDUCE_ORDER):
+        if stage == 1 and held is not None:
+            flat, held = lax.optimization_barrier((flat, held))
         count = sizes[axis]
         lanes = 128 if flat.shape[0] % (count * 128) == 0 else flat.shape[0] // count
         parts = lax.all_to_all(flat.reshape(count, -1, lanes), axis, 0, 0, tiled=True)
@@ -98,7 +100,7 @@
         lanes = 128 if flat.shape[0] % 128 == 0 else flat.shape[0]
         spread = jnp.broadcast_to(flat.reshape(1, -1, lanes), (count, flat.shape[0] // lanes, lanes))
         flat = lax.all_to_all(spread, axis, 0, 0, tiled=True).reshape(-1)
-    return flat.reshape(value.shape)
+    return flat.reshape(value.shape), held
 
 
 def make_local(sizes):
@@ -180,6 +182,9 @@
                 )
             )
         grad_part = jnp.stack(tap_grads, 0)
+        summed, (padded_h, padded_g, dense_x, dense_g) = reduce_everywhere(
+            grad_part, sizes, (padded_h, padded_g, dense_x, dense_g)
+        )
         convolved = jnp.zeros((voxels, channels), jnp.float32)
         backward = jnp.zeros((voxels, channels), jnp.float32)
         for tap_index, (shift_x, shift_y, shift_z) in enumerate(ALL_TAPS):
@@ -202,7 +207,6 @@
         final = home[bucket]
         final_x = final[:, :channels]
         final_dx = final[:, channels:]
-        summed = reduce_everywhere(grad_part, sizes)
         norm_scale = 1.0 / math.sqrt(peer_count * rep_count * owners.shape[0])
         weight_grad = (summed * norm_scale).reshape(27, channels, channels)
         return (final_x[None], final_dx[None], weight_grad)

time: 258 us -> 238 us (0.922)
  matrix products: 35.1 us -> 21.1 us
  blocking collectives: 11.1 us -> 6.3 us
  waiting for transfers between devices: 54.1 us -> 49.9 us
  local copies, waits for them, and re-layouts: 25.1 us -> 29.3 us
    dot_general x27, matrix products: 14.3 us -> 6.1 us  [local(): lax.dot_general(view_h, grads_flat, (((0,), (0,)), ((), ())), preferred_e...]
    all_to_all x3 -> x4, waiting for transfers between devices: 23.7 us -> 16.6 us  [reduce_everywhere(): lax.all_to_all(flat.reshape(count, -1, lanes), axis, 0, 0, tiled=True)]
    dot_general x27, matrix products: 13.6 us -> 7.01 us  [local(): jnp.dot(view_h, tap_weight, preferred_element_type=jnp.float32)]
    all_to_all x1 -> x0, blocking collectives: 4.79 us -> none  [reduce_everywhere(): lax.all_to_all(flat.reshape(count, -1, lanes), axis, 0, 0, tiled=True)]
    ppermute x1, waiting for transfers between devices: 0.01 us -> 3.06 us  [local(): from_above = lax.ppermute(faces[..., :2 * channels], SPACE_AXES, down)]
    all_to_all x3 -> x4, starting transfers between devices: 23.3 us -> 24.5 us  [reduce_everywhere(): lax.all_to_all(flat.reshape(count, -1, lanes), axis, 0, 0, tiled=True)]
  transfers between devices with their start and end apart: 10 -> 11, of which waited for: 7 -> 8; matrix products, arithmetic and copies ran while one was open for 9% -> 12% of each run, Pallas kernels for 0% -> 0%
where the time goes in v3:
time: 238 us; the launch traced here: 236 us
  starting transfers between devices  64.9 us (27%)
  between operations  51 us (21%)
  waiting for transfers between devices  49.9 us (21%)
  local copies, waits for them, and re-layouts  29.3 us (12%)
  matrix products  21.1 us (9%)
  other arithmetic  13.9 us (6%)
  blocking collectives  6.3 us (3%)
    all_to_all x4, starting transfers between devices, reduce_everywhere(): lax.all_to_all(flat.reshape(count, -1, lanes), axis, 0, 0, tiled=True)  24.5 us
    all_to_all x3, waiting for transfers between devices, reduce_everywhere(): flat = lax.all_to_all(spread, axis, 0, 0, tiled=True).reshape(-1)  18.3 us
    all_to_all x4, waiting for transfers between devices, reduce_everywhere(): lax.all_to_all(flat.reshape(count, -1, lanes), axis, 0, 0, tiled=True)  16.6 us
    all_to_all x1, starting transfers between devices, local(): lax.all_to_all(ret, SPACE_AXES, 0, 0, tiled=True).reshape(-1, 2 * channels)  12.2 us
    all_to_all x1, waiting for transfers between devices, local(): lax.all_to_all(ret, SPACE_AXES, 0, 0, tiled=True).reshape(-1, 2 * channels)  11.9 us
    all_to_all x1, starting transfers between devices, local(): recv = lax.all_to_all(send, SPACE_AXES, 0, 0, tiled=True)  11.6 us
    all_to_all x3, starting transfers between devices, reduce_everywhere(): flat = lax.all_to_all(spread, axis, 0, 0, tiled=True).reshape(-1)  10.9 us
    dot_general x27, matrix products, local(): lax.dot_general(view_g, tap_weight, (((1,), (1,)), ((), ())), preferred_e...  7.98 us
  transfers between devices with their start and end apart: 11, of which 8 were waited for; matrix products, arithmetic and copies ran while one was open for 12% of the time, Pallas kernels for 0%

profile of v3, /device:TPU:1, one launch (start us, length us, event | category | flops | bytes accessed | tf_op | source)
XLA Modules:
  0.0 236.4 jit_solution(3148672215419476635)
XLA Ops:
  0.6 0.7 fusion.42
  1.3 0.6 reduce-window.6
  2.2 0.8 fusion.41
  3.0 0.7 compare_select_fusion.1
  3.6 1.9 scatter_custom_fusion
  5.7 1.6 scatter_custom_fusion.1
  7.5 0.5 broadcast.1054
  8.0 0.8 reduce.5
  8.8 0.8 reshape.1768
  9.5 11.6 %all-to-all-start = ((bf16[64,2,1152]{2,1,0:T(2,128)(2,1)}), bf16[64,2,1152]{2,1,0:T(2,128)(2,1)S(1)}, u32[]{:S(2)}, u32[]{:S(2)}) async-start(bf16[64,2,1152]{2,1,0:T(2,128)(2,1)} %reshape.1768), calls=%async_computation | async-start | bytes 589824 | tf_op jit(solution)/shard_map/all_to_all | solution.py:148
  21.2 0.7 fusion.233
  33.8 0.7 fusion.234
  71.2 2.4 scatter_custom_fusion.2
  74.2 0.6 pad_clamp_fusion
  74.8 3.5 %collective-permute-start = (bf16[1,8,8,256]{3,2,1,0:T(8,128)(2,1)S(1)}, bf16[1,8,8,256]{3,2,1,0:T(8,128)(2,1)S(1)}, u32[]{:S(2)}, u32[]{:S(2)}) collective-permute-start(bf16[1,8,8,256]{3,2,1,0:T(8,128)(2,1)S(1)} %pad_maximum_fusion.3), channel_id=1, source_target_pairs={{0,8},{8,16},{16,24},{24,32},{32,40},{40,48},{48,56},{56,64},{64,7... | collective-permute-start | bytes 98312 | tf_op jit(solution)/shard_map/ppermute | solution.py:169
  78.6 0.3 maximum_maximum_fusion.5
  78.9 0.8 fusion.229
  79.8 0.7 fusion.228
  80.5 0.6 constant_dynamic-slice_fusion.8
  81.2 0.6 constant_dynamic-slice_fusion.13
  81.9 2.1 collective-permute-start.1
  84.1 3.1 %collective-permute-done.1 = bf16[1,8,8,256]{3,2,1,0:T(8,128)(2,1)S(1)} collective-permute-done((bf16[1,8,8,256]{3,2,1,0:T(8,128)(2,1)S(1)}, bf16[1,8,8,256]{3,2,1,0:T(8,128)(2,1)S(1)}, u32[]{:S(2)}, u32[]{:S(2)}) %collective-permute-start.1) | collective-permute-done | bytes 32800 | tf_op jit(solution)/shard_map/ppermute | solution.py:170
  88.0 0.3 maximum_maximum_fusion
  88.3 0.6 pad_slice_fusion.23
  89.0 0.6 pad_slice_fusion.31
  96.4 1.2 copy-done.1
  97.7 3.7 %all-to-all-start.1 = ((f32[2,1728,128]{2,1,0:T(8,128)}), f32[2,1728,128]{2,1,0:T(8,128)S(1)}, u32[]{:S(2)}, u32[]{:S(2)}) async-start(f32[2,1728,128]{2,1,0:T(8,128)} %bitcast.597), calls=%async_computation.1 | async-start | bytes 3538944 | tf_op jit(solution)/shard_map/all_to_all | solution.py:96
  101.8 0.3 maximum_maximum_fusion.1
  102.0 1.6 all-to-all-done.1
  103.6 1.1 reduce_sum.49
  104.7 1.0 fusion.225
  105.8 1.5 fusion.224
  107.3 1.0 fusion.223
  108.3 1.5 fusion.222
  110.4 5.1 %all-to-all-start.3 = ((f32[4,432,128]{2,1,0:T(8,128)}), f32[4,432,128]{2,1,0:T(8,128)S(1)}, u32[]{:S(2)}, u32[]{:S(2)}) async-start(f32[4,432,128]{2,1,0:T(8,128)} %bitcast.244), calls=%async_computation.3 | async-start | bytes 1769472 | tf_op jit(solution)/shard_map/all_to_all | solution.py:96
  115.5 1.1 convolution_add_fusion.25
  116.6 1.1 convolution_add_fusion.24
  117.8 1.1 convolution_add_fusion.23
  129.1 0.7 reshape_reshape.7
  129.8 5.7 %all-to-all-start.4 = ((f32[8,54,128]{2,1,0:T(8,128)}), f32[8,54,128]{2,1,0:T(8,128)S(1)}, u32[]{:S(2)}, u32[]{:S(2)}) async-start(f32[8,54,128]{2,1,0:T(8,128)} %reshape_reshape.7), calls=%async_computation.4 | async-start | bytes 458752 | tf_op jit(solution)/shard_map/all_to_all | solution.py:96
  135.5 1.1 convolution_add_fusion.30
  136.9 8.4 %all-to-all-done.4 = f32[8,54,128]{2,1,0:T(8,128)S(1)} async-done(((f32[8,54,128]{2,1,0:T(8,128)}), f32[8,54,128]{2,1,0:T(8,128)S(1)}, u32[]{:S(2)}, u32[]{:S(2)}) %all-to-all-start.4) | async-done | bytes 221216 | tf_op jit(solution)/shard_map/all_to_all | solution.py:96
  145.3 0.7 reshape_reshape.16
  146.0 10.0 %all-to-all-start.5 = ((f32[8,1,864]{2,1,0:T(1,128)}), f32[8,1,864]{2,1,0:T(1,128)S(1)}, u32[]{:S(2)}, u32[]{:S(2)}) async-start(f32[8,1,864]{2,1,0:T(1,128)} %reshape_reshape.16), calls=%async_computation.5 | async-start | bytes 57344 | tf_op jit(solution)/shard_map/all_to_all | solution.py:96
  156.3 6.6 %all-to-all-done.5 = f32[8,1,864]{2,1,0:T(1,128)S(1)} async-done(((f32[8,1,864]{2,1,0:T(1,128)}), f32[8,1,864]{2,1,0:T(1,128)S(1)}, u32[]{:S(2)}, u32[]{:S(2)}) %all-to-all-start.5) | async-done | bytes 27680 | tf_op jit(solution)/shard_map/all_to_all | solution.py:96
  162.9 0.6 broadcast_in_dim.336
  163.5 3.6 %all-to-all-start.6 = ((f32[8,1,864]{2,1,0:T(1,128)}), f32[8,1,864]{2,1,0:T(1,128)S(1)}, u32[]{:S(2)}, u32[]{:S(2)}) async-start(f32[8,1,864]{2,1,0:T(1,128)} %broadcast_in_dim.336), calls=%async_computation.6 | async-start | bytes 57344 | tf_op jit(solution)/shard_map/all_to_all | solution.py:102
  167.3 6.2 %all-to-all-done.6 = f32[8,1,864]{2,1,0:T(1,128)S(1)} async-done(((f32[8,1,864]{2,1,0:T(1,128)}), f32[8,1,864]{2,1,0:T(1,128)S(1)}, u32[]{:S(2)}, u32[]{:S(2)}) %all-to-all-start.6) | async-done | bytes 27680 | tf_op jit(solution)/shard_map/all_to_all | solution.py:102
  173.7 0.7 broadcast_in_dim.338
  174.4 3.5 %all-to-all-start.7 = ((f32[8,54,128]{2,1,0:T(8,128)}), f32[8,54,128]{2,1,0:T(8,128)S(1)}, u32[]{:S(2)}, u32[]{:S(2)}) async-start(f32[8,54,128]{2,1,0:T(8,128)} %broadcast_in_dim.338), calls=%async_computation.7 | async-start | bytes 458752 | tf_op jit(solution)/shard_map/all_to_all | solution.py:102
  178.6 2.0 gather_fusion
  180.7 2.1 reduce.6
  182.9 0.9 reshape.1770
  183.8 3.1 %all-to-all-done.7 = f32[8,54,128]{2,1,0:T(8,128)S(1)} async-done(((f32[8,54,128]{2,1,0:T(8,128)}), f32[8,54,128]{2,1,0:T(8,128)S(1)}, u32[]{:S(2)}, u32[]{:S(2)}) %all-to-all-start.7) | async-done | bytes 221216 | tf_op jit(solution)/shard_map/all_to_all | solution.py:102
  186.9 12.2 %all-to-all-start.2 = ((bf16[64,2,1024]{2,1,0:T(2,128)(2,1)}), bf16[64,2,1024]{2,1,0:T(2,128)(2,1)S(1)}, u32[]{:S(2)}, u32[]{:S(2)}) async-start(bf16[64,2,1024]{2,1,0:T(2,128)(2,1)} %reshape.1770), calls=%async_computation.2 | async-start | bytes 524288 | tf_op jit(solution)/shard_map/all_to_all | solution.py:206
  199.1 11.9 %all-to-all-done.2 = bf16[64,2,1024]{2,1,0:T(2,128)(2,1)S(1)} async-done(((bf16[64,2,1024]{2,1,0:T(2,128)(2,1)}), bf16[64,2,1024]{2,1,0:T(2,128)(2,1)S(1)}, u32[]{:S(2)}, u32[]{:S(2)}) %all-to-all-start.2) | async-done | bytes 262176 | tf_op jit(solution)/shard_map/all_to_all | solution.py:206
  211.1 1.0 broadcast_in_dim.340
  212.0 3.8 %all-to-all-start.8 = ((f32[4,432,128]{2,1,0:T(8,128)}), f32[4,432,128]{2,1,0:T(8,128)S(1)}, u32[]{:S(2)}, u32[]{:S(2)}) async-start(f32[4,432,128]{2,1,0:T(8,128)} %broadcast_in_dim.340), calls=%async_computation.8 | async-start | bytes 1769472 | tf_op jit(solution)/shard_map/all_to_all | solution.py:102
  216.1 1.5 reduce.2
  217.7 1.3 gather_fusion.1
  219.0 0.7 slice_bitcast_fusion
  219.7 8.9 %all-to-all-done.8 = f32[4,432,128]{2,1,0:T(8,128)S(1)} async-done(((f32[4,432,128]{2,1,0:T(8,128)}), f32[4,432,128]{2,1,0:T(8,128)S(1)}, u32[]{:S(2)}, u32[]{:S(2)}) %all-to-all-start.8) | async-done | bytes 884768 | tf_op jit(solution)/shard_map/all_to_all | solution.py:102
  228.7 6.3 %all_to_all.62 = f32[2,1728,128]{2,1,0:T(8,128)S(1)} all-to-all(f32[2,1728,128]{2,1,0:T(8,128)S(1)} %broadcast_in_dim.342), channel_id=1, replica_groups=mesh['sx'=4,'sy'=8,'sc'=2,'rep'=8] {'sc'}, dimensions={0} | all-to-all | bytes 3538944 | tf_op jit(solution)/shard_map/all_to_all | solution.py:102
  235.0 1.4 broadcast_multiply_fusion
  (306 shorter events, 21.5 us)
Async XLA Ops:
  2.2 19.0 %copy-start.51 = (s32[1,1,26]{2,1,0:T(1,128)S(1)}, s32[1,1,26]{2,1,0:T(1,128)}, u32[]{:S(2)}) copy-start(s32[1,1,26]{2,1,0:T(1,128)} %param.10) | copy-start | bytes 316
  9.5 61.0 %all-to-all-start = ((bf16[64,2,1152]{2,1,0:T(2,128)(2,1)}), bf16[64,2,1152]{2,1,0:T(2,128)(2,1)S(1)}, u32[]{:S(2)}, u32[]{:S(2)}) async-start(bf16[64,2,1152]{2,1,0:T(2,128)(2,1)} %reshape.1768), calls=%async_computation | async-start | bytes 589824 | tf_op jit(solution)/shard_map/all_to_all | solution.py:148
  74.8 9.2 %collective-permute-start = (bf16[1,8,8,256]{3,2,1,0:T(8,128)(2,1)S(1)}, bf16[1,8,8,256]{3,2,1,0:T(8,128)(2,1)S(1)}, u32[]{:S(2)}, u32[]{:S(2)}) collective-permute-start(bf16[1,8,8,256]{3,2,1,0:T(8,128)(2,1)S(1)} %pad_maximum_fusion.3), channel_id=1, source_target_pairs={{0,8},{8,16},{16,24},{24,32},{32,40},{40,48},{48,56},{56,64},{64,7... | collective-permute-start | bytes 98312 | tf_op jit(solution)/shard_map/ppermute | solution.py:169
  81.9 5.2 %collective-permute-start.1 = (bf16[1,8,8,256]{3,2,1,0:T(8,128)(2,1)S(1)}, bf16[1,8,8,256]{3,2,1,0:T(8,128)(2,1)S(1)}, u32[]{:S(2)}, u32[]{:S(2)}) collective-permute-start(bf16[1,8,8,256]{3,2,1,0:T(8,128)(2,1)S(1)} %pad_maximum_fusion.4), channel_id=1, source_target_pairs={{8,0},{16,8},{24,16},{32,24},{40,32},{48,40},{56,48},{64,56},{72,6... | collective-permute-start | bytes 98312 | tf_op jit(solution)/shard_map/ppermute | solution.py:170
  89.8 2.1 copy-start.50
  89.8 2.4 %copy-start.49 = (bf16[1,8,8,8,128]{4,3,2,1,0:T(8,128)(2,1)S(1)}, bf16[1,8,8,8,128]{4,3,2,1,0:T(8,128)(2,1)}, u32[]{:S(2)}) copy-start(bf16[1,8,8,8,128]{4,3,2,1,0:T(8,128)(2,1)} %get-tuple-element.661) | copy-start | bytes 393220
  89.8 2.6 %copy-start.48 = (bf16[1,8,8,8,128]{4,3,2,1,0:T(8,128)(2,1)S(1)}, bf16[1,8,8,8,128]{4,3,2,1,0:T(8,128)(2,1)}, u32[]{:S(2)}) copy-start(bf16[1,8,8,8,128]{4,3,2,1,0:T(8,128)(2,1)} %get-tuple-element.660) | copy-start | bytes 393220
  92.4 1.1 copy-start.47
  92.7 1.1 copy-start.46
  96.4 1.2 copy-start.1
  97.6 3.8 %copy-start.62 = (bf16[2,1,1,128]{3,2,1,0:T(2,128)(2,1)S(1)}, bf16[2,1,1,128]{3,2,1,0:T(2,128)(2,1)}, u32[]{:S(2)}) copy-start(bf16[2,1,1,128]{3,2,1,0:T(2,128)(2,1)} %get-tuple-element.708) | copy-start | bytes 1540
  97.6 3.8 %copy-start.61 = (bf16[2,1,1,128]{3,2,1,0:T(2,128)(2,1)S(1)}, bf16[2,1,1,128]{3,2,1,0:T(2,128)(2,1)}, u32[]{:S(2)}) copy-start(bf16[2,1,1,128]{3,2,1,0:T(2,128)(2,1)} %get-tuple-element.707) | copy-start | bytes 1540
  97.6 3.9 %copy-start.59 = (bf16[2,1,1,128]{3,2,1,0:T(2,128)(2,1)S(1)}, bf16[2,1,1,128]{3,2,1,0:T(2,128)(2,1)}, u32[]{:S(2)}) copy-start(bf16[2,1,1,128]{3,2,1,0:T(2,128)(2,1)} %get-tuple-element.706) | copy-start | bytes 1540
  97.6 4.0 %copy-start.57 = (bf16[2,1,1,128]{3,2,1,0:T(2,128)(2,1)S(1)}, bf16[2,1,1,128]{3,2,1,0:T(2,128)(2,1)}, u32[]{:S(2)}) copy-start(bf16[2,1,1,128]{3,2,1,0:T(2,128)(2,1)} %get-tuple-element.705) | copy-start | bytes 1540
  97.6 4.0 %copy-start.60 = (bf16[2,1,1,128]{3,2,1,0:T(2,128)(2,1)S(1)}, bf16[2,1,1,128]{3,2,1,0:T(2,128)(2,1)}, u32[]{:S(2)}) copy-start(bf16[2,1,1,128]{3,2,1,0:T(2,128)(2,1)} %get-tuple-element.700) | copy-start | bytes 1540
  97.6 4.0 %copy-start.58 = (bf16[2,1,1,128]{3,2,1,0:T(2,128)(2,1)S(1)}, bf16[2,1,1,128]{3,2,1,0:T(2,128)(2,1)}, u32[]{:S(2)}) copy-start(bf16[2,1,1,128]{3,2,1,0:T(2,128)(2,1)} %get-tuple-element.699) | copy-start | bytes 1540
  97.6 4.1 %copy-start.52 = (bf16[1,8,1,1,128]{4,3,2,1,0:T(2,128)(2,1)S(1)}, bf16[1,8,1,1,128]{4,3,2,1,0:T(2,128)(2,1)}, u32[]{:S(2)}) copy-start(bf16[1,8,1,1,128]{4,3,2,1,0:T(2,128)(2,1)} %get-tuple-element.765) | copy-start | bytes 6148
  97.6 4.1 %copy-start.53 = (bf16[1,8,1,1,128]{4,3,2,1,0:T(2,128)(2,1)S(1)}, bf16[1,8,1,1,128]{4,3,2,1,0:T(2,128)(2,1)}, u32[]{:S(2)}) copy-start(bf16[1,8,1,1,128]{4,3,2,1,0:T(2,128)(2,1)} %get-tuple-element.766) | copy-start | bytes 6148
  97.6 4.1 %copy-start.54 = (bf16[1,8,1,1,128]{4,3,2,1,0:T(2,128)(2,1)S(1)}, bf16[1,8,1,1,128]{4,3,2,1,0:T(2,128)(2,1)}, u32[]{:S(2)}) copy-start(bf16[1,8,1,1,128]{4,3,2,1,0:T(2,128)(2,1)} %get-tuple-element.767) | copy-start | bytes 6148
  97.6 4.1 %copy-start.55 = (bf16[1,8,1,1,128]{4,3,2,1,0:T(2,128)(2,1)S(1)}, bf16[1,8,1,1,128]{4,3,2,1,0:T(2,128)(2,1)}, u32[]{:S(2)}) copy-start(bf16[1,8,1,1,128]{4,3,2,1,0:T(2,128)(2,1)} %get-tuple-element.768) | copy-start | bytes 6148
  97.7 6.0 %all-to-all-start.1 = ((f32[2,1728,128]{2,1,0:T(8,128)}), f32[2,1728,128]{2,1,0:T(8,128)S(1)}, u32[]{:S(2)}, u32[]{:S(2)}) async-start(f32[2,1728,128]{2,1,0:T(8,128)} %bitcast.597), calls=%async_computation.1 | async-start | bytes 3538944 | tf_op jit(solution)/shard_map/all_to_all | solution.py:96
  108.3 1.7 copy-start
  110.4 18.7 %all-to-all-start.3 = ((f32[4,432,128]{2,1,0:T(8,128)}), f32[4,432,128]{2,1,0:T(8,128)S(1)}, u32[]{:S(2)}, u32[]{:S(2)}) async-start(f32[4,432,128]{2,1,0:T(8,128)} %bitcast.244), calls=%async_computation.3 | async-start | bytes 1769472 | tf_op jit(solution)/shard_map/all_to_all | solution.py:96
  115.5 3.5 %copy-start.45 = (bf16[1,8,8,8,128]{4,3,2,1,0:T(8,128)(2,1)S(1)}, bf16[1,8,8,8,128]{4,3,2,1,0:T(8,128)(2,1)}, u32[]{:S(2)}) copy-start(bf16[1,8,8,8,128]{4,3,2,1,0:T(8,128)(2,1)} %get-tuple-element.634) | copy-start | bytes 393220
  115.5 3.7 %copy-start.44 = (bf16[1,8,8,8,128]{4,3,2,1,0:T(8,128)(2,1)S(1)}, bf16[1,8,8,8,128]{4,3,2,1,0:T(8,128)(2,1)}, u32[]{:S(2)}) copy-start(bf16[1,8,8,8,128]{4,3,2,1,0:T(8,128)(2,1)} %get-tuple-element.633) | copy-start | bytes 393220
  115.5 3.9 %copy-start.43 = (bf16[1,8,8,8,128]{4,3,2,1,0:T(8,128)(2,1)S(1)}, bf16[1,8,8,8,128]{4,3,2,1,0:T(8,128)(2,1)}, u32[]{:S(2)}) copy-start(bf16[1,8,8,8,128]{4,3,2,1,0:T(8,128)(2,1)} %get-tuple-element.632) | copy-start | bytes 393220
  116.6 3.0 %copy-start.42 = (bf16[1,8,8,8,128]{4,3,2,1,0:T(8,128)(2,1)S(1)}, bf16[1,8,8,8,128]{4,3,2,1,0:T(8,128)(2,1)}, u32[]{:S(2)}) copy-start(bf16[1,8,8,8,128]{4,3,2,1,0:T(8,128)(2,1)} %get-tuple-element.631) | copy-start | bytes 393220
  117.8 2.0 copy-start.41
  118.9 1.1 copy-start.40
  119.1 1.1 copy-start.39
  120.0 1.1 copy-start.35
  120.2 1.1 copy-start.34
  120.4 1.1 copy-start.33
  120.7 1.1 copy-start.32
  122.0 1.1 copy-start.26
  122.6 1.1 copy-start.25
  122.8 1.1 copy-start.23
  123.1 1.2 copy-start.21
  123.3 1.2 copy-start.20
  123.5 1.2 copy-start.19
  123.7 1.3 copy-start.18
  124.0 1.3 copy-start.17
  124.2 1.3 copy-start.16
  124.5 1.3 copy-start.15
  124.7 1.3 copy-start.14
  125.0 1.3 copy-start.13
  125.3 1.3 copy-start.12
  125.5 1.3 copy-start.11
  125.8 1.3 copy-start.10
  126.0 1.3 copy-start.9
  126.3 1.3 copy-start.8
  126.5 1.3 copy-start.7
  126.8 1.3 copy-start.6
  127.0 1.3 copy-start.5
  127.3 1.2 copy-start.4
  127.5 1.2 copy-start.3
  128.8 7.9 %copy-start.2 = (bf16[1,8,8,8,128]{4,3,2,1,0:T(8,128)(2,1)S(1)}, bf16[1,8,8,8,128]{4,3,2,1,0:T(8,128)(2,1)}, u32[]{:S(2)}) copy-start(bf16[1,8,8,8,128]{4,3,2,1,0:T(8,128)(2,1)} %get-tuple-element.588) | copy-start | bytes 393220
  129.8 15.5 %all-to-all-start.4 = ((f32[8,54,128]{2,1,0:T(8,128)}), f32[8,54,128]{2,1,0:T(8,128)S(1)}, u32[]{:S(2)}, u32[]{:S(2)}) async-start(f32[8,54,128]{2,1,0:T(8,128)} %reshape_reshape.7), calls=%async_computation.4 | async-start | bytes 458752 | tf_op jit(solution)/shard_map/all_to_all | solution.py:96
  146.0 16.9 %all-to-all-start.5 = ((f32[8,1,864]{2,1,0:T(1,128)}), f32[8,1,864]{2,1,0:T(1,128)S(1)}, u32[]{:S(2)}, u32[]{:S(2)}) async-start(f32[8,1,864]{2,1,0:T(1,128)} %reshape_reshape.16), calls=%async_computation.5 | async-start | bytes 57344 | tf_op jit(solution)/shard_map/all_to_all | solution.py:96
  163.5 10.1 %all-to-all-start.6 = ((f32[8,1,864]{2,1,0:T(1,128)}), f32[8,1,864]{2,1,0:T(1,128)S(1)}, u32[]{:S(2)}, u32[]{:S(2)}) async-start(f32[8,1,864]{2,1,0:T(1,128)} %broadcast_in_dim.336), calls=%async_computation.6 | async-start | bytes 57344 | tf_op jit(solution)/shard_map/all_to_all | solution.py:102
  174.4 4.2 %copy-start.56 = (s32[1024]{0:T(1024)S(1)}, s32[1024]{0:T(1024)}, u32[]{:S(2)}) copy-start(s32[1024]{0:T(1024)} %get-tuple-element.774) | copy-start | bytes 12292
  174.4 12.4 %all-to-all-start.7 = ((f32[8,54,128]{2,1,0:T(8,128)}), f32[8,54,128]{2,1,0:T(8,128)S(1)}, u32[]{:S(2)}, u32[]{:S(2)}) async-start(f32[8,54,128]{2,1,0:T(8,128)} %broadcast_in_dim.338), calls=%async_computation.7 | async-start | bytes 458752 | tf_op jit(solution)/shard_map/all_to_all | solution.py:102
  186.9 24.2 %all-to-all-start.2 = ((bf16[64,2,1024]{2,1,0:T(2,128)(2,1)}), bf16[64,2,1024]{2,1,0:T(2,128)(2,1)S(1)}, u32[]{:S(2)}, u32[]{:S(2)}) async-start(bf16[64,2,1024]{2,1,0:T(2,128)(2,1)} %reshape.1770), calls=%async_computation.2 | async-start | bytes 524288 | tf_op jit(solution)/shard_map/all_to_all | solution.py:206
  212.0 16.6 %all-to-all-start.8 = ((f32[4,432,128]{2,1,0:T(8,128)}), f32[4,432,128]{2,1,0:T(8,128)S(1)}, u32[]{:S(2)}, u32[]{:S(2)}) async-start(f32[4,432,128]{2,1,0:T(8,128)} %broadcast_in_dim.340), calls=%async_computation.8 | async-start | bytes 1769472 | tf_op jit(solution)/shard_map/all_to_all | solution.py:102
  (10 other events, 11.0 us)

commit v4 on v3

--- a/solution.py
+++ b/solution.py
@@ -88,18 +88,21 @@
 
 def reduce_everywhere(value, sizes, held=None):
     flat = value.reshape(-1)
+    lengths = []
     for stage, axis in enumerate(REDUCE_ORDER):
         if stage == 1 and held is not None:
             flat, held = lax.optimization_barrier((flat, held))
         count = sizes[axis]
-        lanes = 128 if flat.shape[0] % (count * 128) == 0 else flat.shape[0] // count
-        parts = lax.all_to_all(flat.reshape(count, -1, lanes), axis, 0, 0, tiled=True)
+        lengths.append(flat.shape[0])
+        tile = count * 8 * 128
+        if flat.shape[0] % tile:
+            flat = jnp.pad(flat, (0, tile * (-(-flat.shape[0] // tile)) - flat.shape[0]))
+        parts = lax.all_to_all(flat.reshape(count, -1, 128), axis, 0, 0, tiled=True)
         flat = jnp.sum(parts, 0).reshape(-1)
-    for axis in reversed(REDUCE_ORDER):
+    for axis, length in zip(reversed(REDUCE_ORDER), reversed(lengths)):
         count = sizes[axis]
-        lanes = 128 if flat.shape[0] % 128 == 0 else flat.shape[0]
-        spread = jnp.broadcast_to(flat.reshape(1, -1, lanes), (count, flat.shape[0] // lanes, lanes))
-        flat = lax.all_to_all(spread, axis, 0, 0, tiled=True).reshape(-1)
+        spread = jnp.broadcast_to(flat.reshape(1, -1, 128), (count, flat.shape[0] // 128, 128))
+        flat = lax.all_to_all(spread, axis, 0, 0, tiled=True).reshape(-1)[:length]
     return flat.reshape(value.shape), held
 
 

time: 238 us -> 238 us (level)
  no operation moved by 1% of the time
where the time goes in v4:
time: 238 us; the launch traced here: 237 us
  starting transfers between devices  65 us (27%)
  between operations  51.2 us (22%)
  waiting for transfers between devices  49.9 us (21%)
  local copies, waits for them, and re-layouts  29.2 us (12%)
  matrix products  21.1 us (9%)
  other arithmetic  14 us (6%)
  blocking collectives  6.3 us (3%)
    all_to_all x4, starting transfers between devices, reduce_everywhere(): parts = lax.all_to_all(flat.reshape(count, -1, 128), axis, 0, 0, tiled=True)  24.6 us
    all_to_all x3, waiting for transfers between devices, reduce_everywhere(): flat = lax.all_to_all(spread, axis, 0, 0, tiled=True).reshape(-1)[:length]  18.3 us
    all_to_all x4, waiting for transfers between devices, reduce_everywhere(): parts = lax.all_to_all(flat.reshape(count, -1, 128), axis, 0, 0, tiled=True)  16.6 us
    all_to_all x1, starting transfers between devices, local(): lax.all_to_all(ret, SPACE_AXES, 0, 0, tiled=True).reshape(-1, 2 * channels)  12.3 us
    all_to_all x1, waiting for transfers between devices, local(): lax.all_to_all(ret, SPACE_AXES, 0, 0, tiled=True).reshape(-1, 2 * channels)  11.9 us
    all_to_all x1, starting transfers between devices, local(): recv = lax.all_to_all(send, SPACE_AXES, 0, 0, tiled=True)  11.6 us
    all_to_all x3, starting transfers between devices, reduce_everywhere(): flat = lax.all_to_all(spread, axis, 0, 0, tiled=True).reshape(-1)[:length]  10.9 us
    dot_general x27, matrix products, local(): lax.dot_general(view_g, tap_weight, (((1,), (1,)), ((), ())), preferred_e...  7.99 us
  transfers between devices with their start and end apart: 11, of which 8 were waited for; matrix products, arithmetic and copies ran while one was open for 12% of the time, Pallas kernels for 0%

profile of v4, /device:TPU:1, one launch (start us, length us, event | category | flops | bytes accessed | tf_op | source)
XLA Modules:
  0.0 236.6 jit_solution(7387355947789336666)
XLA Ops:
  0.6 0.7 fusion.42
  1.3 0.6 reduce-window.6
  2.2 0.8 fusion.41
  3.0 0.7 compare_select_fusion.1
  3.6 1.9 scatter_custom_fusion
  5.7 1.6 scatter_custom_fusion.1
  7.5 0.6 broadcast.1056
  8.0 0.8 reduce.3
  8.9 0.8 reshape.1787
  9.7 11.6 %all-to-all-start = ((bf16[64,2,1152]{2,1,0:T(2,128)(2,1)}), bf16[64,2,1152]{2,1,0:T(2,128)(2,1)S(1)}, u32[]{:S(2)}, u32[]{:S(2)}) async-start(bf16[64,2,1152]{2,1,0:T(2,128)(2,1)} %reshape.1787), calls=%async_computation | async-start | bytes 589824 | tf_op jit(solution)/shard_map/all_to_all | solution.py:151
  21.3 0.7 fusion.233
  34.3 0.7 fusion.234
  71.6 2.4 scatter_custom_fusion.2
  74.5 0.6 pad_clamp_fusion
  75.1 3.5 %collective-permute-start = (bf16[1,8,8,256]{3,2,1,0:T(8,128)(2,1)S(1)}, bf16[1,8,8,256]{3,2,1,0:T(8,128)(2,1)S(1)}, u32[]{:S(2)}, u32[]{:S(2)}) collective-permute-start(bf16[1,8,8,256]{3,2,1,0:T(8,128)(2,1)S(1)} %pad_maximum_fusion.3), channel_id=1, source_target_pairs={{0,8},{8,16},{16,24},{24,32},{32,40},{40,48},{48,56},{56,64},{64,7... | collective-permute-start | bytes 98312 | tf_op jit(solution)/shard_map/ppermute | solution.py:172
  78.9 0.3 maximum_maximum_fusion.5
  79.3 0.8 fusion.229
  80.1 0.7 fusion.228
  80.8 0.6 constant_dynamic-slice_fusion.8
  81.5 0.6 constant_dynamic-slice_fusion.13
  82.2 2.1 collective-permute-start.1
  84.4 3.1 %collective-permute-done.1 = bf16[1,8,8,256]{3,2,1,0:T(8,128)(2,1)S(1)} collective-permute-done((bf16[1,8,8,256]{3,2,1,0:T(8,128)(2,1)S(1)}, bf16[1,8,8,256]{3,2,1,0:T(8,128)(2,1)S(1)}, u32[]{:S(2)}, u32[]{:S(2)}) %collective-permute-start.1) | collective-permute-done | bytes 32800 | tf_op jit(solution)/shard_map/ppermute | solution.py:173
  88.3 0.3 maximum_maximum_fusion
  88.6 0.6 pad_slice_fusion.23
  89.3 0.6 pad_slice_fusion.31
  96.7 1.2 copy-done.1
  98.0 3.7 %all-to-all-start.1 = ((f32[2,1728,128]{2,1,0:T(8,128)}), f32[2,1728,128]{2,1,0:T(8,128)S(1)}, u32[]{:S(2)}, u32[]{:S(2)}) async-start(f32[2,1728,128]{2,1,0:T(8,128)} %bitcast.605), calls=%async_computation.1 | async-start | bytes 3538944 | tf_op jit(solution)/shard_map/all_to_all | solution.py:100
  102.1 0.3 maximum_maximum_fusion.1
  102.4 1.6 all-to-all-done.1
  104.0 1.1 reduce_sum.49
  105.1 1.0 fusion.225
  106.1 1.5 fusion.224
  107.6 1.0 fusion.223
  108.6 1.5 fusion.222
  110.7 5.1 %all-to-all-start.3 = ((f32[4,432,128]{2,1,0:T(8,128)}), f32[4,432,128]{2,1,0:T(8,128)S(1)}, u32[]{:S(2)}, u32[]{:S(2)}) async-start(f32[4,432,128]{2,1,0:T(8,128)} %bitcast.244), calls=%async_computation.3 | async-start | bytes 1769472 | tf_op jit(solution)/shard_map/all_to_all | solution.py:100
  115.8 1.1 convolution_add_fusion.25
  116.9 1.1 convolution_add_fusion.24
  118.1 1.1 convolution_add_fusion.23
  129.4 0.7 pad.15
  130.1 5.7 %all-to-all-start.4 = ((f32[8,56,128]{2,1,0:T(8,128)}), f32[8,56,128]{2,1,0:T(8,128)S(1)}, u32[]{:S(2)}, u32[]{:S(2)}) async-start(f32[8,56,128]{2,1,0:T(8,128)} %bitcast.246), calls=%async_computation.4 | async-start | bytes 458752 | tf_op jit(solution)/shard_map/all_to_all | solution.py:100
  135.8 1.1 convolution_add_fusion.30
  137.2 8.4 %all-to-all-done.4 = f32[8,56,128]{2,1,0:T(8,128)S(1)} async-done(((f32[8,56,128]{2,1,0:T(8,128)}), f32[8,56,128]{2,1,0:T(8,128)S(1)}, u32[]{:S(2)}, u32[]{:S(2)}) %all-to-all-start.4) | async-done | bytes 229408 | tf_op jit(solution)/shard_map/all_to_all | solution.py:100
  145.6 0.6 pad_bitcast_fusion
  146.2 10.1 %all-to-all-start.5 = ((f32[8,8,128]{2,1,0:T(8,128)}), f32[8,8,128]{2,1,0:T(8,128)S(1)}, u32[]{:S(2)}, u32[]{:S(2)}) async-start(f32[8,8,128]{2,1,0:T(8,128)} %pad_bitcast_fusion), calls=%async_computation.5 | async-start | bytes 65536 | tf_op jit(solution)/shard_map/all_to_all | solution.py:100
  156.5 6.6 %all-to-all-done.5 = f32[8,8,128]{2,1,0:T(8,128)S(1)} async-done(((f32[8,8,128]{2,1,0:T(8,128)}), f32[8,8,128]{2,1,0:T(8,128)S(1)}, u32[]{:S(2)}, u32[]{:S(2)}) %all-to-all-start.5) | async-done | bytes 32800 | tf_op jit(solution)/shard_map/all_to_all | solution.py:100
  163.1 0.6 broadcast_in_dim.334
  163.8 3.6 %all-to-all-start.6 = ((f32[8,8,128]{2,1,0:T(8,128)}), f32[8,8,128]{2,1,0:T(8,128)S(1)}, u32[]{:S(2)}, u32[]{:S(2)}) async-start(f32[8,8,128]{2,1,0:T(8,128)} %broadcast_in_dim.334), calls=%async_computation.6 | async-start | bytes 65536 | tf_op jit(solution)/shard_map/all_to_all | solution.py:105
  167.6 6.3 %all-to-all-done.6 = f32[8,8,128]{2,1,0:T(8,128)S(1)} async-done(((f32[8,8,128]{2,1,0:T(8,128)}), f32[8,8,128]{2,1,0:T(8,128)S(1)}, u32[]{:S(2)}, u32[]{:S(2)}) %all-to-all-start.6) | async-done | bytes 32800 | tf_op jit(solution)/shard_map/all_to_all | solution.py:105
  173.9 0.7 broadcast_in_dim.336
  174.6 3.5 %all-to-all-start.7 = ((f32[8,56,128]{2,1,0:T(8,128)}), f32[8,56,128]{2,1,0:T(8,128)S(1)}, u32[]{:S(2)}, u32[]{:S(2)}) async-start(f32[8,56,128]{2,1,0:T(8,128)} %broadcast_in_dim.336), calls=%async_computation.7 | async-start | bytes 458752 | tf_op jit(solution)/shard_map/all_to_all | solution.py:105
  178.8 2.0 gather_fusion
  180.9 2.2 reduce.4
  183.1 0.9 reshape.1789
  183.9 3.1 %all-to-all-done.7 = f32[8,56,128]{2,1,0:T(8,128)S(1)} async-done(((f32[8,56,128]{2,1,0:T(8,128)}), f32[8,56,128]{2,1,0:T(8,128)S(1)}, u32[]{:S(2)}, u32[]{:S(2)}) %all-to-all-start.7) | async-done | bytes 229408 | tf_op jit(solution)/shard_map/all_to_all | solution.py:105
  187.0 12.3 %all-to-all-start.2 = ((bf16[64,2,1024]{2,1,0:T(2,128)(2,1)}), bf16[64,2,1024]{2,1,0:T(2,128)(2,1)S(1)}, u32[]{:S(2)}, u32[]{:S(2)}) async-start(bf16[64,2,1024]{2,1,0:T(2,128)(2,1)} %reshape.1789), calls=%async_computation.2 | async-start | bytes 524288 | tf_op jit(solution)/shard_map/all_to_all | solution.py:209
  199.3 11.9 %all-to-all-done.2 = bf16[64,2,1024]{2,1,0:T(2,128)(2,1)S(1)} async-done(((bf16[64,2,1024]{2,1,0:T(2,128)(2,1)}), bf16[64,2,1024]{2,1,0:T(2,128)(2,1)S(1)}, u32[]{:S(2)}, u32[]{:S(2)}) %all-to-all-start.2) | async-done | bytes 262176 | tf_op jit(solution)/shard_map/all_to_all | solution.py:209
  211.3 1.0 broadcast_in_dim.337
  212.2 3.8 %all-to-all-start.8 = ((f32[4,432,128]{2,1,0:T(8,128)}), f32[4,432,128]{2,1,0:T(8,128)S(1)}, u32[]{:S(2)}, u32[]{:S(2)}) async-start(f32[4,432,128]{2,1,0:T(8,128)} %broadcast_in_dim.337), calls=%async_computation.8 | async-start | bytes 1769472 | tf_op jit(solution)/shard_map/all_to_all | solution.py:105
  216.3 1.5 reduce.1
  217.9 1.3 gather_fusion.1
  219.2 0.7 slice_bitcast_fusion
  219.9 8.9 %all-to-all-done.8 = f32[4,432,128]{2,1,0:T(8,128)S(1)} async-done(((f32[4,432,128]{2,1,0:T(8,128)}), f32[4,432,128]{2,1,0:T(8,128)S(1)}, u32[]{:S(2)}, u32[]{:S(2)}) %all-to-all-start.8) | async-done | bytes 884768 | tf_op jit(solution)/shard_map/all_to_all | solution.py:105
  228.9 6.3 %all_to_all.62 = f32[2,1728,128]{2,1,0:T(8,128)S(1)} all-to-all(f32[2,1728,128]{2,1,0:T(8,128)S(1)} %broadcast_in_dim.339), channel_id=1, replica_groups=mesh['sx'=4,'sy'=8,'sc'=2,'rep'=8] {'sc'}, dimensions={0} | all-to-all | bytes 3538944 | tf_op jit(solution)/shard_map/all_to_all | solution.py:105
  235.2 1.4 broadcast_multiply_fusion
  (305 shorter events, 21.4 us)
Async XLA Ops:
  2.2 19.1 %copy-start.51 = (s32[1,1,26]{2,1,0:T(1,128)S(1)}, s32[1,1,26]{2,1,0:T(1,128)}, u32[]{:S(2)}) copy-start(s32[1,1,26]{2,1,0:T(1,128)} %param.10) | copy-start | bytes 316
  9.7 61.2 %all-to-all-start = ((bf16[64,2,1152]{2,1,0:T(2,128)(2,1)}), bf16[64,2,1152]{2,1,0:T(2,128)(2,1)S(1)}, u32[]{:S(2)}, u32[]{:S(2)}) async-start(bf16[64,2,1152]{2,1,0:T(2,128)(2,1)} %reshape.1787), calls=%async_computation | async-start | bytes 589824 | tf_op jit(solution)/shard_map/all_to_all | solution.py:151
  75.1 9.2 %collective-permute-start = (bf16[1,8,8,256]{3,2,1,0:T(8,128)(2,1)S(1)}, bf16[1,8,8,256]{3,2,1,0:T(8,128)(2,1)S(1)}, u32[]{:S(2)}, u32[]{:S(2)}) collective-permute-start(bf16[1,8,8,256]{3,2,1,0:T(8,128)(2,1)S(1)} %pad_maximum_fusion.3), channel_id=1, source_target_pairs={{0,8},{8,16},{16,24},{24,32},{32,40},{40,48},{48,56},{56,64},{64,7... | collective-permute-start | bytes 98312 | tf_op jit(solution)/shard_map/ppermute | solution.py:172
  82.2 5.2 %collective-permute-start.1 = (bf16[1,8,8,256]{3,2,1,0:T(8,128)(2,1)S(1)}, bf16[1,8,8,256]{3,2,1,0:T(8,128)(2,1)S(1)}, u32[]{:S(2)}, u32[]{:S(2)}) collective-permute-start(bf16[1,8,8,256]{3,2,1,0:T(8,128)(2,1)S(1)} %pad_maximum_fusion.4), channel_id=1, source_target_pairs={{8,0},{16,8},{24,16},{32,24},{40,32},{48,40},{56,48},{64,56},{72,6... | collective-permute-start | bytes 98312 | tf_op jit(solution)/shard_map/ppermute | solution.py:173
  90.1 2.1 copy-start.50
  90.1 2.4 %copy-start.49 = (bf16[1,8,8,8,128]{4,3,2,1,0:T(8,128)(2,1)S(1)}, bf16[1,8,8,8,128]{4,3,2,1,0:T(8,128)(2,1)}, u32[]{:S(2)}) copy-start(bf16[1,8,8,8,128]{4,3,2,1,0:T(8,128)(2,1)} %get-tuple-element.661) | copy-start | bytes 393220
  90.1 2.6 %copy-start.48 = (bf16[1,8,8,8,128]{4,3,2,1,0:T(8,128)(2,1)S(1)}, bf16[1,8,8,8,128]{4,3,2,1,0:T(8,128)(2,1)}, u32[]{:S(2)}) copy-start(bf16[1,8,8,8,128]{4,3,2,1,0:T(8,128)(2,1)} %get-tuple-element.660) | copy-start | bytes 393220
  92.7 1.1 copy-start.47
  93.0 1.1 copy-start.46
  96.7 1.2 copy-start.1
  97.9 3.8 %copy-start.62 = (bf16[2,1,1,128]{3,2,1,0:T(2,128)(2,1)S(1)}, bf16[2,1,1,128]{3,2,1,0:T(2,128)(2,1)}, u32[]{:S(2)}) copy-start(bf16[2,1,1,128]{3,2,1,0:T(2,128)(2,1)} %get-tuple-element.708) | copy-start | bytes 1540
  97.9 3.8 %copy-start.61 = (bf16[2,1,1,128]{3,2,1,0:T(2,128)(2,1)S(1)}, bf16[2,1,1,128]{3,2,1,0:T(2,128)(2,1)}, u32[]{:S(2)}) copy-start(bf16[2,1,1,128]{3,2,1,0:T(2,128)(2,1)} %get-tuple-element.707) | copy-start | bytes 1540
  97.9 3.9 %copy-start.59 = (bf16[2,1,1,128]{3,2,1,0:T(2,128)(2,1)S(1)}, bf16[2,1,1,128]{3,2,1,0:T(2,128)(2,1)}, u32[]{:S(2)}) copy-start(bf16[2,1,1,128]{3,2,1,0:T(2,128)(2,1)} %get-tuple-element.706) | copy-start | bytes 1540
  97.9 4.0 %copy-start.57 = (bf16[2,1,1,128]{3,2,1,0:T(2,128)(2,1)S(1)}, bf16[2,1,1,128]{3,2,1,0:T(2,128)(2,1)}, u32[]{:S(2)}) copy-start(bf16[2,1,1,128]{3,2,1,0:T(2,128)(2,1)} %get-tuple-element.705) | copy-start | bytes 1540
  97.9 4.0 %copy-start.60 = (bf16[2,1,1,128]{3,2,1,0:T(2,128)(2,1)S(1)}, bf16[2,1,1,128]{3,2,1,0:T(2,128)(2,1)}, u32[]{:S(2)}) copy-start(bf16[2,1,1,128]{3,2,1,0:T(2,128)(2,1)} %get-tuple-element.700) | copy-start | bytes 1540
  97.9 4.0 %copy-start.58 = (bf16[2,1,1,128]{3,2,1,0:T(2,128)(2,1)S(1)}, bf16[2,1,1,128]{3,2,1,0:T(2,128)(2,1)}, u32[]{:S(2)}) copy-start(bf16[2,1,1,128]{3,2,1,0:T(2,128)(2,1)} %get-tuple-element.699) | copy-start | bytes 1540
  97.9 4.1 %copy-start.52 = (bf16[1,8,1,1,128]{4,3,2,1,0:T(2,128)(2,1)S(1)}, bf16[1,8,1,1,128]{4,3,2,1,0:T(2,128)(2,1)}, u32[]{:S(2)}) copy-start(bf16[1,8,1,1,128]{4,3,2,1,0:T(2,128)(2,1)} %get-tuple-element.765) | copy-start | bytes 6148
  98.0 4.1 %copy-start.53 = (bf16[1,8,1,1,128]{4,3,2,1,0:T(2,128)(2,1)S(1)}, bf16[1,8,1,1,128]{4,3,2,1,0:T(2,128)(2,1)}, u32[]{:S(2)}) copy-start(bf16[1,8,1,1,128]{4,3,2,1,0:T(2,128)(2,1)} %get-tuple-element.766) | copy-start | bytes 6148
  98.0 4.1 %copy-start.54 = (bf16[1,8,1,1,128]{4,3,2,1,0:T(2,128)(2,1)S(1)}, bf16[1,8,1,1,128]{4,3,2,1,0:T(2,128)(2,1)}, u32[]{:S(2)}) copy-start(bf16[1,8,1,1,128]{4,3,2,1,0:T(2,128)(2,1)} %get-tuple-element.767) | copy-start | bytes 6148
  98.0 4.1 %copy-start.55 = (bf16[1,8,1,1,128]{4,3,2,1,0:T(2,128)(2,1)S(1)}, bf16[1,8,1,1,128]{4,3,2,1,0:T(2,128)(2,1)}, u32[]{:S(2)}) copy-start(bf16[1,8,1,1,128]{4,3,2,1,0:T(2,128)(2,1)} %get-tuple-element.768) | copy-start | bytes 6148
  98.0 6.0 %all-to-all-start.1 = ((f32[2,1728,128]{2,1,0:T(8,128)}), f32[2,1728,128]{2,1,0:T(8,128)S(1)}, u32[]{:S(2)}, u32[]{:S(2)}) async-start(f32[2,1728,128]{2,1,0:T(8,128)} %bitcast.605), calls=%async_computation.1 | async-start | bytes 3538944 | tf_op jit(solution)/shard_map/all_to_all | solution.py:100
  108.6 1.7 copy-start
  110.7 18.7 %all-to-all-start.3 = ((f32[4,432,128]{2,1,0:T(8,128)}), f32[4,432,128]{2,1,0:T(8,128)S(1)}, u32[]{:S(2)}, u32[]{:S(2)}) async-start(f32[4,432,128]{2,1,0:T(8,128)} %bitcast.244), calls=%async_computation.3 | async-start | bytes 1769472 | tf_op jit(solution)/shard_map/all_to_all | solution.py:100
  115.8 3.5 %copy-start.45 = (bf16[1,8,8,8,128]{4,3,2,1,0:T(8,128)(2,1)S(1)}, bf16[1,8,8,8,128]{4,3,2,1,0:T(8,128)(2,1)}, u32[]{:S(2)}) copy-start(bf16[1,8,8,8,128]{4,3,2,1,0:T(8,128)(2,1)} %get-tuple-element.634) | copy-start | bytes 393220
  115.8 3.7 %copy-start.44 = (bf16[1,8,8,8,128]{4,3,2,1,0:T(8,128)(2,1)S(1)}, bf16[1,8,8,8,128]{4,3,2,1,0:T(8,128)(2,1)}, u32[]{:S(2)}) copy-start(bf16[1,8,8,8,128]{4,3,2,1,0:T(8,128)(2,1)} %get-tuple-element.633) | copy-start | bytes 393220
  115.8 3.9 %copy-start.43 = (bf16[1,8,8,8,128]{4,3,2,1,0:T(8,128)(2,1)S(1)}, bf16[1,8,8,8,128]{4,3,2,1,0:T(8,128)(2,1)}, u32[]{:S(2)}) copy-start(bf16[1,8,8,8,128]{4,3,2,1,0:T(8,128)(2,1)} %get-tuple-element.632) | copy-start | bytes 393220
  116.9 3.0 %copy-start.42 = (bf16[1,8,8,8,128]{4,3,2,1,0:T(8,128)(2,1)S(1)}, bf16[1,8,8,8,128]{4,3,2,1,0:T(8,128)(2,1)}, u32[]{:S(2)}) copy-start(bf16[1,8,8,8,128]{4,3,2,1,0:T(8,128)(2,1)} %get-tuple-element.631) | copy-start | bytes 393220
  118.1 2.0 copy-start.41
  119.2 1.1 copy-start.40
  119.4 1.1 copy-start.39
  119.7 1.1 copy-start.38
  119.9 1.1 copy-start.37
  120.3 1.1 copy-start.35
  120.8 1.1 copy-start.33
  121.0 1.1 copy-start.32
  122.9 1.1 copy-start.25
  123.2 1.1 copy-start.23
  123.4 1.2 copy-start.21
  123.6 1.2 copy-start.20
  123.8 1.2 copy-start.19
  124.0 1.3 copy-start.18
  124.3 1.3 copy-start.17
  124.5 1.3 copy-start.16
  124.8 1.3 copy-start.15
  125.1 1.3 copy-start.14
  125.3 1.3 copy-start.13
  125.6 1.3 copy-start.12
  125.8 1.3 copy-start.11
  126.1 1.3 copy-start.10
  126.3 1.3 copy-start.9
  126.6 1.3 copy-start.8
  126.8 1.3 copy-start.7
  127.1 1.3 copy-start.6
  127.3 1.3 copy-start.5
  127.6 1.2 copy-start.4
  127.9 1.2 copy-start.3
  129.1 7.8 %copy-start.2 = (bf16[1,8,8,8,128]{4,3,2,1,0:T(8,128)(2,1)S(1)}, bf16[1,8,8,8,128]{4,3,2,1,0:T(8,128)(2,1)}, u32[]{:S(2)}) copy-start(bf16[1,8,8,8,128]{4,3,2,1,0:T(8,128)(2,1)} %get-tuple-element.588) | copy-start | bytes 393220
  130.1 15.4 %all-to-all-start.4 = ((f32[8,56,128]{2,1,0:T(8,128)}), f32[8,56,128]{2,1,0:T(8,128)S(1)}, u32[]{:S(2)}, u32[]{:S(2)}) async-start(f32[8,56,128]{2,1,0:T(8,128)} %bitcast.246), calls=%async_computation.4 | async-start | bytes 458752 | tf_op jit(solution)/shard_map/all_to_all | solution.py:100
  146.2 16.9 %all-to-all-start.5 = ((f32[8,8,128]{2,1,0:T(8,128)}), f32[8,8,128]{2,1,0:T(8,128)S(1)}, u32[]{:S(2)}, u32[]{:S(2)}) async-start(f32[8,8,128]{2,1,0:T(8,128)} %pad_bitcast_fusion), calls=%async_computation.5 | async-start | bytes 65536 | tf_op jit(solution)/shard_map/all_to_all | solution.py:100
  163.8 10.1 %all-to-all-start.6 = ((f32[8,8,128]{2,1,0:T(8,128)}), f32[8,8,128]{2,1,0:T(8,128)S(1)}, u32[]{:S(2)}, u32[]{:S(2)}) async-start(f32[8,8,128]{2,1,0:T(8,128)} %broadcast_in_dim.334), calls=%async_computation.6 | async-start | bytes 65536 | tf_op jit(solution)/shard_map/all_to_all | solution.py:105
  174.5 4.2 %copy-start.56 = (s32[1024]{0:T(1024)S(1)}, s32[1024]{0:T(1024)}, u32[]{:S(2)}) copy-start(s32[1024]{0:T(1024)} %get-tuple-element.774) | copy-start | bytes 12292
  174.6 12.4 %all-to-all-start.7 = ((f32[8,56,128]{2,1,0:T(8,128)}), f32[8,56,128]{2,1,0:T(8,128)S(1)}, u32[]{:S(2)}, u32[]{:S(2)}) async-start(f32[8,56,128]{2,1,0:T(8,128)} %broadcast_in_dim.336), calls=%async_computation.7 | async-start | bytes 458752 | tf_op jit(solution)/shard_map/all_to_all | solution.py:105
  187.0 24.3 %all-to-all-start.2 = ((bf16[64,2,1024]{2,1,0:T(2,128)(2,1)}), bf16[64,2,1024]{2,1,0:T(2,128)(2,1)S(1)}, u32[]{:S(2)}, u32[]{:S(2)}) async-start(bf16[64,2,1024]{2,1,0:T(2,128)(2,1)} %reshape.1789), calls=%async_computation.2 | async-start | bytes 524288 | tf_op jit(solution)/shard_map/all_to_all | solution.py:209
  212.2 16.6 %all-to-all-start.8 = ((f32[4,432,128]{2,1,0:T(8,128)}), f32[4,432,128]{2,1,0:T(8,128)S(1)}, u32[]{:S(2)}, u32[]{:S(2)}) async-start(f32[4,432,128]{2,1,0:T(8,128)} %broadcast_in_dim.337), calls=%async_computation.8 | async-start | bytes 1769472 | tf_op jit(solution)/shard_map/all_to_all | solution.py:105
  (10 other events, 11.0 us)

commit v5 on v2

--- a/solution.py
+++ b/solution.py
@@ -86,19 +86,39 @@
     ].reshape(-1, channels)
 
 
-def reduce_everywhere(value, sizes):
+def reduce_everywhere(value, sizes, held, make_carry):
     flat = value.reshape(-1)
-    for axis in REDUCE_ORDER:
+    for stage, axis in enumerate(REDUCE_ORDER):
+        if stage == 1:
+            flat, held = lax.optimization_barrier((flat, held))
         count = sizes[axis]
         lanes = 128 if flat.shape[0] % (count * 128) == 0 else flat.shape[0] // count
         parts = lax.all_to_all(flat.reshape(count, -1, lanes), axis, 0, 0, tiled=True)
         flat = jnp.sum(parts, 0).reshape(-1)
+    carry, carry_axes = None, []
     for axis in reversed(REDUCE_ORDER):
         count = sizes[axis]
+        if axis == "sy":
+            carry = make_carry(held)
+            carry_axes = ["sx", "sy", "sc"]
         lanes = 128 if flat.shape[0] % 128 == 0 else flat.shape[0]
         spread = jnp.broadcast_to(flat.reshape(1, -1, lanes), (count, flat.shape[0] // lanes, lanes))
-        flat = lax.all_to_all(spread, axis, 0, 0, tiled=True).reshape(-1)
-    return flat.reshape(value.shape)
+        if carry is None:
+            flat = lax.all_to_all(spread, axis, 0, 0, tiled=True).reshape(-1)
+            continue
+        where = carry_axes.index(axis)
+        order = [where] + [i for i in range(len(carry_axes)) if i != where] + [3]
+        carry = jnp.transpose(carry, order)
+        carry_axes = [carry_axes[i] for i in order[:3]]
+        moved_shape = carry.shape
+        rows_here = spread.shape[1]
+        sent = jnp.concatenate([spread, carry.reshape(count, -1, 128)], 1)
+        got = lax.all_to_all(sent, axis, 0, 0, tiled=True)
+        flat = got[:, :rows_here].reshape(-1)
+        carry = got[:, rows_here:].reshape(moved_shape)
+    order = [carry_axes.index(name) for name in ("sx", "sy", "sc")] + [3]
+    home = jnp.transpose(carry, order)
+    return flat.reshape(value.shape), held, home
 
 
 def make_local(sizes):
@@ -180,29 +200,36 @@
                 )
             )
         grad_part = jnp.stack(tap_grads, 0)
-        convolved = jnp.zeros((voxels, channels), jnp.float32)
-        backward = jnp.zeros((voxels, channels), jnp.float32)
-        for tap_index, (shift_x, shift_y, shift_z) in enumerate(ALL_TAPS):
-            view_h = tap_view(padded_h, shift_x, shift_y, shift_z, 1)
-            view_g = tap_view(padded_g, shift_x, shift_y, shift_z, -1)
-            tap_weight = weights[tap_index]
-            convolved = convolved + jnp.dot(view_h, tap_weight, preferred_element_type=jnp.float32)
-            backward = backward + lax.dot_general(
-                view_g, tap_weight, (((1,), (1,)), ((), ())), preferred_element_type=jnp.float32
+        def make_carry(held):
+            padded_h, padded_g, dense_x, dense_g = held
+            convolved = jnp.zeros((voxels, channels), jnp.float32)
+            backward = jnp.zeros((voxels, channels), jnp.float32)
+            for tap_index, (shift_x, shift_y, shift_z) in enumerate(ALL_TAPS):
+                view_h = tap_view(padded_h, shift_x, shift_y, shift_z, 1)
+                view_g = tap_view(padded_g, shift_x, shift_y, shift_z, -1)
+                tap_weight = weights[tap_index]
+                convolved = convolved + jnp.dot(view_h, tap_weight, preferred_element_type=jnp.float32)
+                backward = backward + lax.dot_general(
+                    view_g, tap_weight, (((1,), (1,)), ((), ())), preferred_element_type=jnp.float32
+                )
+            out_x = (dense_x.astype(jnp.float32) + convolved).astype(data_type)
+            out_dx = (dense_g.astype(jnp.float32) + jnp.where(dense_x > 0, backward, 0.0)).astype(
+                data_type
             )
-        out_x = (dense_x.astype(jnp.float32) + convolved).astype(data_type)
-        out_dx = (dense_g.astype(jnp.float32) + jnp.where(dense_x > 0, backward, 0.0)).astype(
-            data_type
-        )
-        out_both = jnp.concatenate(
-            [jnp.concatenate([out_x, out_dx], -1), jnp.zeros((1, 2 * channels), data_type)], 0
-        )
-        ret = out_both[arrived].reshape(peer_count, capacity * 2 * channels)
-        home = lax.all_to_all(ret, SPACE_AXES, 0, 0, tiled=True).reshape(-1, 2 * channels)
+
+            out_both = jnp.concatenate(
+                [jnp.concatenate([out_x, out_dx], -1), jnp.zeros((1, 2 * channels), data_type)], 0
+            )
+            ret = out_both[arrived].astype(jnp.float32)
+            return ret.reshape(sizes["sx"], sizes["sy"], sizes["sc"], capacity * 2 * channels)
+
+        summed, _, home = reduce_everywhere(
+            grad_part, sizes, (padded_h, padded_g, dense_x, dense_g), make_carry
+        )
+        home = home.reshape(-1, 2 * channels).astype(data_type)
         final = home[bucket]
         final_x = final[:, :channels]
         final_dx = final[:, channels:]
-        summed = reduce_everywhere(grad_part, sizes)
         norm_scale = 1.0 / math.sqrt(peer_count * rep_count * owners.shape[0])
         weight_grad = (summed * norm_scale).reshape(27, channels, channels)
         return (final_x[None], final_dx[None], weight_grad)

time: 258 us -> 231 us (0.90)
  blocking collectives: 11.1 us -> 48.5 us
  waiting for transfers between devices: 54.1 us -> 24.4 us
  starting transfers between devices: 62.7 us -> 45.1 us
  matrix products: 35.1 us -> 20.2 us
  other arithmetic: 15.6 us -> 10.6 us
  local copies, waits for them, and re-layouts: 25.1 us -> 29.2 us
    all_to_all x2 -> x3, blocking collectives: 11.1 us -> 48.5 us  [reduce_everywhere(): got = lax.all_to_all(sent, axis, 0, 0, tiled=True)]
    all_to_all x3 -> x1, waiting for transfers between devices: 18.4 us -> 3.78 us  [reduce_everywhere(): flat = lax.all_to_all(spread, axis, 0, 0, tiled=True).reshape(-1)]
    all_to_all x1 -> x0, waiting for transfers between devices: 12 us -> none  [local(): lax.all_to_all(ret, SPACE_AXES, 0, 0, tiled=True).reshape(-1, 2 * channels)]
    all_to_all x1 -> x0, starting transfers between devices: 11.1 us -> none  [local(): lax.all_to_all(ret, SPACE_AXES, 0, 0, tiled=True).reshape(-1, 2 * channels)]
    dot_general x27, matrix products: 14.3 us -> 6.1 us  [local(): lax.dot_general(view_h, grads_flat, (((0,), (0,)), ((), ())), preferred_e...]
    all_to_all x3 -> x1, starting transfers between devices: 11 us -> 3.34 us  [reduce_everywhere(): flat = lax.all_to_all(spread, axis, 0, 0, tiled=True).reshape(-1)]
    dot_general x54, matrix products: 20.8 us -> 14.1 us  [the longest x27 7.98 us: make_carry(): lax.dot_general(view_g, tap_weight, (((1,), (1,)), ((), ())), preferred_e...]
    all_to_all x3 -> x4, waiting for transfers between devices: 23.7 us -> 17.6 us  [reduce_everywhere(): lax.all_to_all(flat.reshape(count, -1, lanes), axis, 0, 0, tiled=True)]
  transfers between devices with their start and end apart: 10 -> 8, of which waited for: 7 -> 5; matrix products, arithmetic and copies ran while one was open for 9% -> 10% of each run, Pallas kernels for 0% -> 0%
where the time goes in v5:
time: 231 us; the launch traced here: 229 us
  between operations  51 us (22%)
  blocking collectives  48.5 us (21%)
  starting transfers between devices  45.1 us (20%)
  local copies, waits for them, and re-layouts  29.2 us (13%)
  waiting for transfers between devices  24.4 us (11%)
  matrix products  20.2 us (9%)
  other arithmetic  10.6 us (5%)
    all_to_all x3, blocking collectives, reduce_everywhere(): got = lax.all_to_all(sent, axis, 0, 0, tiled=True)  48.5 us
    all_to_all x4, starting transfers between devices, reduce_everywhere(): lax.all_to_all(flat.reshape(count, -1, lanes), axis, 0, 0, tiled=True)  24.6 us
    all_to_all x4, waiting for transfers between devices, reduce_everywhere(): lax.all_to_all(flat.reshape(count, -1, lanes), axis, 0, 0, tiled=True)  17.6 us
    all_to_all x1, starting transfers between devices, local(): recv = lax.all_to_all(send, SPACE_AXES, 0, 0, tiled=True)  11.6 us
    dot_general x27, matrix products, make_carry(): lax.dot_general(view_g, tap_weight, (((1,), (1,)), ((), ())), preferred_e...  7.98 us
    slice x8, local copies, waits for them, and re-layouts, tap_view(): padded[:, start_x:start_x + 8, start_y:start_y + 8, start_z:start_z + 8, :]  6.94 us
    dot_general x27, matrix products, make_carry(): jnp.dot(view_h, tap_weight, preferred_element_type=jnp.float32)  6.12 us
    dot_general x27, matrix products, local(): lax.dot_general(view_h, grads_flat, (((0,), (0,)), ((), ())), preferred_e...  6.1 us
  transfers between devices with their start and end apart: 8, of which 5 were waited for; matrix products, arithmetic and copies ran while one was open for 10% of the time, Pallas kernels for 0%

profile of v5, /device:TPU:1, one launch (start us, length us, event | category | flops | bytes accessed | tf_op | source)
XLA Modules:
  0.0 229.1 jit_solution(4224795119176553506)
XLA Ops:
  0.6 0.7 fusion.42
  1.3 0.6 reduce-window.6
  2.2 0.8 fusion.41
  3.0 0.7 compare_select_fusion.1
  3.6 1.9 scatter_custom_fusion
  5.7 1.6 scatter_custom_fusion.1
  7.5 0.5 broadcast.1053
  8.0 0.8 reduce.4
  8.8 0.8 reshape.1795
  9.6 11.6 %all-to-all-start = ((bf16[64,2,1152]{2,1,0:T(2,128)(2,1)}), bf16[64,2,1152]{2,1,0:T(2,128)(2,1)S(1)}, u32[]{:S(2)}, u32[]{:S(2)}) async-start(bf16[64,2,1152]{2,1,0:T(2,128)(2,1)} %reshape.1795), calls=%async_computation | async-start | bytes 589824 | tf_op jit(solution)/shard_map/all_to_all | solution.py:166
  21.2 0.7 fusion.233
  34.3 0.7 fusion.234
  70.5 0.3 reshape.1796
  71.2 2.4 %scatter_custom_fusion.2 = bf16[513,256]{1,0:T(8,128)(2,1)S(1)} fusion(s32[512]{0:T(512)S(1)} %bitcast.700, bf16[512,256]{1,0:T(8,128)(2,1)S(1)} %reshape.1783, bf16[]{:T(256)} %constant.19.clone.1), kind=kCustom, calls=%fused_computation.146 | custom fusion | bytes 262658 | tf_op jit(solution)/shard_map/scatter | solution.py:174
  74.1 0.6 pad_clamp_fusion
  74.7 3.5 %collective-permute-start = (bf16[1,8,8,256]{3,2,1,0:T(8,128)(2,1)S(1)}, bf16[1,8,8,256]{3,2,1,0:T(8,128)(2,1)S(1)}, u32[]{:S(2)}, u32[]{:S(2)}) collective-permute-start(bf16[1,8,8,256]{3,2,1,0:T(8,128)(2,1)S(1)} %pad_maximum_fusion.6), channel_id=1, source_target_pairs={{0,8},{8,16},{16,24},{24,32},{32,40},{40,48},{48,56},{56,64},{64,7... | collective-permute-start | bytes 98312 | tf_op jit(solution)/shard_map/ppermute | solution.py:187
  78.6 0.3 maximum_maximum_fusion.5
  78.9 0.8 fusion.229
  79.7 0.7 fusion.228
  80.5 0.6 constant_dynamic-slice_fusion.8
  81.1 0.6 constant_dynamic-slice_fusion.13
  81.9 2.1 collective-permute-start.1
  84.0 3.1 %collective-permute-done.1 = bf16[1,8,8,256]{3,2,1,0:T(8,128)(2,1)S(1)} collective-permute-done((bf16[1,8,8,256]{3,2,1,0:T(8,128)(2,1)S(1)}, bf16[1,8,8,256]{3,2,1,0:T(8,128)(2,1)S(1)}, u32[]{:S(2)}, u32[]{:S(2)}) %collective-permute-start.1) | collective-permute-done | bytes 32800 | tf_op jit(solution)/shard_map/ppermute | solution.py:188
  87.5 0.2 maximum_maximum_fusion.2
  87.7 0.2 maximum_maximum_fusion.3
  88.0 0.3 maximum_maximum_fusion
  88.3 0.6 pad_slice_fusion.23
  88.9 0.6 pad_slice_fusion.31
  96.3 1.2 copy-done.1
  97.6 3.7 %all-to-all-start.1 = ((f32[2,1728,128]{2,1,0:T(8,128)}), f32[2,1728,128]{2,1,0:T(8,128)S(1)}, u32[]{:S(2)}, u32[]{:S(2)}) async-start(f32[2,1728,128]{2,1,0:T(8,128)} %bitcast.608), calls=%async_computation.1 | async-start | bytes 3538944 | tf_op jit(solution)/shard_map/all_to_all | solution.py:96
  101.7 0.3 maximum_maximum_fusion.1
  102.0 1.6 all-to-all-done.1
  103.6 1.1 reduce_sum.49
  104.7 1.0 fusion.225
  105.7 1.5 fusion.224
  107.2 1.0 fusion.223
  108.2 1.5 fusion.222
  110.3 5.1 %all-to-all-start.2 = ((f32[4,432,128]{2,1,0:T(8,128)}), f32[4,432,128]{2,1,0:T(8,128)S(1)}, u32[]{:S(2)}, u32[]{:S(2)}) async-start(f32[4,432,128]{2,1,0:T(8,128)} %bitcast.161), calls=%async_computation.2 | async-start | bytes 1769472 | tf_op jit(solution)/shard_map/all_to_all | solution.py:96
  115.4 1.1 convolution_add_fusion.25
  116.6 1.1 convolution_add_fusion.24
  117.7 1.1 convolution_add_fusion.23
  129.8 0.7 reshape_reshape.7
  130.5 5.7 %all-to-all-start.3 = ((f32[8,54,128]{2,1,0:T(8,128)}), f32[8,54,128]{2,1,0:T(8,128)S(1)}, u32[]{:S(2)}, u32[]{:S(2)}) async-start(f32[8,54,128]{2,1,0:T(8,128)} %reshape_reshape.7), calls=%async_computation.3 | async-start | bytes 458752 | tf_op jit(solution)/shard_map/all_to_all | solution.py:96
  136.6 9.4 %all-to-all-done.3 = f32[8,54,128]{2,1,0:T(8,128)S(1)} async-done(((f32[8,54,128]{2,1,0:T(8,128)}), f32[8,54,128]{2,1,0:T(8,128)S(1)}, u32[]{:S(2)}, u32[]{:S(2)}) %all-to-all-start.3) | async-done | bytes 221216 | tf_op jit(solution)/shard_map/all_to_all | solution.py:96
  146.0 0.7 reshape_reshape.16
  146.7 10.0 %all-to-all-start.4 = ((f32[8,1,864]{2,1,0:T(1,128)}), f32[8,1,864]{2,1,0:T(1,128)S(1)}, u32[]{:S(2)}, u32[]{:S(2)}) async-start(f32[8,1,864]{2,1,0:T(1,128)} %reshape_reshape.16), calls=%async_computation.4 | async-start | bytes 57344 | tf_op jit(solution)/shard_map/all_to_all | solution.py:96
  157.0 6.6 %all-to-all-done.4 = f32[8,1,864]{2,1,0:T(1,128)S(1)} async-done(((f32[8,1,864]{2,1,0:T(1,128)}), f32[8,1,864]{2,1,0:T(1,128)S(1)}, u32[]{:S(2)}, u32[]{:S(2)}) %all-to-all-start.4) | async-done | bytes 27680 | tf_op jit(solution)/shard_map/all_to_all | solution.py:96
  163.6 0.6 broadcast_in_dim.333
  164.3 3.3 %all-to-all-start.5 = ((f32[8,1,864]{2,1,0:T(1,128)}), f32[8,1,864]{2,1,0:T(1,128)S(1)}, u32[]{:S(2)}, u32[]{:S(2)}) async-start(f32[8,1,864]{2,1,0:T(1,128)} %broadcast_in_dim.333), calls=%async_computation.5 | async-start | bytes 57344 | tf_op jit(solution)/shard_map/all_to_all | solution.py:107
  167.8 2.0 gather_fusion
  169.8 0.3 reshape.1746
  170.2 0.4 reshape.1717
  170.6 3.8 %all-to-all-done.5 = f32[8,1,864]{2,1,0:T(1,128)S(1)} async-done(((f32[8,1,864]{2,1,0:T(1,128)}), f32[8,1,864]{2,1,0:T(1,128)S(1)}, u32[]{:S(2)}, u32[]{:S(2)}) %all-to-all-start.5) | async-done | bytes 27680 | tf_op jit(solution)/shard_map/all_to_all | solution.py:107
  174.6 19.3 %all_to_all.52 = f32[8,182,128]{2,1,0:T(8,128)S(1)} all-to-all(f32[8,182,128]{2,1,0:T(8,128)S(1)} %pad_maximum_fusion.2), channel_id=1, replica_groups=mesh['sx'=4,'sy'=8,'sc'=2,'rep'=8] {'sy'}, dimensions={0} | all-to-all | bytes 1490944 | tf_op jit(solution)/shard_map/all_to_all | solution.py:116
  194.0 0.3 reshape.484
  194.3 0.4 reshape.485
  194.9 16.0 %all_to_all.53 = f32[4,688,128]{2,1,0:T(8,128)S(1)} all-to-all(f32[4,688,128]{2,1,0:T(8,128)S(1)} %pad_maximum_fusion.1), channel_id=1, replica_groups=mesh['sx'=4,'sy'=8,'sc'=2,'rep'=8] {'sx'}, dimensions={0} | all-to-all | bytes 2818048 | tf_op jit(solution)/shard_map/all_to_all | solution.py:116
  211.0 0.3 reshape.486
  211.3 0.3 copy.118
  212.1 13.1 %all_to_all.54 = f32[2,2240,128]{2,1,0:T(8,128)S(1)} all-to-all(f32[2,2240,128]{2,1,0:T(8,128)S(1)} %pad_maximum_fusion), channel_id=1, replica_groups=mesh['sx'=4,'sy'=8,'sc'=2,'rep'=8] {'sc'}, dimensions={0} | all-to-all | bytes 4587520 | tf_op jit(solution)/shard_map/all_to_all | solution.py:116
  225.3 0.3 copy.119
  225.8 1.3 gather_fusion.1
  227.1 0.7 slice_bitcast_fusion
  227.7 1.4 slice_multiply_fusion
  (318 shorter events, 21.6 us)
Async XLA Ops:
  2.2 19.0 %copy-start.52 = (s32[1,1,26]{2,1,0:T(1,128)S(1)}, s32[1,1,26]{2,1,0:T(1,128)}, u32[]{:S(2)}) copy-start(s32[1,1,26]{2,1,0:T(1,128)} %param.10) | copy-start | bytes 316
  9.6 61.0 %all-to-all-start = ((bf16[64,2,1152]{2,1,0:T(2,128)(2,1)}), bf16[64,2,1152]{2,1,0:T(2,128)(2,1)S(1)}, u32[]{:S(2)}, u32[]{:S(2)}) async-start(bf16[64,2,1152]{2,1,0:T(2,128)(2,1)} %reshape.1795), calls=%async_computation | async-start | bytes 589824 | tf_op jit(solution)/shard_map/all_to_all | solution.py:166
  74.7 9.2 %collective-permute-start = (bf16[1,8,8,256]{3,2,1,0:T(8,128)(2,1)S(1)}, bf16[1,8,8,256]{3,2,1,0:T(8,128)(2,1)S(1)}, u32[]{:S(2)}, u32[]{:S(2)}) collective-permute-start(bf16[1,8,8,256]{3,2,1,0:T(8,128)(2,1)S(1)} %pad_maximum_fusion.6), channel_id=1, source_target_pairs={{0,8},{8,16},{16,24},{24,32},{32,40},{40,48},{48,56},{56,64},{64,7... | collective-permute-start | bytes 98312 | tf_op jit(solution)/shard_map/ppermute | solution.py:187
  81.9 5.2 %collective-permute-start.1 = (bf16[1,8,8,256]{3,2,1,0:T(8,128)(2,1)S(1)}, bf16[1,8,8,256]{3,2,1,0:T(8,128)(2,1)S(1)}, u32[]{:S(2)}, u32[]{:S(2)}) collective-permute-start(bf16[1,8,8,256]{3,2,1,0:T(8,128)(2,1)S(1)} %pad_maximum_fusion.7), channel_id=1, source_target_pairs={{8,0},{16,8},{24,16},{32,24},{40,32},{48,40},{56,48},{64,56},{72,6... | collective-permute-start | bytes 98312 | tf_op jit(solution)/shard_map/ppermute | solution.py:188
  89.7 2.1 copy-start.51
  89.7 2.4 %copy-start.50 = (bf16[1,8,8,8,128]{4,3,2,1,0:T(8,128)(2,1)S(1)}, bf16[1,8,8,8,128]{4,3,2,1,0:T(8,128)(2,1)}, u32[]{:S(2)}) copy-start(bf16[1,8,8,8,128]{4,3,2,1,0:T(8,128)(2,1)} %get-tuple-element.661) | copy-start | bytes 393220
  89.7 2.6 %copy-start.49 = (bf16[1,8,8,8,128]{4,3,2,1,0:T(8,128)(2,1)S(1)}, bf16[1,8,8,8,128]{4,3,2,1,0:T(8,128)(2,1)}, u32[]{:S(2)}) copy-start(bf16[1,8,8,8,128]{4,3,2,1,0:T(8,128)(2,1)} %get-tuple-element.660) | copy-start | bytes 393220
  92.4 1.1 copy-start.48
  92.6 1.1 copy-start.47
  96.3 1.2 copy-start.1
  97.5 3.8 %copy-start.63 = (bf16[2,1,1,128]{3,2,1,0:T(2,128)(2,1)S(1)}, bf16[2,1,1,128]{3,2,1,0:T(2,128)(2,1)}, u32[]{:S(2)}) copy-start(bf16[2,1,1,128]{3,2,1,0:T(2,128)(2,1)} %get-tuple-element.708) | copy-start | bytes 1540
  97.5 3.8 %copy-start.62 = (bf16[2,1,1,128]{3,2,1,0:T(2,128)(2,1)S(1)}, bf16[2,1,1,128]{3,2,1,0:T(2,128)(2,1)}, u32[]{:S(2)}) copy-start(bf16[2,1,1,128]{3,2,1,0:T(2,128)(2,1)} %get-tuple-element.707) | copy-start | bytes 1540
  97.5 3.9 %copy-start.60 = (bf16[2,1,1,128]{3,2,1,0:T(2,128)(2,1)S(1)}, bf16[2,1,1,128]{3,2,1,0:T(2,128)(2,1)}, u32[]{:S(2)}) copy-start(bf16[2,1,1,128]{3,2,1,0:T(2,128)(2,1)} %get-tuple-element.706) | copy-start | bytes 1540
  97.5 4.0 %copy-start.58 = (bf16[2,1,1,128]{3,2,1,0:T(2,128)(2,1)S(1)}, bf16[2,1,1,128]{3,2,1,0:T(2,128)(2,1)}, u32[]{:S(2)}) copy-start(bf16[2,1,1,128]{3,2,1,0:T(2,128)(2,1)} %get-tuple-element.705) | copy-start | bytes 1540
  97.5 4.0 %copy-start.61 = (bf16[2,1,1,128]{3,2,1,0:T(2,128)(2,1)S(1)}, bf16[2,1,1,128]{3,2,1,0:T(2,128)(2,1)}, u32[]{:S(2)}) copy-start(bf16[2,1,1,128]{3,2,1,0:T(2,128)(2,1)} %get-tuple-element.700) | copy-start | bytes 1540
  97.6 4.0 %copy-start.59 = (bf16[2,1,1,128]{3,2,1,0:T(2,128)(2,1)S(1)}, bf16[2,1,1,128]{3,2,1,0:T(2,128)(2,1)}, u32[]{:S(2)}) copy-start(bf16[2,1,1,128]{3,2,1,0:T(2,128)(2,1)} %get-tuple-element.699) | copy-start | bytes 1540
  97.6 4.1 %copy-start.53 = (bf16[1,8,1,1,128]{4,3,2,1,0:T(2,128)(2,1)S(1)}, bf16[1,8,1,1,128]{4,3,2,1,0:T(2,128)(2,1)}, u32[]{:S(2)}) copy-start(bf16[1,8,1,1,128]{4,3,2,1,0:T(2,128)(2,1)} %get-tuple-element.765) | copy-start | bytes 6148
  97.6 4.1 %copy-start.54 = (bf16[1,8,1,1,128]{4,3,2,1,0:T(2,128)(2,1)S(1)}, bf16[1,8,1,1,128]{4,3,2,1,0:T(2,128)(2,1)}, u32[]{:S(2)}) copy-start(bf16[1,8,1,1,128]{4,3,2,1,0:T(2,128)(2,1)} %get-tuple-element.766) | copy-start | bytes 6148
  97.6 4.1 %copy-start.55 = (bf16[1,8,1,1,128]{4,3,2,1,0:T(2,128)(2,1)S(1)}, bf16[1,8,1,1,128]{4,3,2,1,0:T(2,128)(2,1)}, u32[]{:S(2)}) copy-start(bf16[1,8,1,1,128]{4,3,2,1,0:T(2,128)(2,1)} %get-tuple-element.767) | copy-start | bytes 6148
  97.6 4.1 %copy-start.56 = (bf16[1,8,1,1,128]{4,3,2,1,0:T(2,128)(2,1)S(1)}, bf16[1,8,1,1,128]{4,3,2,1,0:T(2,128)(2,1)}, u32[]{:S(2)}) copy-start(bf16[1,8,1,1,128]{4,3,2,1,0:T(2,128)(2,1)} %get-tuple-element.768) | copy-start | bytes 6148
  97.6 6.0 %all-to-all-start.1 = ((f32[2,1728,128]{2,1,0:T(8,128)}), f32[2,1728,128]{2,1,0:T(8,128)S(1)}, u32[]{:S(2)}, u32[]{:S(2)}) async-start(f32[2,1728,128]{2,1,0:T(8,128)} %bitcast.608), calls=%async_computation.1 | async-start | bytes 3538944 | tf_op jit(solution)/shard_map/all_to_all | solution.py:96
  108.2 1.7 copy-start
  110.3 19.4 %all-to-all-start.2 = ((f32[4,432,128]{2,1,0:T(8,128)}), f32[4,432,128]{2,1,0:T(8,128)S(1)}, u32[]{:S(2)}, u32[]{:S(2)}) async-start(f32[4,432,128]{2,1,0:T(8,128)} %bitcast.161), calls=%async_computation.2 | async-start | bytes 1769472 | tf_op jit(solution)/shard_map/all_to_all | solution.py:96
  115.4 3.5 %copy-start.46 = (bf16[1,8,8,8,128]{4,3,2,1,0:T(8,128)(2,1)S(1)}, bf16[1,8,8,8,128]{4,3,2,1,0:T(8,128)(2,1)}, u32[]{:S(2)}) copy-start(bf16[1,8,8,8,128]{4,3,2,1,0:T(8,128)(2,1)} %get-tuple-element.634) | copy-start | bytes 393220
  115.4 3.7 %copy-start.45 = (bf16[1,8,8,8,128]{4,3,2,1,0:T(8,128)(2,1)S(1)}, bf16[1,8,8,8,128]{4,3,2,1,0:T(8,128)(2,1)}, u32[]{:S(2)}) copy-start(bf16[1,8,8,8,128]{4,3,2,1,0:T(8,128)(2,1)} %get-tuple-element.633) | copy-start | bytes 393220
  115.4 3.9 %copy-start.44 = (bf16[1,8,8,8,128]{4,3,2,1,0:T(8,128)(2,1)S(1)}, bf16[1,8,8,8,128]{4,3,2,1,0:T(8,128)(2,1)}, u32[]{:S(2)}) copy-start(bf16[1,8,8,8,128]{4,3,2,1,0:T(8,128)(2,1)} %get-tuple-element.632) | copy-start | bytes 393220
  116.6 3.0 %copy-start.43 = (bf16[1,8,8,8,128]{4,3,2,1,0:T(8,128)(2,1)S(1)}, bf16[1,8,8,8,128]{4,3,2,1,0:T(8,128)(2,1)}, u32[]{:S(2)}) copy-start(bf16[1,8,8,8,128]{4,3,2,1,0:T(8,128)(2,1)} %get-tuple-element.631) | copy-start | bytes 393220
  117.7 2.0 copy-start.42
  118.9 1.1 copy-start.41
  119.1 1.1 copy-start.40
  119.3 1.1 copy-start.39
  119.5 1.1 copy-start.38
  119.7 1.1 copy-start.37
  120.0 1.1 copy-start.36
  120.2 1.1 copy-start.35
  121.5 1.1 copy-start.29
  122.4 1.1 copy-start.23
  122.6 1.1 copy-start.26
  122.8 1.1 copy-start.24
  123.0 1.2 copy-start.22
  123.2 1.2 copy-start.21
  123.4 1.2 copy-start.20
  123.7 1.3 copy-start.19
  123.9 1.3 copy-start.18
  124.2 1.3 copy-start.17
  124.4 1.3 copy-start.16
  124.7 1.3 copy-start.15
  124.9 1.3 copy-start.14
  125.2 1.3 copy-start.13
  125.4 1.3 copy-start.12
  125.7 1.3 copy-start.11
  126.0 1.3 copy-start.10
  126.2 1.3 copy-start.9
  126.5 1.3 copy-start.8
  126.7 1.3 copy-start.7
  127.0 1.3 copy-start.6
  127.2 1.3 copy-start.5
  127.5 1.3 copy-start.4
  127.7 1.2 copy-start.3
  128.0 1.2 copy-start.2
  130.5 15.5 %all-to-all-start.3 = ((f32[8,54,128]{2,1,0:T(8,128)}), f32[8,54,128]{2,1,0:T(8,128)S(1)}, u32[]{:S(2)}, u32[]{:S(2)}) async-start(f32[8,54,128]{2,1,0:T(8,128)} %reshape_reshape.7), calls=%async_computation.3 | async-start | bytes 458752 | tf_op jit(solution)/shard_map/all_to_all | solution.py:96
  136.4 31.4 %copy-start.57 = (s32[1024]{0:T(1024)S(1)}, s32[1024]{0:T(1024)}, u32[]{:S(2)}) copy-start(s32[1024]{0:T(1024)} %get-tuple-element.774) | copy-start | bytes 12292
  146.7 16.9 %all-to-all-start.4 = ((f32[8,1,864]{2,1,0:T(1,128)}), f32[8,1,864]{2,1,0:T(1,128)S(1)}, u32[]{:S(2)}, u32[]{:S(2)}) async-start(f32[8,1,864]{2,1,0:T(1,128)} %reshape_reshape.16), calls=%async_computation.4 | async-start | bytes 57344 | tf_op jit(solution)/shard_map/all_to_all | solution.py:96
  164.3 10.1 %all-to-all-start.5 = ((f32[8,1,864]{2,1,0:T(1,128)}), f32[8,1,864]{2,1,0:T(1,128)S(1)}, u32[]{:S(2)}, u32[]{:S(2)}) async-start(f32[8,1,864]{2,1,0:T(1,128)} %broadcast_in_dim.333), calls=%async_computation.5 | async-start | bytes 57344 | tf_op jit(solution)/shard_map/all_to_all | solution.py:107
  (8 other events, 8.8 us)

commit v6 on v5

--- a/solution.py
+++ b/solution.py
@@ -86,7 +86,7 @@
     ].reshape(-1, channels)
 
 
-def reduce_everywhere(value, sizes, held, make_carry):
+def reduce_everywhere(value, sizes, held, make_carry, scale):
     flat = value.reshape(-1)
     for stage, axis in enumerate(REDUCE_ORDER):
         if stage == 1:
@@ -95,6 +95,7 @@
         lanes = 128 if flat.shape[0] % (count * 128) == 0 else flat.shape[0] // count
         parts = lax.all_to_all(flat.reshape(count, -1, lanes), axis, 0, 0, tiled=True)
         flat = jnp.sum(parts, 0).reshape(-1)
+    flat = flat * scale
     carry, carry_axes = None, []
     for axis in reversed(REDUCE_ORDER):
         count = sizes[axis]
@@ -223,15 +224,15 @@
             ret = out_both[arrived].astype(jnp.float32)
             return ret.reshape(sizes["sx"], sizes["sy"], sizes["sc"], capacity * 2 * channels)
 
-        summed, _, home = reduce_everywhere(
-            grad_part, sizes, (padded_h, padded_g, dense_x, dense_g), make_carry
+        norm_scale = 1.0 / math.sqrt(peer_count * rep_count * owners.shape[0])
+        weight_grad, _, home = reduce_everywhere(
+            grad_part, sizes, (padded_h, padded_g, dense_x, dense_g), make_carry, norm_scale
         )
         home = home.reshape(-1, 2 * channels).astype(data_type)
         final = home[bucket]
         final_x = final[:, :channels]
         final_dx = final[:, channels:]
-        norm_scale = 1.0 / math.sqrt(peer_count * rep_count * owners.shape[0])
-        weight_grad = (summed * norm_scale).reshape(27, channels, channels)
+        weight_grad = weight_grad.reshape(27, channels, channels)
         return (final_x[None], final_dx[None], weight_grad)
 
     return local

time: 231 us -> 231 us (level)
  no operation moved by 1% of the time
where the time goes in v6:
time: 231 us; the launch traced here: 229 us
  between operations  51 us (22%)
  blocking collectives  48.5 us (21%)
  starting transfers between devices  45.1 us (20%)
  local copies, waits for them, and re-layouts  30.5 us (13%)
  waiting for transfers between devices  24.4 us (11%)
  matrix products  20.2 us (9%)
  other arithmetic  9.29 us (4%)
    all_to_all x3, blocking collectives, reduce_everywhere(): got = lax.all_to_all(sent, axis, 0, 0, tiled=True)  48.5 us
    all_to_all x4, starting transfers between devices, reduce_everywhere(): lax.all_to_all(flat.reshape(count, -1, lanes), axis, 0, 0, tiled=True)  24.6 us
    all_to_all x4, waiting for transfers between devices, reduce_everywhere(): lax.all_to_all(flat.reshape(count, -1, lanes), axis, 0, 0, tiled=True)  17.6 us
    all_to_all x1, starting transfers between devices, local(): recv = lax.all_to_all(send, SPACE_AXES, 0, 0, tiled=True)  11.6 us
    dot_general x27, matrix products, make_carry(): lax.dot_general(view_g, tap_weight, (((1,), (1,)), ((), ())), preferred_e...  7.98 us
    slice x8, local copies, waits for them, and re-layouts, tap_view(): padded[:, start_x:start_x + 8, start_y:start_y + 8, start_z:start_z + 8, :]  6.94 us
    dot_general x27, matrix products, make_carry(): jnp.dot(view_h, tap_weight, preferred_element_type=jnp.float32)  6.12 us
    dot_general x27, matrix products, local(): lax.dot_general(view_h, grads_flat, (((0,), (0,)), ((), ())), preferred_e...  6.1 us
  transfers between devices with their start and end apart: 8, of which 5 were waited for; matrix products, arithmetic and copies ran while one was open for 10% of the time, Pallas kernels for 0%

profile of v6, /device:TPU:1, one launch (start us, length us, event | category | flops | bytes accessed | tf_op | source)
XLA Modules:
  0.0 229.1 jit_solution(133316337009660452)
XLA Ops:
  0.6 0.7 fusion.42
  1.3 0.6 reduce-window.6
  2.2 0.8 fusion.41
  3.0 0.7 compare_select_fusion.1
  3.6 1.9 scatter_custom_fusion
  5.7 1.6 scatter_custom_fusion.1
  7.5 0.5 broadcast.1054
  8.0 0.8 reduce.4
  8.8 0.8 reshape.1797
  9.6 11.6 %all-to-all-start = ((bf16[64,2,1152]{2,1,0:T(2,128)(2,1)}), bf16[64,2,1152]{2,1,0:T(2,128)(2,1)S(1)}, u32[]{:S(2)}, u32[]{:S(2)}) async-start(bf16[64,2,1152]{2,1,0:T(2,128)(2,1)} %reshape.1797), calls=%async_computation | async-start | bytes 589824 | tf_op jit(solution)/shard_map/all_to_all | solution.py:167
  21.2 0.7 fusion.233
  34.3 0.7 fusion.234
  70.5 0.3 reshape.1798
  71.2 2.4 %scatter_custom_fusion.2 = bf16[513,256]{1,0:T(8,128)(2,1)S(1)} fusion(s32[512]{0:T(512)S(1)} %bitcast.700, bf16[512,256]{1,0:T(8,128)(2,1)S(1)} %reshape.1785, bf16[]{:T(256)} %constant.19.clone.1), kind=kCustom, calls=%fused_computation.145 | custom fusion | bytes 262658 | tf_op jit(solution)/shard_map/scatter | solution.py:175
  74.1 0.6 pad_clamp_fusion
  74.7 3.5 %collective-permute-start = (bf16[1,8,8,256]{3,2,1,0:T(8,128)(2,1)S(1)}, bf16[1,8,8,256]{3,2,1,0:T(8,128)(2,1)S(1)}, u32[]{:S(2)}, u32[]{:S(2)}) collective-permute-start(bf16[1,8,8,256]{3,2,1,0:T(8,128)(2,1)S(1)} %pad_maximum_fusion.6), channel_id=1, source_target_pairs={{0,8},{8,16},{16,24},{24,32},{32,40},{40,48},{48,56},{56,64},{64,7... | collective-permute-start | bytes 98312 | tf_op jit(solution)/shard_map/ppermute | solution.py:188
  78.6 0.3 maximum_maximum_fusion.5
  78.9 0.8 fusion.229
  79.7 0.7 fusion.228
  80.5 0.6 constant_dynamic-slice_fusion.8
  81.1 0.6 constant_dynamic-slice_fusion.13
  81.9 2.1 collective-permute-start.1
  84.0 3.1 %collective-permute-done.1 = bf16[1,8,8,256]{3,2,1,0:T(8,128)(2,1)S(1)} collective-permute-done((bf16[1,8,8,256]{3,2,1,0:T(8,128)(2,1)S(1)}, bf16[1,8,8,256]{3,2,1,0:T(8,128)(2,1)S(1)}, u32[]{:S(2)}, u32[]{:S(2)}) %collective-permute-start.1) | collective-permute-done | bytes 32800 | tf_op jit(solution)/shard_map/ppermute | solution.py:189
  87.5 0.2 maximum_maximum_fusion.2
  87.7 0.2 maximum_maximum_fusion.3
  88.0 0.3 maximum_maximum_fusion
  88.3 0.6 pad_slice_fusion.23
  88.9 0.6 pad_slice_fusion.31
  96.3 1.2 copy-done.1
  97.6 3.7 %all-to-all-start.1 = ((f32[2,1728,128]{2,1,0:T(8,128)}), f32[2,1728,128]{2,1,0:T(8,128)S(1)}, u32[]{:S(2)}, u32[]{:S(2)}) async-start(f32[2,1728,128]{2,1,0:T(8,128)} %bitcast.608), calls=%async_computation.1 | async-start | bytes 3538944 | tf_op jit(solution)/shard_map/all_to_all | solution.py:96
  101.7 0.3 maximum_maximum_fusion.1
  102.0 1.6 all-to-all-done.1
  103.6 1.1 reduce_sum.49
  104.7 1.0 fusion.225
  105.7 1.5 fusion.224
  107.2 1.0 fusion.223
  108.2 1.5 fusion.222
  110.3 5.1 %all-to-all-start.2 = ((f32[4,432,128]{2,1,0:T(8,128)}), f32[4,432,128]{2,1,0:T(8,128)S(1)}, u32[]{:S(2)}, u32[]{:S(2)}) async-start(f32[4,432,128]{2,1,0:T(8,128)} %bitcast.161), calls=%async_computation.2 | async-start | bytes 1769472 | tf_op jit(solution)/shard_map/all_to_all | solution.py:96
  115.4 1.1 convolution_add_fusion.25
  116.6 1.1 convolution_add_fusion.24
  117.7 1.1 convolution_add_fusion.23
  129.8 0.7 reshape_reshape.16
  130.5 5.7 %all-to-all-start.3 = ((f32[8,54,128]{2,1,0:T(8,128)}), f32[8,54,128]{2,1,0:T(8,128)S(1)}, u32[]{:S(2)}, u32[]{:S(2)}) async-start(f32[8,54,128]{2,1,0:T(8,128)} %reshape_reshape.16), calls=%async_computation.3 | async-start | bytes 458752 | tf_op jit(solution)/shard_map/all_to_all | solution.py:96
  136.6 9.4 %all-to-all-done.3 = f32[8,54,128]{2,1,0:T(8,128)S(1)} async-done(((f32[8,54,128]{2,1,0:T(8,128)}), f32[8,54,128]{2,1,0:T(8,128)S(1)}, u32[]{:S(2)}, u32[]{:S(2)}) %all-to-all-start.3) | async-done | bytes 221216 | tf_op jit(solution)/shard_map/all_to_all | solution.py:96
  146.0 0.7 reshape_reshape.17
  146.7 10.0 %all-to-all-start.4 = ((f32[8,1,864]{2,1,0:T(1,128)}), f32[8,1,864]{2,1,0:T(1,128)S(1)}, u32[]{:S(2)}, u32[]{:S(2)}) async-start(f32[8,1,864]{2,1,0:T(1,128)} %reshape_reshape.17), calls=%async_computation.4 | async-start | bytes 57344 | tf_op jit(solution)/shard_map/all_to_all | solution.py:96
  157.0 6.6 %all-to-all-done.4 = f32[8,1,864]{2,1,0:T(1,128)S(1)} async-done(((f32[8,1,864]{2,1,0:T(1,128)}), f32[8,1,864]{2,1,0:T(1,128)S(1)}, u32[]{:S(2)}, u32[]{:S(2)}) %all-to-all-start.4) | async-done | bytes 27680 | tf_op jit(solution)/shard_map/all_to_all | solution.py:96
  163.7 0.6 broadcast_in_dim.333
  164.3 3.3 %all-to-all-start.5 = ((f32[8,1,864]{2,1,0:T(1,128)}), f32[8,1,864]{2,1,0:T(1,128)S(1)}, u32[]{:S(2)}, u32[]{:S(2)}) async-start(f32[8,1,864]{2,1,0:T(1,128)} %broadcast_in_dim.333), calls=%async_computation.5 | async-start | bytes 57344 | tf_op jit(solution)/shard_map/all_to_all | solution.py:108
  167.8 2.0 gather_fusion
  169.8 0.3 reshape.1748
  170.2 0.4 reshape.1719
  170.6 3.8 %all-to-all-done.5 = f32[8,1,864]{2,1,0:T(1,128)S(1)} async-done(((f32[8,1,864]{2,1,0:T(1,128)}), f32[8,1,864]{2,1,0:T(1,128)S(1)}, u32[]{:S(2)}, u32[]{:S(2)}) %all-to-all-start.5) | async-done | bytes 27680 | tf_op jit(solution)/shard_map/all_to_all | solution.py:108
  174.6 19.3 %all_to_all.52 = f32[8,182,128]{2,1,0:T(8,128)S(1)} all-to-all(f32[8,182,128]{2,1,0:T(8,128)S(1)} %pad_maximum_fusion.2), channel_id=1, replica_groups=mesh['sx'=4,'sy'=8,'sc'=2,'rep'=8] {'sy'}, dimensions={0} | all-to-all | bytes 1490944 | tf_op jit(solution)/shard_map/all_to_all | solution.py:117
  194.0 0.3 reshape.486
  194.3 0.4 reshape.487
  195.0 16.0 %all_to_all.53 = f32[4,688,128]{2,1,0:T(8,128)S(1)} all-to-all(f32[4,688,128]{2,1,0:T(8,128)S(1)} %pad_maximum_fusion.1), channel_id=1, replica_groups=mesh['sx'=4,'sy'=8,'sc'=2,'rep'=8] {'sx'}, dimensions={0} | all-to-all | bytes 2818048 | tf_op jit(solution)/shard_map/all_to_all | solution.py:117
  211.0 0.3 reshape.488
  211.3 0.3 copy.118
  212.1 13.1 %all_to_all.54 = f32[2,2240,128]{2,1,0:T(8,128)S(1)} all-to-all(f32[2,2240,128]{2,1,0:T(8,128)S(1)} %pad_maximum_fusion), channel_id=1, replica_groups=mesh['sx'=4,'sy'=8,'sc'=2,'rep'=8] {'sc'}, dimensions={0} | all-to-all | bytes 4587520 | tf_op jit(solution)/shard_map/all_to_all | solution.py:117
  225.3 0.3 copy.119
  225.8 1.3 gather_fusion.1
  227.1 0.7 slice_bitcast_fusion
  227.8 1.3 slice.1532
  (319 shorter events, 21.6 us)
Async XLA Ops:
  2.2 19.0 %copy-start.52 = (s32[1,1,26]{2,1,0:T(1,128)S(1)}, s32[1,1,26]{2,1,0:T(1,128)}, u32[]{:S(2)}) copy-start(s32[1,1,26]{2,1,0:T(1,128)} %param.10) | copy-start | bytes 316
  9.6 61.0 %all-to-all-start = ((bf16[64,2,1152]{2,1,0:T(2,128)(2,1)}), bf16[64,2,1152]{2,1,0:T(2,128)(2,1)S(1)}, u32[]{:S(2)}, u32[]{:S(2)}) async-start(bf16[64,2,1152]{2,1,0:T(2,128)(2,1)} %reshape.1797), calls=%async_computation | async-start | bytes 589824 | tf_op jit(solution)/shard_map/all_to_all | solution.py:167
  74.7 9.2 %collective-permute-start = (bf16[1,8,8,256]{3,2,1,0:T(8,128)(2,1)S(1)}, bf16[1,8,8,256]{3,2,1,0:T(8,128)(2,1)S(1)}, u32[]{:S(2)}, u32[]{:S(2)}) collective-permute-start(bf16[1,8,8,256]{3,2,1,0:T(8,128)(2,1)S(1)} %pad_maximum_fusion.6), channel_id=1, source_target_pairs={{0,8},{8,16},{16,24},{24,32},{32,40},{40,48},{48,56},{56,64},{64,7... | collective-permute-start | bytes 98312 | tf_op jit(solution)/shard_map/ppermute | solution.py:188
  81.9 5.2 %collective-permute-start.1 = (bf16[1,8,8,256]{3,2,1,0:T(8,128)(2,1)S(1)}, bf16[1,8,8,256]{3,2,1,0:T(8,128)(2,1)S(1)}, u32[]{:S(2)}, u32[]{:S(2)}) collective-permute-start(bf16[1,8,8,256]{3,2,1,0:T(8,128)(2,1)S(1)} %pad_maximum_fusion.7), channel_id=1, source_target_pairs={{8,0},{16,8},{24,16},{32,24},{40,32},{48,40},{56,48},{64,56},{72,6... | collective-permute-start | bytes 98312 | tf_op jit(solution)/shard_map/ppermute | solution.py:189
  89.7 2.1 copy-start.51
  89.7 2.4 %copy-start.50 = (bf16[1,8,8,8,128]{4,3,2,1,0:T(8,128)(2,1)S(1)}, bf16[1,8,8,8,128]{4,3,2,1,0:T(8,128)(2,1)}, u32[]{:S(2)}) copy-start(bf16[1,8,8,8,128]{4,3,2,1,0:T(8,128)(2,1)} %get-tuple-element.661) | copy-start | bytes 393220
  89.7 2.6 %copy-start.49 = (bf16[1,8,8,8,128]{4,3,2,1,0:T(8,128)(2,1)S(1)}, bf16[1,8,8,8,128]{4,3,2,1,0:T(8,128)(2,1)}, u32[]{:S(2)}) copy-start(bf16[1,8,8,8,128]{4,3,2,1,0:T(8,128)(2,1)} %get-tuple-element.660) | copy-start | bytes 393220
  92.4 1.1 copy-start.48
  92.6 1.1 copy-start.47
  96.3 1.2 copy-start.1
  97.5 3.8 %copy-start.63 = (bf16[2,1,1,128]{3,2,1,0:T(2,128)(2,1)S(1)}, bf16[2,1,1,128]{3,2,1,0:T(2,128)(2,1)}, u32[]{:S(2)}) copy-start(bf16[2,1,1,128]{3,2,1,0:T(2,128)(2,1)} %get-tuple-element.708) | copy-start | bytes 1540
  97.5 3.8 %copy-start.62 = (bf16[2,1,1,128]{3,2,1,0:T(2,128)(2,1)S(1)}, bf16[2,1,1,128]{3,2,1,0:T(2,128)(2,1)}, u32[]{:S(2)}) copy-start(bf16[2,1,1,128]{3,2,1,0:T(2,128)(2,1)} %get-tuple-element.707) | copy-start | bytes 1540
  97.5 3.9 %copy-start.60 = (bf16[2,1,1,128]{3,2,1,0:T(2,128)(2,1)S(1)}, bf16[2,1,1,128]{3,2,1,0:T(2,128)(2,1)}, u32[]{:S(2)}) copy-start(bf16[2,1,1,128]{3,2,1,0:T(2,128)(2,1)} %get-tuple-element.706) | copy-start | bytes 1540
  97.5 4.0 %copy-start.58 = (bf16[2,1,1,128]{3,2,1,0:T(2,128)(2,1)S(1)}, bf16[2,1,1,128]{3,2,1,0:T(2,128)(2,1)}, u32[]{:S(2)}) copy-start(bf16[2,1,1,128]{3,2,1,0:T(2,128)(2,1)} %get-tuple-element.705) | copy-start | bytes 1540
  97.5 4.0 %copy-start.61 = (bf16[2,1,1,128]{3,2,1,0:T(2,128)(2,1)S(1)}, bf16[2,1,1,128]{3,2,1,0:T(2,128)(2,1)}, u32[]{:S(2)}) copy-start(bf16[2,1,1,128]{3,2,1,0:T(2,128)(2,1)} %get-tuple-element.700) | copy-start | bytes 1540
  97.6 4.0 %copy-start.59 = (bf16[2,1,1,128]{3,2,1,0:T(2,128)(2,1)S(1)}, bf16[2,1,1,128]{3,2,1,0:T(2,128)(2,1)}, u32[]{:S(2)}) copy-start(bf16[2,1,1,128]{3,2,1,0:T(2,128)(2,1)} %get-tuple-element.699) | copy-start | bytes 1540
  97.6 4.1 %copy-start.53 = (bf16[1,8,1,1,128]{4,3,2,1,0:T(2,128)(2,1)S(1)}, bf16[1,8,1,1,128]{4,3,2,1,0:T(2,128)(2,1)}, u32[]{:S(2)}) copy-start(bf16[1,8,1,1,128]{4,3,2,1,0:T(2,128)(2,1)} %get-tuple-element.765) | copy-start | bytes 6148
  97.6 4.1 %copy-start.54 = (bf16[1,8,1,1,128]{4,3,2,1,0:T(2,128)(2,1)S(1)}, bf16[1,8,1,1,128]{4,3,2,1,0:T(2,128)(2,1)}, u32[]{:S(2)}) copy-start(bf16[1,8,1,1,128]{4,3,2,1,0:T(2,128)(2,1)} %get-tuple-element.766) | copy-start | bytes 6148
  97.6 4.1 %copy-start.55 = (bf16[1,8,1,1,128]{4,3,2,1,0:T(2,128)(2,1)S(1)}, bf16[1,8,1,1,128]{4,3,2,1,0:T(2,128)(2,1)}, u32[]{:S(2)}) copy-start(bf16[1,8,1,1,128]{4,3,2,1,0:T(2,128)(2,1)} %get-tuple-element.767) | copy-start | bytes 6148
  97.6 4.1 %copy-start.56 = (bf16[1,8,1,1,128]{4,3,2,1,0:T(2,128)(2,1)S(1)}, bf16[1,8,1,1,128]{4,3,2,1,0:T(2,128)(2,1)}, u32[]{:S(2)}) copy-start(bf16[1,8,1,1,128]{4,3,2,1,0:T(2,128)(2,1)} %get-tuple-element.768) | copy-start | bytes 6148
  97.6 6.0 %all-to-all-start.1 = ((f32[2,1728,128]{2,1,0:T(8,128)}), f32[2,1728,128]{2,1,0:T(8,128)S(1)}, u32[]{:S(2)}, u32[]{:S(2)}) async-start(f32[2,1728,128]{2,1,0:T(8,128)} %bitcast.608), calls=%async_computation.1 | async-start | bytes 3538944 | tf_op jit(solution)/shard_map/all_to_all | solution.py:96
  108.2 1.7 copy-start
  110.3 19.4 %all-to-all-start.2 = ((f32[4,432,128]{2,1,0:T(8,128)}), f32[4,432,128]{2,1,0:T(8,128)S(1)}, u32[]{:S(2)}, u32[]{:S(2)}) async-start(f32[4,432,128]{2,1,0:T(8,128)} %bitcast.161), calls=%async_computation.2 | async-start | bytes 1769472 | tf_op jit(solution)/shard_map/all_to_all | solution.py:96
  115.4 3.5 %copy-start.46 = (bf16[1,8,8,8,128]{4,3,2,1,0:T(8,128)(2,1)S(1)}, bf16[1,8,8,8,128]{4,3,2,1,0:T(8,128)(2,1)}, u32[]{:S(2)}) copy-start(bf16[1,8,8,8,128]{4,3,2,1,0:T(8,128)(2,1)} %get-tuple-element.634) | copy-start | bytes 393220
  115.4 3.7 %copy-start.45 = (bf16[1,8,8,8,128]{4,3,2,1,0:T(8,128)(2,1)S(1)}, bf16[1,8,8,8,128]{4,3,2,1,0:T(8,128)(2,1)}, u32[]{:S(2)}) copy-start(bf16[1,8,8,8,128]{4,3,2,1,0:T(8,128)(2,1)} %get-tuple-element.633) | copy-start | bytes 393220
  115.4 3.9 %copy-start.44 = (bf16[1,8,8,8,128]{4,3,2,1,0:T(8,128)(2,1)S(1)}, bf16[1,8,8,8,128]{4,3,2,1,0:T(8,128)(2,1)}, u32[]{:S(2)}) copy-start(bf16[1,8,8,8,128]{4,3,2,1,0:T(8,128)(2,1)} %get-tuple-element.632) | copy-start | bytes 393220
  116.6 3.0 %copy-start.43 = (bf16[1,8,8,8,128]{4,3,2,1,0:T(8,128)(2,1)S(1)}, bf16[1,8,8,8,128]{4,3,2,1,0:T(8,128)(2,1)}, u32[]{:S(2)}) copy-start(bf16[1,8,8,8,128]{4,3,2,1,0:T(8,128)(2,1)} %get-tuple-element.631) | copy-start | bytes 393220
  117.7 2.0 copy-start.42
  118.9 1.1 copy-start.41
  119.1 1.1 copy-start.40
  119.3 1.1 copy-start.39
  119.5 1.1 copy-start.38
  119.7 1.1 copy-start.37
  120.0 1.1 copy-start.36
  120.2 1.1 copy-start.35
  121.5 1.1 copy-start.29
  122.4 1.1 copy-start.23
  122.6 1.1 copy-start.26
  122.8 1.1 copy-start.24
  123.0 1.2 copy-start.22
  123.2 1.2 copy-start.21
  123.4 1.2 copy-start.20
  123.7 1.3 copy-start.19
  123.9 1.3 copy-start.18
  124.2 1.3 copy-start.17
  124.4 1.3 copy-start.16
  124.7 1.3 copy-start.15
  124.9 1.3 copy-start.14
  125.2 1.3 copy-start.13
  125.4 1.3 copy-start.12
  125.7 1.3 copy-start.11
  126.0 1.3 copy-start.10
  126.2 1.3 copy-start.9
  126.5 1.3 copy-start.8
  126.7 1.3 copy-start.7
  127.0 1.3 copy-start.6
  127.2 1.3 copy-start.5
  127.5 1.3 copy-start.4
  127.7 1.2 copy-start.3
  128.0 1.2 copy-start.2
  130.5 15.5 %all-to-all-start.3 = ((f32[8,54,128]{2,1,0:T(8,128)}), f32[8,54,128]{2,1,0:T(8,128)S(1)}, u32[]{:S(2)}, u32[]{:S(2)}) async-start(f32[8,54,128]{2,1,0:T(8,128)} %reshape_reshape.16), calls=%async_computation.3 | async-start | bytes 458752 | tf_op jit(solution)/shard_map/all_to_all | solution.py:96
  136.4 31.4 %copy-start.57 = (s32[1024]{0:T(1024)S(1)}, s32[1024]{0:T(1024)}, u32[]{:S(2)}) copy-start(s32[1024]{0:T(1024)} %get-tuple-element.774) | copy-start | bytes 12292
  146.7 16.9 %all-to-all-start.4 = ((f32[8,1,864]{2,1,0:T(1,128)}), f32[8,1,864]{2,1,0:T(1,128)S(1)}, u32[]{:S(2)}, u32[]{:S(2)}) async-start(f32[8,1,864]{2,1,0:T(1,128)} %reshape_reshape.17), calls=%async_computation.4 | async-start | bytes 57344 | tf_op jit(solution)/shard_map/all_to_all | solution.py:96
  164.3 10.1 %all-to-all-start.5 = ((f32[8,1,864]{2,1,0:T(1,128)}), f32[8,1,864]{2,1,0:T(1,128)S(1)}, u32[]{:S(2)}, u32[]{:S(2)}) async-start(f32[8,1,864]{2,1,0:T(1,128)} %broadcast_in_dim.333), calls=%async_computation.5 | async-start | bytes 57344 | tf_op jit(solution)/shard_map/all_to_all | solution.py:108
  (8 other events, 8.8 us)
